TPU v7x, 32 devices: a whole 2x2x4 slice. The times are simulated.
32 devices in a mesh: member: 8 (over z, core), lat: 4 (over y, x).
Axes of the slice: x: 2, y: 2, z: 4, core: 2. Of those that a mesh axis runs over, the one named last changes fastest.
Arguments:
- latents: bfloat16 [8, 12, 45, 720], P('member', 'lat'), may hold values from -6 to 6
- filters: bfloat16 [5, 45, 45], replicated, may hold values from -0.125 to 0.125
- project: bfloat16 [5, 45], replicated, may hold values from -0.875 to 0.875
- subcell_maps: bfloat16 [4, 5, 5], replicated, may hold values from -2.5 to 2.5
- verifying_truth: float32 [4, 5, 12, 720], P(None, None, 'lat', 'member'), may hold values from -6 to 6
- basis_rows: int32 [12, 49], replicated, may hold values from 0 to 5
- step_rows: int32 [12], replicated, may hold values from 1 to 3
Outputs:
- d_latent: bfloat16 [8, 12, 45, 720], P('member', 'lat')
Inputs may be any that keep to these rules, and one draw needn't show every extreme that they name: `basis_rows`: the value 5 marks a tap outside the filter's support; smaller values name a basis filter.
All inputs are finite; a program needn't handle non-finite values.
Results may differ from a plain program's by a relative error of at most 0.0077.
Values may be sent and summed in bfloat16 or wider, within the bound.
No kernel may reach another device: no remote copies, remote signals or barrier semaphores. Data moves between devices by JAX's collectives and lax.ppermute only.
A program may use at most 64 MiB of HBM per device.

v0:
```python
import jax
import jax.numpy as jnp
from jax import lax
from jax.experimental import pallas as pl
from jax.experimental.pallas import tpu as pltpu
from jax.sharding import PartitionSpec as P

TAPS = 7
HALF = 3
MAX_STEP = 3


def round_up(value, unit):
    return (value + unit - 1) // unit * unit


def ring_width(width):
    return round_up(width + 4 * HALF * MAX_STEP + 2, 128)


def to_ring(block, width_p):
    width = block.shape[-1]
    extra = width_p - width
    lo = extra // 2
    hi = extra - lo
    return jnp.concatenate(
        [block, block[..., :lo], block[..., width - hi :]], axis=-1
    )


def pad_axis(block, axis, size):
    pads = [(0, 0)] * block.ndim
    pads[axis] = (0, size - block.shape[axis])
    return jnp.pad(block, pads)


def halo(block, axis_name, width):
    count = lax.axis_size(axis_name)
    forward = [(i, i + 1) for i in range(count - 1)]
    backward = [(target, source) for source, target in forward]
    low = lax.ppermute(block[block.shape[0] - width :], axis_name, forward)
    high = lax.ppermute(block[:width], axis_name, backward)
    return low, high


def latitude_rows(count, total):
    rows = jnp.arange(count, dtype=jnp.int32).astype(jnp.float32)
    return jnp.cos(((rows + 0.5) / total - 0.5) * jnp.pi)


def subcell_weight(first, count, total):
    rows = (first + jnp.arange(count, dtype=jnp.int32)).astype(jnp.float32)
    sub_row = jnp.array([0.0, 0.0, 1.0, 1.0], jnp.float32)
    fine = 2.0 * rows[None, :] + sub_row[:, None]
    return jnp.cos(((fine + 0.5) / (2.0 * total) - 0.5) * jnp.pi)


def softened_sign(diff):
    return diff / jnp.sqrt(diff * diff + 0.01)


SQRT_2_OVER_PI = 0.7978845608028654


def gelu(x):
    inner = SQRT_2_OVER_PI * (x + 0.044715 * (x * x * x))
    return x * (0.5 * (1.0 + jnp.tanh(inner)))


def gelu_grad(x):
    inner = SQRT_2_OVER_PI * (x + 0.044715 * (x * x * x))
    t = jnp.tanh(inner)
    d_inner = SQRT_2_OVER_PI * (1.0 + 3.0 * 0.044715 * (x * x))
    return 0.5 * (1.0 + t) + x * (0.5 * (1.0 - t * t)) * d_inner


def forward_kernel(shift_ref, quad_ref, prev_ref, own_ref, next_ref, w_ref, proj_ref,
                   sub_ref, filt_ref, fc_ref):
    rows, cp, _ = own_ref.shape
    ext = (
        [prev_ref[e] for e in range(HALF)]
        + [own_ref[e] for e in range(rows)]
        + [next_ref[e] for e in range(HALF)]
    )
    for i in range(rows):
        stacked = jnp.concatenate(ext[i : i + TAPS], axis=0)
        taps = jnp.dot(w_ref[i], stacked, preferred_element_type=jnp.float32)
        total = taps[HALF * cp : (HALF + 1) * cp]
        for b in range(TAPS):
            if b == HALF:
                continue
            total = total + pltpu.roll(
                taps[b * cp : (b + 1) * cp], shift_ref[i * TAPS + b], 1
            )
        filtered = total * quad_ref[i]
        filt_ref[i] = filtered
        activated = gelu(filtered).astype(jnp.bfloat16)
        coarse = jnp.dot(
            proj_ref[...], activated, preferred_element_type=jnp.float32
        ).astype(jnp.bfloat16)
        fc_ref[i] = jnp.dot(
            sub_ref[...], coarse, preferred_element_type=jnp.float32
        ).astype(jnp.bfloat16)


def grad_filtered_kernel(gc_ref, filt_ref, proj_t_ref, out_ref):
    rows = filt_ref.shape[0]
    for i in range(rows):
        grad_act = jnp.dot(proj_t_ref[...], gc_ref[i], preferred_element_type=jnp.float32)
        out_ref[i] = (grad_act * gelu_grad(filt_ref[i])).astype(jnp.bfloat16)


def backward_kernel(shift_ref, quad_ref, prev_ref, own_ref, next_ref, w_ref, out_ref):
    rows, cp, _ = own_ref.shape
    channels, width = out_ref.shape[1], out_ref.shape[2]
    ext = (
        [prev_ref[e] for e in range(HALF)]
        + [own_ref[e] for e in range(rows)]
        + [next_ref[e] for e in range(HALF)]
    )
    acc = [None] * rows
    for e in range(rows + 2 * HALF):
        a_lo = max(0, 2 * HALF - e)
        a_hi = min(TAPS - 1, rows - 1 + 2 * HALF - e)
        if a_lo > a_hi:
            continue
        source = ext[e]
        rolled = []
        for b in range(TAPS):
            if b == HALF:
                rolled.append(source)
            else:
                rolled.append(pltpu.roll(source, shift_ref[e * TAPS + b], 1))
        stacked = jnp.concatenate(rolled, axis=0)
        part = jnp.dot(
            w_ref[e, a_lo * cp : (a_hi + 1) * cp, :],
            stacked,
            preferred_element_type=jnp.float32,
        )
        scale = quad_ref[e]
        for a in range(a_lo, a_hi + 1):
            i2 = e + a - 2 * HALF
            piece = part[(a - a_lo) * cp : (a - a_lo + 1) * cp] * scale
            acc[i2] = piece if acc[i2] is None else acc[i2] + piece
    for i2 in range(rows):
        out_ref[i2] = acc[i2][:channels, :width].astype(out_ref.dtype)


def vmem():
    return pl.BlockSpec(memory_space=pltpu.VMEM)


def smem():
    return pl.BlockSpec(memory_space=pltpu.SMEM)


def on_device(latents, filters, project, subcell_maps, verifying_truth, basis_rows, step_rows):
    rows = latents.shape[1]
    channels = latents.shape[2]
    width = latents.shape[3]
    kinds = filters.shape[0]
    variables = project.shape[0]
    subcells = subcell_maps.shape[0]
    cp = round_up(channels, 16)
    vp = round_up(variables, 16)
    svp = round_up(subcells * variables, 16)
    width_p = ring_width(width)
    total_rows = rows * lax.axis_size("lat")
    first = lax.axis_index("lat") * rows

    quad_all = latitude_rows(total_rows, total_rows)
    quad = lax.dynamic_slice_in_dim(quad_all, first, rows, 0)
    couple_factor = subcell_weight(first, rows, total_rows)

    table = jnp.concatenate([filters, jnp.zeros((1,) + filters.shape[1:], filters.dtype)], 0)
    table = pad_axis(pad_axis(table, 1, cp), 2, cp)
    kind_ids = jnp.arange(kinds + 1, dtype=jnp.int32)
    taps_b = jnp.arange(TAPS, dtype=jnp.int32) - HALF

    own_basis = lax.dynamic_slice_in_dim(basis_rows, first, rows, 0).reshape(rows, TAPS, TAPS)
    own_step = lax.dynamic_slice_in_dim(step_rows, first, rows, 0)
    onehot_f = (own_basis[..., None] == kind_ids).astype(filters.dtype)
    w_fwd = jnp.einsum("iabk,koc->iboac", onehot_f, table).reshape(rows, TAPS * cp, TAPS * cp)
    shift_f = jnp.mod(-taps_b[None, :] * own_step[:, None], width_p).reshape(-1)

    pad_basis = jnp.concatenate([basis_rows[:1]] * HALF + [basis_rows] + [basis_rows[-1:]] * HALF, 0)
    pad_step = jnp.concatenate([step_rows[:1]] * HALF + [step_rows] + [step_rows[-1:]] * HALF, 0)
    pad_quad = jnp.concatenate([quad_all[:1]] * HALF + [quad_all] + [quad_all[-1:]] * HALF, 0)
    src_count = rows + 2 * HALF
    src_basis = lax.dynamic_slice_in_dim(pad_basis, first, src_count, 0).reshape(src_count, TAPS, TAPS)
    src_step = lax.dynamic_slice_in_dim(pad_step, first, src_count, 0)
    src_quad = lax.dynamic_slice_in_dim(pad_quad, first, src_count, 0)
    onehot_b = (src_basis[..., None] == kind_ids).astype(filters.dtype)
    w_bwd = jnp.einsum("eabk,koc->eacbo", onehot_b, table).reshape(
        src_count, TAPS * cp, TAPS * cp
    )
    shift_b = jnp.mod(taps_b[None, :] * src_step[:, None], width_p).reshape(-1)

    proj_p = pad_axis(pad_axis(project, 0, vp), 1, cp)
    sub_p = pad_axis(pad_axis(subcell_maps.reshape(subcells * variables, variables), 0, svp), 1, vp)

    own = to_ring(pad_axis(latents[0], 1, cp), width_p)
    low, high = halo(own, "lat", HALF)

    filtered, fc = pl.pallas_call(
        forward_kernel,
        out_shape=(
            jax.ShapeDtypeStruct((rows, cp, width_p), jnp.float32),
            jax.ShapeDtypeStruct((rows, svp, width_p), jnp.bfloat16),
        ),
        in_specs=[smem(), smem()] + [vmem()] * 6,
        out_specs=(vmem(), vmem()),
    )(shift_f, quad, low, own, high, w_fwd, proj_p, sub_p)

    forecast = fc[:, : subcells * variables, :width].reshape(rows, subcells, variables, width)
    fine_local = forecast.transpose(1, 2, 0, 3)[:, None]
    fine_owned = lax.all_to_all(fine_local, "member", split_axis=4, concat_axis=1, tiled=True)

    samples = fine_owned.astype(jnp.float32)
    members = samples.shape[1]
    truth_term = softened_sign(samples - verifying_truth[:, None])
    couple = softened_sign(samples - samples[:, 0:1])
    for n in range(1, members):
        couple = couple + softened_sign(samples - samples[:, n : n + 1])
    grad_owned = couple_factor[:, None, None, :, None] * (truth_term - couple / members)
    grad_fine = lax.all_to_all(grad_owned, "member", split_axis=1, concat_axis=4, tiled=True)
    grad_coarse = jnp.einsum(
        "svu,smvhw->muhw",
        subcell_maps.astype(jnp.float32),
        grad_fine,
        precision=lax.Precision.HIGHEST,
    )[0].astype(jnp.bfloat16)

    gc = to_ring(pad_axis(grad_coarse.transpose(1, 0, 2), 1, vp), width_p)
    proj_t = pad_axis(pad_axis(project.T, 0, cp), 1, vp)
    grad_filtered = pl.pallas_call(
        grad_filtered_kernel,
        out_shape=jax.ShapeDtypeStruct((rows, cp, width_p), jnp.bfloat16),
        in_specs=[vmem()] * 3,
        out_specs=vmem(),
    )(gc, filtered, proj_t)

    g_low, g_high = halo(grad_filtered, "lat", HALF)
    result = pl.pallas_call(
        backward_kernel,
        out_shape=jax.ShapeDtypeStruct((rows, channels, width), jnp.bfloat16),
        in_specs=[smem(), smem()] + [vmem()] * 4,
        out_specs=vmem(),
    )(shift_b, src_quad, g_low, grad_filtered, g_high, w_bwd)
    return result[None]


def solution(mesh):
    placed = (
        P("member", "lat", None, None),
        P(),
        P(),
        P(),
        P(None, None, "lat", "member"),
        P(),
        P(),
    )
    return jax.shard_map(
        on_device,
        mesh=mesh,
        in_specs=placed,
        out_specs=P("member", "lat", None, None),
        check_vma=False,
    )
```

profile of v0, /device:TPU:14, one launch (start us, length us, event | category | flops | bytes accessed | tf_op | source)
XLA Modules:
  0.0 116.8 jit_solution(2998190522567398860)
XLA Ops:
  0.0 0.9 pad_slice_fusion.3
  0.9 1.0 pad.41
  2.0 2.5 %collective-permute-start.1 = (bf16[3,48,768]{2,1,0:T(8,128)(2,1)S(1)}, bf16[3,48,768]{2,1,0:T(8,128)(2,1)S(1)}, u32[]{:S(2)}, u32[]{:S(2)}) collective-permute-start(bf16[3,48,768]{2,1,0:T(8,128)(2,1)S(1)} %pad_maximum_fusion.own_ref), channel_id=1, source_target_pairs={{1,0},{2,1},{3,2},{5,4},{6,5},{7,6},{9,8},{10,9},{11,10},{13,12},{... | collective-permute-start | bytes 663560 | tf_op jit(solution)/shard_map/ppermute | solution.py:42
  4.4 1.3 %collective-permute-start = (bf16[3,48,768]{2,1,0:T(8,128)(2,1)S(1)}, bf16[3,48,768]{2,1,0:T(8,128)(2,1)S(1)}, u32[]{:S(2)}, u32[]{:S(2)}) collective-permute-start(bf16[3,48,768]{2,1,0:T(8,128)(2,1)S(1)} %pad_maximum_fusion.own_ref), channel_id=1, source_target_pairs={{0,1},{1,2},{2,3},{4,5},{5,6},{6,7},{8,9},{9,10},{10,11},{12,13},{... | collective-permute-start | bytes 663560 | tf_op jit(solution)/shard_map/ppermute | solution.py:41
  5.8 0.6 fusion.14
  6.4 0.7 dynamic_slice.21.quad_ref
  7.1 0.7 dynamic_slice.20
  7.8 1.3 %fusion.15 = (s32[1]{0:T(128)}, s32[1]{0:T(128)}) fusion(s32[12]{0:T(128)} %param.14), kind=kLoop, calls=%fused_computation.36 | loop fusion | bytes 16 | tf_op jit(solution)/shard_map/slice | solution.py:187
  9.1 0.7 fusion.13
  9.8 0.7 constant_dynamic-slice_fusion.1
  10.5 1.3 %pad.59.proj_ref = bf16[16,48]{1,0:T(8,128)(2,1)} pad(bf16[5,45]{1,0:T(8,128)(2,1)} %param.10, bf16[]{:T(256)} %constant.56.clone.1), padding=0_11x0_3 | pad | bytes 1988 | tf_op jit(solution)/shard_map/jit(_pad)/pad | solution.py:34
  11.8 0.8 copy.61
  12.8 3.8 %concatenate.19 = f32[18]{0:T(128)S(1)} concatenate(f32[1]{0:T(128)} %get-tuple-element.24, f32[1]{0:T(128)} %get-tuple-element.24, f32[1]{0:T(128)} %get-tuple-element.24, f32[12]{0:T(128)S(1)} %multiply_cosine_fusion.1, f32[1]{0:T(128)} %get-tuple-element.23, f32[1]{0:T(128)} %get-tuple-element.23, f32[1]{0:T(128)} %get-tuple-element.23), dimensions={0} | concatenate | bytes 144 | tf_op jit(solution)/shard_map/concatenate | solution.py:188
  16.6 0.7 dynamic_slice.19.quad_ref
  17.2 4.5 %concatenate.18 = s32[18]{0:T(128)S(1)} concatenate(s32[1]{0:T(128)} %get-tuple-element.26, s32[1]{0:T(128)} %get-tuple-element.26, s32[1]{0:T(128)} %get-tuple-element.26, s32[12]{0:T(128)} %param.14, s32[1]{0:T(128)} %get-tuple-element.25, s32[1]{0:T(128)} %get-tuple-element.25, s32[1]{0:T(128)} %get-tuple-element.25), dimensions={0} | concatenate | bytes 144 | tf_op jit(solution)/shard_map/concatenate | solution.py:187
  22.0 0.7 copy.66
  22.7 0.6 pad.60.sub_ref
  23.4 0.8 concatenate.23
  24.3 0.6 pad.61.proj_t_ref
  25.1 0.9 copy.52
  25.9 0.7 convolution_bitcast_fusion.1
  26.7 0.5 copy.53
  27.2 2.1 %reshape.86.w_ref = bf16[3,336,336]{2,1,0:T(8,128)(2,1)} reshape(bf16[3,7,48,7,48]{4,3,2,1,0:T(8,128)(2,1)S(1)} %copy.53) | data formatting | bytes 1354752 | tf_op jit(solution)/shard_map/reshape | solution.py:183
  29.3 0.6 and_select_fusion.shift_ref
  29.9 0.7 copy-done.3
  30.6 0.7 copy-done.4
  31.3 4.5 %shard_map.82 = (f32[3,48,768]{2,1,0:T(8,128)}, bf16[3,32,768]{2,1,0:T(8,128)(2,1)}) custom-call(s32[21]{0:T(128)} %and_select_fusion.shift_ref, f32[3]{0:T(128)} %dynamic_slice.21.quad_ref, bf16[3,48,768]{2,1,0:T(8,128)(2,1)} %copy-done.4, bf16[3,48,768]{2,1,0:T(8,128)(2,1)} %copy-done, bf16[3,48,768]{2,1,0:T(8,128)(2,1)} %copy-done.3, ...), custom_call_target="tpu_custom_call" | custom-call | tf_op jit(solution)/shard_map/pallas_call | solution.py:205
  35.8 0.9 slice.71
  36.8 2.8 %copy.57 = bf16[4,1,5,3,720]{2,0,3,1,4:T(4,128)(2,1)S(1)} copy(bf16[4,1,5,3,720]{4,3,2,0,1:T(4,128)(2,1)S(1)} %bitcast.73) | data formatting | bytes 172800 | tf_op jit(solution)/shard_map/broadcast_in_dim | solution.py:216
  39.6 3.0 %reshape.99 = bf16[8,2,2700]{2,1,0:T(2,128)(2,1)} reshape(bf16[720,1,3,4,5]{4,3,2,1,0:T(4,128)(2,1)S(1)} %bitcast.67) | data formatting | bytes 172800
  42.5 5.3 %all-to-all-start = ((bf16[8,2,2700]{2,1,0:T(2,128)(2,1)}), bf16[8,2,2700]{2,1,0:T(2,128)(2,1)S(1)}, u32[]{:S(2)}, u32[]{:S(2)}) async-start(bf16[8,2,2700]{2,1,0:T(2,128)(2,1)} %reshape.99), calls=%async_computation | async-start | bytes 180224 | tf_op jit(solution)/shard_map/all_to_all | solution.py:217
  48.0 4.9 %all-to-all-done = bf16[8,2,2700]{2,1,0:T(2,128)(2,1)S(1)} async-done(((bf16[8,2,2700]{2,1,0:T(2,128)(2,1)}), bf16[8,2,2700]{2,1,0:T(2,128)(2,1)S(1)}, u32[]{:S(2)}, u32[]{:S(2)}) %all-to-all-start) | async-done | bytes 86432 | tf_op jit(solution)/shard_map/all_to_all | solution.py:217
  52.9 2.0 %reshape.100 = bf16[720,1,3,4,5]{4,3,2,1,0:T(4,128)(2,1)S(1)} reshape(bf16[8,2,2700]{2,1,0:T(2,128)(2,1)S(1)} %all-to-all-done) | data formatting | bytes 172800
  54.9 2.0 %copy.58 = bf16[4,1,5,3,720]{4,0,3,2,1:T(4,128)(2,1)S(1)} copy(bf16[4,1,5,3,720]{2,0,3,1,4:T(4,128)(2,1)S(1)} %bitcast.68) | data formatting | bytes 172800 | tf_op jit(solution)/shard_map/all_to_all | solution.py:217
  57.7 0.8 copy.59
  58.5 4.5 %all-to-all-start.1 = ((f32[4,8,5,3,90]{4,0,3,2,1:T(4,128)}), f32[4,8,5,3,90]{4,0,3,2,1:T(4,128)S(1)}, u32[]{:S(2)}, u32[]{:S(2)}) async-start(f32[4,8,5,3,90]{4,0,3,2,1:T(4,128)} %copy.59), calls=%async_computation.1 | async-start | bytes 491520 | tf_op jit(solution)/shard_map/all_to_all | solution.py:226
  63.0 5.2 %convolution_bitcast_fusion = bf16[9,7,48,7,48]{2,0,3,1,4:T(8,128)(2,1)} fusion(s32[9,7,7]{0,2,1:T(8,128)S(1)} %copy.62, bf16[5,45,45]{2,0,1:T(8,128)(2,1)S(1)} %copy.52), kind=kOutput, calls=%fused_computation | convolution fusion | flops 12195414 | bytes 2054142 | tf_op jit(solution)/shard_map/eabk,koc->eacbo/dot_general | solution.py:194
  68.2 14.7 %copy.63 = bf16[9,7,48,7,48]{4,3,2,1,0:T(8,128)(2,1)} copy(bf16[9,7,48,7,48]{2,0,3,1,4:T(8,128)(2,1)} %convolution_bitcast_fusion) | data formatting | bytes 4064256 | tf_op jit(solution)/shard_map/eabk,koc->eacbo/transpose | solution.py:194
  82.9 8.6 %reshape.90.w_ref = bf16[9,336,336]{2,1,0:T(8,128)(2,1)} reshape(bf16[9,7,48,7,48]{4,3,2,1,0:T(8,128)(2,1)} %copy.63) | data formatting | bytes 4064256 | tf_op jit(solution)/shard_map/reshape | solution.py:194
  92.0 0.7 pad_maximum_fusion.1.gc_ref
  92.7 2.0 %shard_map.83.own_ref = bf16[3,48,768]{2,1,0:T(8,128)(2,1)} custom-call(bf16[3,16,768]{2,1,0:T(8,128)(2,1)} %pad_maximum_fusion.1.gc_ref, f32[3,48,768]{2,1,0:T(8,128)} %get-tuple-element.8.filt_ref, bf16[48,16]{1,0:T(8,128)(2,1)} %pad.61.proj_t_ref), custom_call_target="tpu_custom_call" | custom-call | tf_op jit(solution)/shard_map/pallas_call | solution.py:236
  94.8 4.6 %collective-permute-start.3 = (bf16[3,48,768]{2,1,0:T(8,128)(2,1)}, bf16[3,48,768]{2,1,0:T(8,128)(2,1)S(1)}, u32[]{:S(2)}, u32[]{:S(2)}) collective-permute-start(bf16[3,48,768]{2,1,0:T(8,128)(2,1)} %shard_map.83.own_ref), channel_id=1, source_target_pairs={{1,0},{2,1},{3,2},{5,4},{6,5},{7,6},{9,8},{10,9},{11,10},{13,12},{... | collective-permute-start | bytes 663560 | tf_op jit(solution)/shard_map/ppermute | solution.py:42
  99.3 1.3 %collective-permute-start.2 = (bf16[3,48,768]{2,1,0:T(8,128)(2,1)}, bf16[3,48,768]{2,1,0:T(8,128)(2,1)S(1)}, u32[]{:S(2)}, u32[]{:S(2)}) collective-permute-start(bf16[3,48,768]{2,1,0:T(8,128)(2,1)} %shard_map.83.own_ref), channel_id=1, source_target_pairs={{0,1},{1,2},{2,3},{4,5},{5,6},{6,7},{8,9},{9,10},{10,11},{12,13},{... | collective-permute-start | bytes 663560 | tf_op jit(solution)/shard_map/ppermute | solution.py:41
  100.6 0.6 and_select_fusion.1.shift_ref
  101.2 3.4 %collective-permute-done.3.next_ref = bf16[3,48,768]{2,1,0:T(8,128)(2,1)S(1)} collective-permute-done((bf16[3,48,768]{2,1,0:T(8,128)(2,1)}, bf16[3,48,768]{2,1,0:T(8,128)(2,1)S(1)}, u32[]{:S(2)}, u32[]{:S(2)}) %collective-permute-start.3) | collective-permute-done | bytes 221216 | tf_op jit(solution)/shard_map/ppermute | solution.py:42
  104.6 7.4 %collective-permute-done.2.prev_ref = bf16[3,48,768]{2,1,0:T(8,128)(2,1)S(1)} collective-permute-done((bf16[3,48,768]{2,1,0:T(8,128)(2,1)}, bf16[3,48,768]{2,1,0:T(8,128)(2,1)S(1)}, u32[]{:S(2)}, u32[]{:S(2)}) %collective-permute-start.2) | collective-permute-done | bytes 221216 | tf_op jit(solution)/shard_map/ppermute | solution.py:41
  112.0 0.7 copy-done.2
  112.8 4.1 %shard_map.84 = bf16[3,45,720]{2,1,0:T(8,128)(2,1)} custom-call(s32[63]{0:T(128)} %and_select_fusion.1.shift_ref, f32[9]{0:T(128)} %dynamic_slice.19.quad_ref, bf16[3,48,768]{2,1,0:T(8,128)(2,1)} %copy-done.2, bf16[3,48,768]{2,1,0:T(8,128)(2,1)} %shard_map.83.own_ref, bf16[3,48,768]{2,1,0:T(8,128)(2,1)} %copy-done.1, bf16[9,336,336]{2,1,0:T(8,128)(2,1)} %reshape.90.w_ref), custom_call_target="tpu_custom_call" | custom-call | tf_op jit(solution)/shard_map/pallas_call | solution.py:244
  (41 shorter events, 2.4 us)
Async XLA Ops:
  1.9 25.3 %copy-start = (bf16[3,48,768]{2,1,0:T(8,128)(2,1)}, bf16[3,48,768]{2,1,0:T(8,128)(2,1)S(1)}, u32[]{:S(2)}) copy-start(bf16[3,48,768]{2,1,0:T(8,128)(2,1)S(1)} %pad_maximum_fusion.own_ref) | copy-start | bytes 663556
  2.0 28.0 %collective-permute-start.1 = (bf16[3,48,768]{2,1,0:T(8,128)(2,1)S(1)}, bf16[3,48,768]{2,1,0:T(8,128)(2,1)S(1)}, u32[]{:S(2)}, u32[]{:S(2)}) collective-permute-start(bf16[3,48,768]{2,1,0:T(8,128)(2,1)S(1)} %pad_maximum_fusion.own_ref), channel_id=1, source_target_pairs={{1,0},{2,1},{3,2},{5,4},{6,5},{7,6},{9,8},{10,9},{11,10},{13,12},{... | collective-permute-start | bytes 663560 | tf_op jit(solution)/shard_map/ppermute | solution.py:42
  4.4 25.5 %collective-permute-start = (bf16[3,48,768]{2,1,0:T(8,128)(2,1)S(1)}, bf16[3,48,768]{2,1,0:T(8,128)(2,1)S(1)}, u32[]{:S(2)}, u32[]{:S(2)}) collective-permute-start(bf16[3,48,768]{2,1,0:T(8,128)(2,1)S(1)} %pad_maximum_fusion.own_ref), channel_id=1, source_target_pairs={{0,1},{1,2},{2,3},{4,5},{5,6},{6,7},{8,9},{9,10},{10,11},{12,13},{... | collective-permute-start | bytes 663560 | tf_op jit(solution)/shard_map/ppermute | solution.py:41
  29.9 0.7 copy-start.3
  30.6 0.7 copy-start.4
  36.8 11.1 %copy-start.7 = (f32[4]{0:T(128)S(1)}, f32[4]{0:T(128)}, u32[]{:S(2)}) copy-start(f32[4]{0:T(128)} %constant.59.clone) | copy-start | bytes 52
  42.5 10.3 %all-to-all-start = ((bf16[8,2,2700]{2,1,0:T(2,128)(2,1)}), bf16[8,2,2700]{2,1,0:T(2,128)(2,1)S(1)}, u32[]{:S(2)}, u32[]{:S(2)}) async-start(bf16[8,2,2700]{2,1,0:T(2,128)(2,1)} %reshape.99), calls=%async_computation | async-start | bytes 180224 | tf_op jit(solution)/shard_map/all_to_all | solution.py:217
  48.0 9.2 %copy-start.5 = (f32[4,5,3,90]{3,0,2,1:T(4,128)S(1)}, f32[4,5,3,90]{3,0,2,1:T(4,128)}, u32[]{:S(2)}) copy-start(f32[4,5,3,90]{3,0,2,1:T(4,128)} %param.12) | copy-start | bytes 64804
  58.5 33.0 %all-to-all-start.1 = ((f32[4,8,5,3,90]{4,0,3,2,1:T(4,128)}), f32[4,8,5,3,90]{4,0,3,2,1:T(4,128)S(1)}, u32[]{:S(2)}, u32[]{:S(2)}) async-start(f32[4,8,5,3,90]{4,0,3,2,1:T(4,128)} %copy.59), calls=%async_computation.1 | async-start | bytes 491520 | tf_op jit(solution)/shard_map/all_to_all | solution.py:226
  82.9 8.8 %copy-start.6 = (bf16[4,5,5]{2,0,1:T(4,128)(2,1)S(1)}, bf16[4,5,5]{2,0,1:T(4,128)(2,1)}, u32[]{:S(2)}) copy-start(bf16[4,5,5]{2,0,1:T(4,128)(2,1)} %param.11) | copy-start | bytes 604
  94.8 9.9 %collective-permute-start.3 = (bf16[3,48,768]{2,1,0:T(8,128)(2,1)}, bf16[3,48,768]{2,1,0:T(8,128)(2,1)S(1)}, u32[]{:S(2)}, u32[]{:S(2)}) collective-permute-start(bf16[3,48,768]{2,1,0:T(8,128)(2,1)} %shard_map.83.own_ref), channel_id=1, source_target_pairs={{1,0},{2,1},{3,2},{5,4},{6,5},{7,6},{9,8},{10,9},{11,10},{13,12},{... | collective-permute-start | bytes 663560 | tf_op jit(solution)/shard_map/ppermute | solution.py:42
  99.3 12.7 %collective-permute-start.2 = (bf16[3,48,768]{2,1,0:T(8,128)(2,1)}, bf16[3,48,768]{2,1,0:T(8,128)(2,1)S(1)}, u32[]{:S(2)}, u32[]{:S(2)}) collective-permute-start(bf16[3,48,768]{2,1,0:T(8,128)(2,1)} %shard_map.83.own_ref), channel_id=1, source_target_pairs={{0,1},{1,2},{2,3},{4,5},{5,6},{6,7},{8,9},{9,10},{10,11},{12,13},{... | collective-permute-start | bytes 663560 | tf_op jit(solution)/shard_map/ppermute | solution.py:41
  104.6 7.4 %copy-start.1 = (bf16[3,48,768]{2,1,0:T(8,128)(2,1)}, bf16[3,48,768]{2,1,0:T(8,128)(2,1)S(1)}, u32[]{:S(2)}) copy-start(bf16[3,48,768]{2,1,0:T(8,128)(2,1)S(1)} %collective-permute-done.3.next_ref) | copy-start | bytes 663556
  112.0 0.7 copy-start.2
where the time goes:
time: 118 us; the launch traced here: 117 us
  local copies, waits for them, and re-layouts  61.9 us (52%)
  starting transfers between devices  19.5 us (17%)
  waiting for transfers between devices  15.7 us (13%)
  Pallas kernels  10.6 us (9%)
  matrix products  6.16 us (5%)
  other arithmetic  2.73 us (2%)
    transpose x1, local copies, waits for them, and re-layouts, on_device(): jnp.einsum('eabk,koc->eacbo', onehot_b, table)  14.7 us
    unnamed x20, local copies, waits for them, and re-layouts  8.77 us
    reshape x1, local copies, waits for them, and re-layouts, on_device(): jnp.einsum('eabk,koc->eacbo', onehot_b, table)  8.6 us
    ppermute x2, waiting for transfers between devices, halo(): low = lax.ppermute(block[block.shape[0] - width:], axis_name, forward)  7.41 us
    ppermute x2, starting transfers between devices, halo(): high = lax.ppermute(block[:width], axis_name, backward)  7.01 us
    all_to_all x1, starting transfers between devices, on_device(): lax.all_to_all(fine_local, 'member', split_axis=4, concat_axis=1, tiled=T...  5.32 us
    dot_general x1, matrix products, on_device(): jnp.einsum('eabk,koc->eacbo', onehot_b, table)  5.18 us
    all_to_all x1, waiting for transfers between devices, on_device(): lax.all_to_all(fine_local, 'member', split_axis=4, concat_axis=1, tiled=T...  4.89 us
  transfers between devices with their start and end apart: 6, of which 3 were waited for; matrix products, arithmetic and copies ran while one was open for 46% of the time, Pallas kernels for 0%

commit v1 on v0

--- a/solution.py
+++ b/solution.py
@@ -74,25 +74,37 @@
     return 0.5 * (1.0 + t) + x * (0.5 * (1.0 - t * t)) * d_inner
 
 
-def forward_kernel(shift_ref, quad_ref, prev_ref, own_ref, next_ref, w_ref, proj_ref,
-                   sub_ref, filt_ref, fc_ref):
-    rows, cp, _ = own_ref.shape
+def forward_kernel(basis_ref, step_ref, quad_ref, prev_ref, own_ref, next_ref, table_ref,
+                   proj_ref, sub_ref, filt_ref, fc_ref):
+    rows, cp, width_p = own_ref.shape
+    first = lax.axis_index("lat") * rows
     ext = (
         [prev_ref[e] for e in range(HALF)]
         + [own_ref[e] for e in range(rows)]
         + [next_ref[e] for e in range(HALF)]
     )
     for i in range(rows):
+        g = first + i
+        step = step_ref[g]
+        weights = jnp.concatenate(
+            [
+                jnp.concatenate(
+                    [table_ref[0, basis_ref[g * TAPS * TAPS + a * TAPS + b]] for a in range(TAPS)],
+                    axis=1,
+                )
+                for b in range(TAPS)
+            ],
+            axis=0,
+        )
         stacked = jnp.concatenate(ext[i : i + TAPS], axis=0)
-        taps = jnp.dot(w_ref[i], stacked, preferred_element_type=jnp.float32)
+        taps = jnp.dot(weights, stacked, preferred_element_type=jnp.float32)
         total = taps[HALF * cp : (HALF + 1) * cp]
         for b in range(TAPS):
             if b == HALF:
                 continue
-            total = total + pltpu.roll(
-                taps[b * cp : (b + 1) * cp], shift_ref[i * TAPS + b], 1
-            )
-        filtered = total * quad_ref[i]
+            shift = lax.rem((HALF - b) * step + width_p, width_p)
+            total = total + pltpu.roll(taps[b * cp : (b + 1) * cp], shift, 1)
+        filtered = total * quad_ref[g]
         filt_ref[i] = filtered
         activated = gelu(filtered).astype(jnp.bfloat16)
         coarse = jnp.dot(
@@ -110,9 +122,12 @@
         out_ref[i] = (grad_act * gelu_grad(filt_ref[i])).astype(jnp.bfloat16)
 
 
-def backward_kernel(shift_ref, quad_ref, prev_ref, own_ref, next_ref, w_ref, out_ref):
-    rows, cp, _ = own_ref.shape
+def backward_kernel(basis_ref, step_ref, quad_ref, prev_ref, own_ref, next_ref, table_ref,
+                    out_ref):
+    rows, cp, width_p = own_ref.shape
     channels, width = out_ref.shape[1], out_ref.shape[2]
+    total_rows = step_ref.shape[0]
+    first = lax.axis_index("lat") * rows
     ext = (
         [prev_ref[e] for e in range(HALF)]
         + [own_ref[e] for e in range(rows)]
@@ -124,20 +139,29 @@
         a_hi = min(TAPS - 1, rows - 1 + 2 * HALF - e)
         if a_lo > a_hi:
             continue
+        g = jnp.clip(first - HALF + e, 0, total_rows - 1)
+        step = step_ref[g]
+        weights = jnp.concatenate(
+            [
+                jnp.concatenate(
+                    [table_ref[1, basis_ref[g * TAPS * TAPS + a * TAPS + b]] for b in range(TAPS)],
+                    axis=1,
+                )
+                for a in range(a_lo, a_hi + 1)
+            ],
+            axis=0,
+        )
         source = ext[e]
         rolled = []
         for b in range(TAPS):
             if b == HALF:
                 rolled.append(source)
             else:
-                rolled.append(pltpu.roll(source, shift_ref[e * TAPS + b], 1))
+                shift = lax.rem((b - HALF) * step + width_p, width_p)
+                rolled.append(pltpu.roll(source, shift, 1))
         stacked = jnp.concatenate(rolled, axis=0)
-        part = jnp.dot(
-            w_ref[e, a_lo * cp : (a_hi + 1) * cp, :],
-            stacked,
-            preferred_element_type=jnp.float32,
-        )
-        scale = quad_ref[e]
+        part = jnp.dot(weights, stacked, preferred_element_type=jnp.float32)
+        scale = quad_ref[g]
         for a in range(a_lo, a_hi + 1):
             i2 = e + a - 2 * HALF
             piece = part[(a - a_lo) * cp : (a - a_lo + 1) * cp] * scale
@@ -158,7 +182,6 @@
     rows = latents.shape[1]
     channels = latents.shape[2]
     width = latents.shape[3]
-    kinds = filters.shape[0]
     variables = project.shape[0]
     subcells = subcell_maps.shape[0]
     cp = round_up(channels, 16)
@@ -169,32 +192,12 @@
     first = lax.axis_index("lat") * rows
 
     quad_all = latitude_rows(total_rows, total_rows)
-    quad = lax.dynamic_slice_in_dim(quad_all, first, rows, 0)
     couple_factor = subcell_weight(first, rows, total_rows)
 
     table = jnp.concatenate([filters, jnp.zeros((1,) + filters.shape[1:], filters.dtype)], 0)
     table = pad_axis(pad_axis(table, 1, cp), 2, cp)
-    kind_ids = jnp.arange(kinds + 1, dtype=jnp.int32)
-    taps_b = jnp.arange(TAPS, dtype=jnp.int32) - HALF
-
-    own_basis = lax.dynamic_slice_in_dim(basis_rows, first, rows, 0).reshape(rows, TAPS, TAPS)
-    own_step = lax.dynamic_slice_in_dim(step_rows, first, rows, 0)
-    onehot_f = (own_basis[..., None] == kind_ids).astype(filters.dtype)
-    w_fwd = jnp.einsum("iabk,koc->iboac", onehot_f, table).reshape(rows, TAPS * cp, TAPS * cp)
-    shift_f = jnp.mod(-taps_b[None, :] * own_step[:, None], width_p).reshape(-1)
-
-    pad_basis = jnp.concatenate([basis_rows[:1]] * HALF + [basis_rows] + [basis_rows[-1:]] * HALF, 0)
-    pad_step = jnp.concatenate([step_rows[:1]] * HALF + [step_rows] + [step_rows[-1:]] * HALF, 0)
-    pad_quad = jnp.concatenate([quad_all[:1]] * HALF + [quad_all] + [quad_all[-1:]] * HALF, 0)
-    src_count = rows + 2 * HALF
-    src_basis = lax.dynamic_slice_in_dim(pad_basis, first, src_count, 0).reshape(src_count, TAPS, TAPS)
-    src_step = lax.dynamic_slice_in_dim(pad_step, first, src_count, 0)
-    src_quad = lax.dynamic_slice_in_dim(pad_quad, first, src_count, 0)
-    onehot_b = (src_basis[..., None] == kind_ids).astype(filters.dtype)
-    w_bwd = jnp.einsum("eabk,koc->eacbo", onehot_b, table).reshape(
-        src_count, TAPS * cp, TAPS * cp
-    )
-    shift_b = jnp.mod(taps_b[None, :] * src_step[:, None], width_p).reshape(-1)
+    tables = jnp.stack([table, table.transpose(0, 2, 1)])
+    basis_flat = basis_rows.reshape(-1)
 
     proj_p = pad_axis(pad_axis(project, 0, vp), 1, cp)
     sub_p = pad_axis(pad_axis(subcell_maps.reshape(subcells * variables, variables), 0, svp), 1, vp)
@@ -208,9 +211,9 @@
             jax.ShapeDtypeStruct((rows, cp, width_p), jnp.float32),
             jax.ShapeDtypeStruct((rows, svp, width_p), jnp.bfloat16),
         ),
-        in_specs=[smem(), smem()] + [vmem()] * 6,
+        in_specs=[smem(), smem(), smem()] + [vmem()] * 6,
         out_specs=(vmem(), vmem()),
-    )(shift_f, quad, low, own, high, w_fwd, proj_p, sub_p)
+    )(basis_flat, step_rows, quad_all, low, own, high, tables, proj_p, sub_p)
 
     forecast = fc[:, : subcells * variables, :width].reshape(rows, subcells, variables, width)
     fine_local = forecast.transpose(1, 2, 0, 3)[:, None]
@@ -244,9 +247,9 @@
     result = pl.pallas_call(
         backward_kernel,
         out_shape=jax.ShapeDtypeStruct((rows, channels, width), jnp.bfloat16),
-        in_specs=[smem(), smem()] + [vmem()] * 4,
+        in_specs=[smem(), smem(), smem()] + [vmem()] * 4,
         out_specs=vmem(),
-    )(shift_b, src_quad, g_low, grad_filtered, g_high, w_bwd)
+    )(basis_flat, step_rows, quad_all, g_low, grad_filtered, g_high, tables)
     return result[None]
 
 

time: 118 us -> 81.7 us (0.69)
  the two profiles are of different devices: /device:TPU:14 before, /device:TPU:0 now
where the time goes in v1:
time: 81.7 us; the launch traced here: 81 us
  waiting for transfers between devices  27.3 us (33%)
  local copies, waits for them, and re-layouts  21.1 us (26%)
  starting transfers between devices  19.1 us (23%)
  Pallas kernels  10.4 us (13%)
  other arithmetic  2.64 us (3%)
    ppermute x2, waiting for transfers between devices, halo(): high = lax.ppermute(block[:width], axis_name, backward)  9.3 us
    all_to_all x1, waiting for transfers between devices, on_device(): lax.all_to_all(grad_owned, 'member', split_axis=1, concat_axis=4, tiled=T...  8.57 us
    ppermute x2, starting transfers between devices, halo(): low = lax.ppermute(block[block.shape[0] - width:], axis_name, forward)  8.25 us
    unnamed x22, local copies, waits for them, and re-layouts  7.51 us
    all_to_all x1, waiting for transfers between devices, on_device(): lax.all_to_all(fine_local, 'member', split_axis=4, concat_axis=1, tiled=T...  6.1 us
    all_to_all x1, starting transfers between devices, on_device(): lax.all_to_all(fine_local, 'member', split_axis=4, concat_axis=1, tiled=T...  4.88 us
    pallas_call x1, Pallas kernels, on_device(): pl.pallas_call(forward_kernel, out_shape=(jax.ShapeDtypeStruct((rows, cp,...  4.5 us
    pallas_call x1, Pallas kernels, on_device(): pl.pallas_call(backward_kernel, out_shape=jax.ShapeDtypeStruct((rows, cha...  3.84 us
  transfers between devices with their start and end apart: 6, of which 5 were waited for; matrix products, arithmetic and copies ran while one was open for 9% of the time, Pallas kernels for 0%

profile of v1, /device:TPU:0, one launch (start us, length us, event | category | flops | bytes accessed | tf_op | source)
XLA Modules:
  0.0 81.0 jit_solution(13983679780331563642)
XLA Ops:
  0.0 0.9 %pad_slice_fusion.3 = (bf16[3,48,24]{2,1,0:T(8,128)(2,1)S(1)}, bf16[3,48,24]{2,1,0:T(8,128)(2,1)S(1)}) fusion(bf16[3,45,720]{2,1,0:T(8,128)(2,1)} %bitcast.61), kind=kLoop, calls=%fused_computation.16 | loop fusion | bytes 208224 | tf_op jit(solution)/shard_map/slice | solution.py:27
  0.9 1.0 %pad.41 = bf16[3,48,720]{2,1,0:T(8,128)(2,1)S(1)} pad(bf16[3,45,720]{2,1,0:T(8,128)(2,1)} %bitcast.62, bf16[]{:T(256)} %constant.31.clone.1), padding=0_0x0_3x0_0 | pad | bytes 401762 | tf_op jit(solution)/shard_map/jit(_pad)/pad | solution.py:34
  1.8 0.1 pad_maximum_fusion.own_ref
  2.0 4.9 %collective-permute-start = (bf16[3,48,768]{2,1,0:T(8,128)(2,1)S(1)}, bf16[3,48,768]{2,1,0:T(8,128)(2,1)S(1)}, u32[]{:S(2)}, u32[]{:S(2)}) collective-permute-start(bf16[3,48,768]{2,1,0:T(8,128)(2,1)S(1)} %pad_maximum_fusion.own_ref), channel_id=1, source_target_pairs={{0,1},{1,2},{2,3},{4,5},{5,6},{6,7},{8,9},{9,10},{10,11},{12,13},{... | collective-permute-start | bytes 663560 | tf_op jit(solution)/shard_map/ppermute | solution.py:41
  6.8 1.3 %collective-permute-start.1 = (bf16[3,48,768]{2,1,0:T(8,128)(2,1)S(1)}, bf16[3,48,768]{2,1,0:T(8,128)(2,1)S(1)}, u32[]{:S(2)}, u32[]{:S(2)}) collective-permute-start(bf16[3,48,768]{2,1,0:T(8,128)(2,1)S(1)} %pad_maximum_fusion.own_ref), channel_id=1, source_target_pairs={{1,0},{2,1},{3,2},{5,4},{6,5},{7,6},{9,8},{10,9},{11,10},{13,12},{... | collective-permute-start | bytes 663560 | tf_op jit(solution)/shard_map/ppermute | solution.py:42
  8.1 0.6 multiply_cosine_fusion.1.quad_ref
  8.7 1.0 %copy.45 = bf16[5,45,45]{1,2,0:T(8,128)(2,1)S(1)} copy(bf16[5,45,45]{2,1,0:T(8,128)(2,1)} %param.9) | data formatting | bytes 40500 | tf_op args[1]
  9.7 0.1 copy.46
  9.8 1.4 %reshape.59.basis_ref = s32[588]{0:T(1024)} reshape(s32[12,49]{1,0:T(8,128)} %param.13) | data formatting | bytes 4704 | tf_op jit(solution)/shard_map/reshape | solution.py:200
  11.2 0.7 copy.56
  11.9 0.6 pad.62.sub_ref
  12.5 1.3 %pad.61.proj_ref = bf16[16,48]{1,0:T(8,128)(2,1)} pad(bf16[5,45]{1,0:T(8,128)(2,1)} %param.10, bf16[]{:T(256)} %constant.31.clone.1), padding=0_11x0_3 | pad | bytes 1988 | tf_op jit(solution)/shard_map/jit(_pad)/pad | solution.py:34
  13.8 0.7 pad_maximum_fusion.1.table_ref
  14.5 0.0 collective-permute-done.prev_ref
  14.5 3.7 %collective-permute-done.1.next_ref = bf16[3,48,768]{2,1,0:T(8,128)(2,1)S(1)} collective-permute-done((bf16[3,48,768]{2,1,0:T(8,128)(2,1)S(1)}, bf16[3,48,768]{2,1,0:T(8,128)(2,1)S(1)}, u32[]{:S(2)}, u32[]{:S(2)}) %collective-permute-start.1) | collective-permute-done | bytes 221216 | tf_op jit(solution)/shard_map/ppermute | solution.py:42
  18.2 0.7 copy-done.2
  18.9 4.5 %shard_map.82 = (f32[3,48,768]{2,1,0:T(8,128)}, bf16[3,32,768]{2,1,0:T(8,128)(2,1)}) custom-call(s32[588]{0:T(1024)} %reshape.59.basis_ref, s32[12]{0:T(128)} %step_ref.3, f32[12]{0:T(128)} %multiply_cosine_fusion.1.quad_ref, bf16[3,48,768]{2,1,0:T(8,128)(2,1)} %copy-done.1, bf16[3,48,768]{2,1,0:T(8,128)(2,1)} %copy-done, bf16[3,48,768]{2,1,0:T(8,128)(2,1)} %copy-done.2, ...), custom_call_target="tpu_custom_call" | custom-call | tf_op jit(solution)/shard_map/pallas_call | solution.py:208
  23.4 0.9 %slice.41 = bf16[3,20,720]{2,1,0:T(8,128)(2,1)S(1)} slice(bf16[3,32,768]{2,1,0:T(8,128)(2,1)} %get-tuple-element.7), slice={[0:3], [0:20], [0:720]} | slice | bytes 172800 | tf_op jit(solution)/shard_map/slice | solution.py:218
  24.3 0.0 copy-start.8
  24.3 2.8 %copy.50 = bf16[4,1,5,3,720]{2,0,3,1,4:T(4,128)(2,1)S(1)} copy(bf16[4,1,5,3,720]{4,3,2,0,1:T(4,128)(2,1)S(1)} %bitcast.63) | data formatting | bytes 172800 | tf_op jit(solution)/shard_map/broadcast_in_dim | solution.py:219
  27.1 3.0 %reshape.68 = bf16[8,2,2700]{2,1,0:T(2,128)(2,1)} reshape(bf16[720,1,3,4,5]{4,3,2,1,0:T(4,128)(2,1)S(1)} %bitcast.57) | data formatting | bytes 172800
  30.1 4.9 %all-to-all-start = ((bf16[8,2,2700]{2,1,0:T(2,128)(2,1)}), bf16[8,2,2700]{2,1,0:T(2,128)(2,1)S(1)}, u32[]{:S(2)}, u32[]{:S(2)}) async-start(bf16[8,2,2700]{2,1,0:T(2,128)(2,1)} %reshape.68), calls=%async_computation | async-start | bytes 180224 | tf_op jit(solution)/shard_map/all_to_all | solution.py:220
  35.0 0.1 multiply_cosine_fusion
  35.1 0.0 copy-start.5
  35.1 6.1 %all-to-all-done = bf16[8,2,2700]{2,1,0:T(2,128)(2,1)S(1)} async-done(((bf16[8,2,2700]{2,1,0:T(2,128)(2,1)}), bf16[8,2,2700]{2,1,0:T(2,128)(2,1)S(1)}, u32[]{:S(2)}, u32[]{:S(2)}) %all-to-all-start) | async-done | bytes 86432 | tf_op jit(solution)/shard_map/all_to_all | solution.py:220
  41.2 2.0 %reshape.69 = bf16[720,1,3,4,5]{4,3,2,1,0:T(4,128)(2,1)S(1)} reshape(bf16[8,2,2700]{2,1,0:T(2,128)(2,1)S(1)} %all-to-all-done) | data formatting | bytes 172800
  43.2 0.0 copy-start.7
  43.3 2.0 %copy.51 = bf16[4,1,5,3,720]{4,0,3,2,1:T(4,128)(2,1)S(1)} copy(bf16[4,1,5,3,720]{2,0,3,1,4:T(4,128)(2,1)S(1)} %bitcast.58) | data formatting | bytes 172800 | tf_op jit(solution)/shard_map/all_to_all | solution.py:220
  45.2 0.0 copy-start.6
  45.2 0.2 reshape.64
  45.4 0.2 fusion.3
  45.6 0.5 subtract_multiply_fusion
  46.0 0.8 copy.52
  46.8 3.4 %all-to-all-start.1 = ((f32[4,8,5,3,90]{4,0,3,2,1:T(4,128)}), f32[4,8,5,3,90]{4,0,3,2,1:T(4,128)S(1)}, u32[]{:S(2)}, u32[]{:S(2)}) async-start(f32[4,8,5,3,90]{4,0,3,2,1:T(4,128)} %copy.52), calls=%async_computation.1 | async-start | bytes 491520 | tf_op jit(solution)/shard_map/all_to_all | solution.py:229
  50.2 0.1 copy.54
  50.4 0.6 pad.63.proj_t_ref
  51.0 8.6 %all-to-all-done.1 = f32[4,8,5,3,90]{4,0,3,2,1:T(4,128)S(1)} async-done(((f32[4,8,5,3,90]{4,0,3,2,1:T(4,128)}), f32[4,8,5,3,90]{4,0,3,2,1:T(4,128)S(1)}, u32[]{:S(2)}, u32[]{:S(2)}) %all-to-all-start.1) | async-done | bytes 172832 | tf_op jit(solution)/shard_map/all_to_all | solution.py:229
  59.6 0.2 reshape.62
  59.7 0.2 fusion.1
  60.0 0.1 pad_slice_fusion.1
  60.1 0.7 pad_maximum_fusion.2.gc_ref
  60.8 2.0 %shard_map.83.own_ref = bf16[3,48,768]{2,1,0:T(8,128)(2,1)} custom-call(bf16[3,16,768]{2,1,0:T(8,128)(2,1)} %pad_maximum_fusion.2.gc_ref, f32[3,48,768]{2,1,0:T(8,128)} %get-tuple-element.8.filt_ref, bf16[48,16]{1,0:T(8,128)(2,1)} %pad.63.proj_t_ref), custom_call_target="tpu_custom_call" | custom-call | tf_op jit(solution)/shard_map/pallas_call | solution.py:239
  62.8 3.4 %collective-permute-start.2 = (bf16[3,48,768]{2,1,0:T(8,128)(2,1)}, bf16[3,48,768]{2,1,0:T(8,128)(2,1)S(1)}, u32[]{:S(2)}, u32[]{:S(2)}) collective-permute-start(bf16[3,48,768]{2,1,0:T(8,128)(2,1)} %shard_map.83.own_ref), channel_id=1, source_target_pairs={{0,1},{1,2},{2,3},{4,5},{5,6},{6,7},{8,9},{9,10},{10,11},{12,13},{... | collective-permute-start | bytes 663560 | tf_op jit(solution)/shard_map/ppermute | solution.py:41
  66.2 1.3 %collective-permute-start.3 = (bf16[3,48,768]{2,1,0:T(8,128)(2,1)}, bf16[3,48,768]{2,1,0:T(8,128)(2,1)S(1)}, u32[]{:S(2)}, u32[]{:S(2)}) collective-permute-start(bf16[3,48,768]{2,1,0:T(8,128)(2,1)} %shard_map.83.own_ref), channel_id=1, source_target_pairs={{1,0},{2,1},{3,2},{5,4},{6,5},{7,6},{9,8},{10,9},{11,10},{13,12},{... | collective-permute-start | bytes 663560 | tf_op jit(solution)/shard_map/ppermute | solution.py:42
  67.5 3.3 %collective-permute-done.2.prev_ref = bf16[3,48,768]{2,1,0:T(8,128)(2,1)S(1)} collective-permute-done((bf16[3,48,768]{2,1,0:T(8,128)(2,1)}, bf16[3,48,768]{2,1,0:T(8,128)(2,1)S(1)}, u32[]{:S(2)}, u32[]{:S(2)}) %collective-permute-start.2) | collective-permute-done | bytes 221216 | tf_op jit(solution)/shard_map/ppermute | solution.py:41
  70.9 5.6 %collective-permute-done.3.next_ref = bf16[3,48,768]{2,1,0:T(8,128)(2,1)S(1)} collective-permute-done((bf16[3,48,768]{2,1,0:T(8,128)(2,1)}, bf16[3,48,768]{2,1,0:T(8,128)(2,1)S(1)}, u32[]{:S(2)}, u32[]{:S(2)}) %collective-permute-start.3) | collective-permute-done | bytes 221216 | tf_op jit(solution)/shard_map/ppermute | solution.py:42
  76.5 0.7 copy-done.4
  77.2 3.8 %shard_map.84 = bf16[3,45,720]{2,1,0:T(8,128)(2,1)} custom-call(s32[588]{0:T(1024)} %reshape.59.basis_ref, s32[12]{0:T(128)} %step_ref.3, f32[12]{0:T(128)} %multiply_cosine_fusion.1.quad_ref, bf16[3,48,768]{2,1,0:T(8,128)(2,1)} %copy-done.3, bf16[3,48,768]{2,1,0:T(8,128)(2,1)} %shard_map.83.own_ref, bf16[3,48,768]{2,1,0:T(8,128)(2,1)} %copy-done.4, ...), custom_call_target="tpu_custom_call" | custom-call | tf_op jit(solution)/shard_map/pallas_call | solution.py:247
  (18 shorter events, 0.1 us)
Async XLA Ops:
  1.9 16.2 %copy-start = (bf16[3,48,768]{2,1,0:T(8,128)(2,1)}, bf16[3,48,768]{2,1,0:T(8,128)(2,1)S(1)}, u32[]{:S(2)}) copy-start(bf16[3,48,768]{2,1,0:T(8,128)(2,1)S(1)} %pad_maximum_fusion.own_ref) | copy-start | bytes 663556
  2.0 12.5 %collective-permute-start = (bf16[3,48,768]{2,1,0:T(8,128)(2,1)S(1)}, bf16[3,48,768]{2,1,0:T(8,128)(2,1)S(1)}, u32[]{:S(2)}, u32[]{:S(2)}) collective-permute-start(bf16[3,48,768]{2,1,0:T(8,128)(2,1)S(1)} %pad_maximum_fusion.own_ref), channel_id=1, source_target_pairs={{0,1},{1,2},{2,3},{4,5},{5,6},{6,7},{8,9},{9,10},{10,11},{12,13},{... | collective-permute-start | bytes 663560 | tf_op jit(solution)/shard_map/ppermute | solution.py:41
  6.8 11.3 %collective-permute-start.1 = (bf16[3,48,768]{2,1,0:T(8,128)(2,1)S(1)}, bf16[3,48,768]{2,1,0:T(8,128)(2,1)S(1)}, u32[]{:S(2)}, u32[]{:S(2)}) collective-permute-start(bf16[3,48,768]{2,1,0:T(8,128)(2,1)S(1)} %pad_maximum_fusion.own_ref), channel_id=1, source_target_pairs={{1,0},{2,1},{3,2},{5,4},{6,5},{7,6},{9,8},{10,9},{11,10},{13,12},{... | collective-permute-start | bytes 663560 | tf_op jit(solution)/shard_map/ppermute | solution.py:42
  14.5 3.7 %copy-start.1 = (bf16[3,48,768]{2,1,0:T(8,128)(2,1)}, bf16[3,48,768]{2,1,0:T(8,128)(2,1)S(1)}, u32[]{:S(2)}) copy-start(bf16[3,48,768]{2,1,0:T(8,128)(2,1)S(1)} %collective-permute-done.prev_ref) | copy-start | bytes 663556
  18.2 0.7 copy-start.2
  24.3 10.7 %copy-start.8 = (f32[4]{0:T(128)S(1)}, f32[4]{0:T(128)}, u32[]{:S(2)}) copy-start(f32[4]{0:T(128)} %constant.34.clone) | copy-start | bytes 52
  30.1 11.1 %all-to-all-start = ((bf16[8,2,2700]{2,1,0:T(2,128)(2,1)}), bf16[8,2,2700]{2,1,0:T(2,128)(2,1)S(1)}, u32[]{:S(2)}, u32[]{:S(2)}) async-start(bf16[8,2,2700]{2,1,0:T(2,128)(2,1)} %reshape.68), calls=%async_computation | async-start | bytes 180224 | tf_op jit(solution)/shard_map/all_to_all | solution.py:220
  35.1 10.5 %copy-start.5 = (f32[4,5,3,90]{3,0,2,1:T(4,128)S(1)}, f32[4,5,3,90]{3,0,2,1:T(4,128)}, u32[]{:S(2)}) copy-start(f32[4,5,3,90]{3,0,2,1:T(4,128)} %param.12) | copy-start | bytes 64804
  43.2 7.0 %copy-start.7 = (bf16[5,45]{1,0:T(8,128)(2,1)S(1)}, bf16[5,45]{1,0:T(8,128)(2,1)}, u32[]{:S(2)}) copy-start(bf16[5,45]{1,0:T(8,128)(2,1)} %param.10) | copy-start | bytes 1354
  45.2 14.5 %copy-start.6 = (bf16[4,5,5]{2,0,1:T(4,128)(2,1)S(1)}, bf16[4,5,5]{2,0,1:T(4,128)(2,1)}, u32[]{:S(2)}) copy-start(bf16[4,5,5]{2,0,1:T(4,128)(2,1)} %param.11) | copy-start | bytes 604
  46.8 12.7 %all-to-all-start.1 = ((f32[4,8,5,3,90]{4,0,3,2,1:T(4,128)}), f32[4,8,5,3,90]{4,0,3,2,1:T(4,128)S(1)}, u32[]{:S(2)}, u32[]{:S(2)}) async-start(f32[4,8,5,3,90]{4,0,3,2,1:T(4,128)} %copy.52), calls=%async_computation.1 | async-start | bytes 491520 | tf_op jit(solution)/shard_map/all_to_all | solution.py:229
  62.8 8.0 %collective-permute-start.2 = (bf16[3,48,768]{2,1,0:T(8,128)(2,1)}, bf16[3,48,768]{2,1,0:T(8,128)(2,1)S(1)}, u32[]{:S(2)}, u32[]{:S(2)}) collective-permute-start(bf16[3,48,768]{2,1,0:T(8,128)(2,1)} %shard_map.83.own_ref), channel_id=1, source_target_pairs={{0,1},{1,2},{2,3},{4,5},{5,6},{6,7},{8,9},{9,10},{10,11},{12,13},{... | collective-permute-start | bytes 663560 | tf_op jit(solution)/shard_map/ppermute | solution.py:41
  66.2 10.2 %collective-permute-start.3 = (bf16[3,48,768]{2,1,0:T(8,128)(2,1)}, bf16[3,48,768]{2,1,0:T(8,128)(2,1)S(1)}, u32[]{:S(2)}, u32[]{:S(2)}) collective-permute-start(bf16[3,48,768]{2,1,0:T(8,128)(2,1)} %shard_map.83.own_ref), channel_id=1, source_target_pairs={{1,0},{2,1},{3,2},{5,4},{6,5},{7,6},{9,8},{10,9},{11,10},{13,12},{... | collective-permute-start | bytes 663560 | tf_op jit(solution)/shard_map/ppermute | solution.py:42
  70.9 5.6 %copy-start.3 = (bf16[3,48,768]{2,1,0:T(8,128)(2,1)}, bf16[3,48,768]{2,1,0:T(8,128)(2,1)S(1)}, u32[]{:S(2)}) copy-start(bf16[3,48,768]{2,1,0:T(8,128)(2,1)S(1)} %collective-permute-done.2.prev_ref) | copy-start | bytes 663556
  76.5 0.7 copy-start.4

commit v2 on v1

--- a/solution.py
+++ b/solution.py
@@ -115,10 +115,38 @@
         ).astype(jnp.bfloat16)
 
 
-def grad_filtered_kernel(gc_ref, filt_ref, proj_t_ref, out_ref):
-    rows = filt_ref.shape[0]
+def score_kernel(sub_ref, weight_ref, fc_ref, truth_ref, filt_ref, proj_t_ref, out_ref):
+    members, rows, cells, width_p = fc_ref.shape
+    variables = sub_ref.shape[0] // cells
+    subcells = cells // variables
+    vp = proj_t_ref.shape[1]
+    total_rows = weight_ref.shape[0] // subcells
+    me = lax.axis_index("member")
+    first = lax.axis_index("lat") * rows
+    cell_sub = lax.broadcasted_iota(jnp.int32, (cells, 1), 0) // variables
     for i in range(rows):
-        grad_act = jnp.dot(proj_t_ref[...], gc_ref[i], preferred_element_type=jnp.float32)
+        g = first + i
+        mine = fc_ref[me, i].astype(jnp.float32)
+        spread = None
+        for n in range(members):
+            term = softened_sign(mine - fc_ref[n, i].astype(jnp.float32))
+            spread = term if spread is None else spread + term
+        scale = jnp.zeros((cells, 1), jnp.float32)
+        for s in range(subcells):
+            scale = jnp.where(cell_sub == s, weight_ref[s * total_rows + g], scale)
+        grad = scale * (softened_sign(mine - truth_ref[i]) - spread / members)
+        coarse = []
+        for u in range(vp):
+            if u >= variables:
+                coarse.append(jnp.zeros((1, width_p), jnp.float32))
+                continue
+            acc = None
+            for r in range(cells):
+                term = sub_ref[r * variables + u] * grad[r : r + 1]
+                acc = term if acc is None else acc + term
+            coarse.append(acc)
+        grad_coarse = jnp.concatenate(coarse, axis=0).astype(jnp.bfloat16)
+        grad_act = jnp.dot(proj_t_ref[...], grad_coarse, preferred_element_type=jnp.float32)
         out_ref[i] = (grad_act * gelu_grad(filt_ref[i])).astype(jnp.bfloat16)
 
 
@@ -186,13 +214,18 @@
     subcells = subcell_maps.shape[0]
     cp = round_up(channels, 16)
     vp = round_up(variables, 16)
-    svp = round_up(subcells * variables, 16)
+    svp = subcells * variables
     width_p = ring_width(width)
     total_rows = rows * lax.axis_size("lat")
     first = lax.axis_index("lat") * rows
 
     quad_all = latitude_rows(total_rows, total_rows)
-    couple_factor = subcell_weight(first, rows, total_rows)
+    weight_all = subcell_weight(0, total_rows, total_rows).reshape(-1)
+    sub_flat = subcell_maps.astype(jnp.float32).reshape(-1)
+    truth_all = lax.all_gather(verifying_truth, "member", axis=3, tiled=True)
+    truth_ring = to_ring(
+        truth_all.reshape(subcells * variables, rows, width).transpose(1, 0, 2), width_p
+    )
 
     table = jnp.concatenate([filters, jnp.zeros((1,) + filters.shape[1:], filters.dtype)], 0)
     table = pad_axis(pad_axis(table, 1, cp), 2, cp)
@@ -215,33 +248,14 @@
         out_specs=(vmem(), vmem()),
     )(basis_flat, step_rows, quad_all, low, own, high, tables, proj_p, sub_p)
 
-    forecast = fc[:, : subcells * variables, :width].reshape(rows, subcells, variables, width)
-    fine_local = forecast.transpose(1, 2, 0, 3)[:, None]
-    fine_owned = lax.all_to_all(fine_local, "member", split_axis=4, concat_axis=1, tiled=True)
-
-    samples = fine_owned.astype(jnp.float32)
-    members = samples.shape[1]
-    truth_term = softened_sign(samples - verifying_truth[:, None])
-    couple = softened_sign(samples - samples[:, 0:1])
-    for n in range(1, members):
-        couple = couple + softened_sign(samples - samples[:, n : n + 1])
-    grad_owned = couple_factor[:, None, None, :, None] * (truth_term - couple / members)
-    grad_fine = lax.all_to_all(grad_owned, "member", split_axis=1, concat_axis=4, tiled=True)
-    grad_coarse = jnp.einsum(
-        "svu,smvhw->muhw",
-        subcell_maps.astype(jnp.float32),
-        grad_fine,
-        precision=lax.Precision.HIGHEST,
-    )[0].astype(jnp.bfloat16)
-
-    gc = to_ring(pad_axis(grad_coarse.transpose(1, 0, 2), 1, vp), width_p)
+    gathered = lax.all_gather(fc, "member", axis=0, tiled=False)
     proj_t = pad_axis(pad_axis(project.T, 0, cp), 1, vp)
     grad_filtered = pl.pallas_call(
-        grad_filtered_kernel,
+        score_kernel,
         out_shape=jax.ShapeDtypeStruct((rows, cp, width_p), jnp.bfloat16),
-        in_specs=[vmem()] * 3,
+        in_specs=[smem(), smem()] + [vmem()] * 4,
         out_specs=vmem(),
-    )(gc, filtered, proj_t)
+    )(sub_flat, weight_all, gathered, truth_ring, filtered, proj_t)
 
     g_low, g_high = halo(grad_filtered, "lat", HALF)
     result = pl.pallas_call(

time: 81.7 us -> 117 us (1.43)
  blocking collectives: 0 us -> 59.4 us
  waiting for transfers between devices: 27.3 us -> 11.7 us
  starting transfers between devices: 19.1 us -> 11.4 us
  local copies, waits for them, and re-layouts: 21.1 us -> 18.3 us
  Pallas kernels: 10.4 us -> 12.7 us
    all_gather x0 -> x2, blocking collectives: none -> 59.4 us  [the longest x1 41.7 us: on_device(): truth_all = lax.all_gather(verifying_truth, 'member', axis=3, tiled=True)]
    all_to_all x2 -> x0, waiting for transfers between devices: 14.7 us -> none  [the longest x1 8.57 us: on_device(): lax.all_to_all(grad_owned, 'member', split_axis=1, concat_axis=4, tiled=T...]
    all_to_all x2 -> x0, starting transfers between devices: 8.28 us -> none  [the longest x1 4.88 us: on_device(): lax.all_to_all(fine_local, 'member', split_axis=4, concat_axis=1, tiled=T...]
    all_gather x0 -> x1, local copies, waits for them, and re-layouts: none -> 4.8 us  [on_device(): truth_all = lax.all_gather(verifying_truth, 'member', axis=3, tiled=True)]
    broadcast_in_dim x1 -> x0, local copies, waits for them, and re-layouts: 2.79 us -> none  [on_device(): fine_local = forecast.transpose(1, 2, 0, 3)[:, None]]
    unnamed x22 -> x15, local copies, waits for them, and re-layouts: 7.51 us -> 4.88 us
    pallas_call x1, Pallas kernels: 2.03 us -> 4.42 us  [on_device(): pl.pallas_call(score_kernel, out_shape=jax.ShapeDtypeStruct((rows, cp, wi...]
    all_to_all x2 -> x0, local copies, waits for them, and re-layouts: 1.97 us -> none  [the longest x1 1.95 us: on_device(): lax.all_to_all(fine_local, 'member', split_axis=4, concat_axis=1, tiled=T...]
  transfers between devices with their start and end apart: 6 -> 4, of which waited for: 5 -> 2; matrix products, arithmetic and copies ran while one was open for 9% -> 14% of each run, Pallas kernels for 0% -> 0%
where the time goes in v2:
time: 117 us; the launch traced here: 116 us
  blocking collectives  59.4 us (51%)
  local copies, waits for them, and re-layouts  18.3 us (16%)
  Pallas kernels  12.7 us (11%)
  waiting for transfers between devices  11.7 us (10%)
  starting transfers between devices  11.4 us (10%)
  other arithmetic  2.25 us (2%)
    all_gather x1, blocking collectives, on_device(): truth_all = lax.all_gather(verifying_truth, 'member', axis=3, tiled=True)  41.7 us
    all_gather x1, blocking collectives, on_device(): gathered = lax.all_gather(fc, 'member', axis=0, tiled=False)  17.7 us
    ppermute x2, starting transfers between devices, halo(): low = lax.ppermute(block[block.shape[0] - width:], axis_name, forward)  8.84 us
    ppermute x2, waiting for transfers between devices, halo(): high = lax.ppermute(block[:width], axis_name, backward)  7.46 us
    unnamed x15, local copies, waits for them, and re-layouts  4.88 us
    all_gather x1, local copies, waits for them, and re-layouts, on_device(): truth_all = lax.all_gather(verifying_truth, 'member', axis=3, tiled=True)  4.8 us
    pallas_call x1, Pallas kernels, on_device(): pl.pallas_call(forward_kernel, out_shape=(jax.ShapeDtypeStruct((rows, cp,...  4.48 us
    pallas_call x1, Pallas kernels, on_device(): pl.pallas_call(score_kernel, out_shape=jax.ShapeDtypeStruct((rows, cp, wi...  4.42 us
  transfers between devices with their start and end apart: 4, of which 2 were waited for; matrix products, arithmetic and copies ran while one was open for 14% of the time, Pallas kernels for 0%

profile of v2, /device:TPU:0, one launch (start us, length us, event | category | flops | bytes accessed | tf_op | source)
XLA Modules:
  0.0 115.8 jit_solution(3663406939210544346)
XLA Ops:
  0.0 0.9 pad_slice_fusion.1
  0.9 1.0 pad.33
  1.8 0.1 pad_maximum_fusion.own_ref
  1.9 0.0 copy-start
  2.0 4.9 %collective-permute-start = (bf16[3,48,768]{2,1,0:T(8,128)(2,1)S(1)}, bf16[3,48,768]{2,1,0:T(8,128)(2,1)S(1)}, u32[]{:S(2)}, u32[]{:S(2)}) collective-permute-start(bf16[3,48,768]{2,1,0:T(8,128)(2,1)S(1)} %pad_maximum_fusion.own_ref), channel_id=1, source_target_pairs={{0,1},{1,2},{2,3},{4,5},{5,6},{6,7},{8,9},{9,10},{10,11},{12,13},{... | collective-permute-start | bytes 663560 | tf_op jit(solution)/shard_map/ppermute | solution.py:41
  6.8 1.3 %collective-permute-start.1 = (bf16[3,48,768]{2,1,0:T(8,128)(2,1)S(1)}, bf16[3,48,768]{2,1,0:T(8,128)(2,1)S(1)}, u32[]{:S(2)}, u32[]{:S(2)}) collective-permute-start(bf16[3,48,768]{2,1,0:T(8,128)(2,1)S(1)} %pad_maximum_fusion.own_ref), channel_id=1, source_target_pairs={{1,0},{2,1},{3,2},{5,4},{6,5},{7,6},{9,8},{10,9},{11,10},{13,12},{... | collective-permute-start | bytes 663560 | tf_op jit(solution)/shard_map/ppermute | solution.py:42
  8.1 1.3 %pad.51.proj_ref = bf16[16,48]{1,0:T(8,128)(2,1)} pad(bf16[5,45]{1,0:T(8,128)(2,1)} %param.10, bf16[]{:T(256)} %constant.22.clone.1), padding=0_11x0_3 | pad | bytes 1988 | tf_op jit(solution)/shard_map/jit(_pad)/pad | solution.py:34
  9.4 0.8 copy.32
  10.2 0.7 copy.33
  10.9 0.7 copy.24
  11.6 1.0 copy.25
  12.6 0.1 copy.26
  12.7 1.4 %reshape.31.basis_ref = s32[588]{0:T(1024)} reshape(s32[12,49]{1,0:T(8,128)} %param.13) | data formatting | bytes 4704 | tf_op jit(solution)/shard_map/reshape | solution.py:233
  14.1 0.6 pad.38.sub_ref
  14.7 1.0 copy.29
  15.7 0.0 copy-start.5
  15.7 41.7 %all_gather.11 = f32[4,5,3,720]{1,0,2,3:T(4,128)} all-gather(f32[4,5,3,90]{1,0,2,3:T(4,128)S(1)} %copy.29), channel_id=1, replica_groups=mesh['member'=8,'lat'=4] {'member'}, dimensions={3}, use_global_device_ids=true | all-gather | bytes 194400 | tf_op jit(solution)/shard_map/all_gather | solution.py:225
  57.4 4.8 %copy.30 = f32[4,5,3,720]{3,2,1,0:T(4,128)S(1)} copy(f32[4,5,3,720]{1,0,2,3:T(4,128)} %all_gather.11) | data formatting | bytes 345600 | tf_op jit(solution)/shard_map/all_gather | solution.py:225
  62.2 0.0 copy-done
  62.3 0.1 fusion
  62.4 0.6 pad.52.proj_t_ref
  63.0 0.6 reshape.37.sub_ref
  63.6 0.0 copy-done.5
  63.6 0.1 multiply_cosine_fusion
  63.7 0.7 reshape.40.weight_ref
  64.3 0.7 pad_maximum_fusion.2.table_ref
  65.0 0.6 multiply_cosine_fusion.1.quad_ref
  65.6 0.8 pad_maximum_fusion.1.truth_ref
  66.4 0.0 collective-permute-done.prev_ref
  66.4 0.0 copy-start.1
  66.4 0.0 collective-permute-done.1.next_ref
  66.4 0.7 copy-done.1
  67.1 0.0 copy-start.2
  67.1 0.7 copy-done.2
  67.8 4.5 %shard_map.82 = (f32[3,48,768]{2,1,0:T(8,128)}, bf16[3,20,768]{2,1,0:T(8,128)(2,1)}) custom-call(s32[588]{0:T(1024)} %reshape.31.basis_ref, s32[12]{0:T(128)} %step_ref.3, f32[12]{0:T(128)} %multiply_cosine_fusion.1.quad_ref, bf16[3,48,768]{2,1,0:T(8,128)(2,1)} %copy-done.1, bf16[3,48,768]{2,1,0:T(8,128)(2,1)} %copy-done, bf16[3,48,768]{2,1,0:T(8,128)(2,1)} %copy-done.2, ...), custom_call_target="tpu_custom_call" | custom-call | tf_op jit(solution)/shard_map/pallas_call | solution.py:241
  72.2 17.7 %all-gather = bf16[24,20,768]{2,1,0:T(8,128)(2,1)} all-gather(bf16[3,20,768]{2,1,0:T(8,128)(2,1)} %get-tuple-element.7), channel_id=2, replica_groups=mesh['member'=8,'lat'=4] {'member'}, dimensions={0}, use_global_device_ids=true | all-gather | bytes 829440 | tf_op jit(solution)/shard_map/all_gather | solution.py:251
  89.9 4.4 %shard_map.83.own_ref = bf16[3,48,768]{2,1,0:T(8,128)(2,1)} custom-call(f32[100]{0:T(128)} %reshape.37.sub_ref, f32[48]{0:T(128)} %reshape.40.weight_ref, bf16[8,3,20,768]{3,2,1,0:T(8,128)(2,1)} %bitcast.14, f32[3,20,768]{2,1,0:T(8,128)} %pad_maximum_fusion.1.truth_ref, f32[3,48,768]{2,1,0:T(8,128)} %get-tuple-element.8.filt_ref, bf16[48,16]{1,0:T(8,128)(2,1)} %pad.52.proj_t_ref), custom_call_target="tpu_custom_call" | custom-call | tf_op jit(solution)/shard_map/pallas_call | solution.py:253
  94.4 4.0 %collective-permute-start.2 = (bf16[3,48,768]{2,1,0:T(8,128)(2,1)}, bf16[3,48,768]{2,1,0:T(8,128)(2,1)S(1)}, u32[]{:S(2)}, u32[]{:S(2)}) collective-permute-start(bf16[3,48,768]{2,1,0:T(8,128)(2,1)} %shard_map.83.own_ref), channel_id=1, source_target_pairs={{0,1},{1,2},{2,3},{4,5},{5,6},{6,7},{8,9},{9,10},{10,11},{12,13},{... | collective-permute-start | bytes 663560 | tf_op jit(solution)/shard_map/ppermute | solution.py:41
  98.4 1.3 %collective-permute-start.3 = (bf16[3,48,768]{2,1,0:T(8,128)(2,1)}, bf16[3,48,768]{2,1,0:T(8,128)(2,1)S(1)}, u32[]{:S(2)}, u32[]{:S(2)}) collective-permute-start(bf16[3,48,768]{2,1,0:T(8,128)(2,1)} %shard_map.83.own_ref), channel_id=1, source_target_pairs={{1,0},{2,1},{3,2},{5,4},{6,5},{7,6},{9,8},{10,9},{11,10},{13,12},{... | collective-permute-start | bytes 663560 | tf_op jit(solution)/shard_map/ppermute | solution.py:42
  99.7 4.2 %collective-permute-done.2.prev_ref = bf16[3,48,768]{2,1,0:T(8,128)(2,1)S(1)} collective-permute-done((bf16[3,48,768]{2,1,0:T(8,128)(2,1)}, bf16[3,48,768]{2,1,0:T(8,128)(2,1)S(1)}, u32[]{:S(2)}, u32[]{:S(2)}) %collective-permute-start.2) | collective-permute-done | bytes 221216 | tf_op jit(solution)/shard_map/ppermute | solution.py:41
  103.8 0.0 copy-start.3
  103.8 7.5 %collective-permute-done.3.next_ref = bf16[3,48,768]{2,1,0:T(8,128)(2,1)S(1)} collective-permute-done((bf16[3,48,768]{2,1,0:T(8,128)(2,1)}, bf16[3,48,768]{2,1,0:T(8,128)(2,1)S(1)}, u32[]{:S(2)}, u32[]{:S(2)}) %collective-permute-start.3) | collective-permute-done | bytes 221216 | tf_op jit(solution)/shard_map/ppermute | solution.py:42
  111.3 0.0 copy-done.3
  111.3 0.0 copy-start.4
  111.3 0.7 copy-done.4
  112.0 3.8 %shard_map.84 = bf16[3,45,720]{2,1,0:T(8,128)(2,1)} custom-call(s32[588]{0:T(1024)} %reshape.31.basis_ref, s32[12]{0:T(128)} %step_ref.3, f32[12]{0:T(128)} %multiply_cosine_fusion.1.quad_ref, bf16[3,48,768]{2,1,0:T(8,128)(2,1)} %copy-done.3, bf16[3,48,768]{2,1,0:T(8,128)(2,1)} %shard_map.83.own_ref, bf16[3,48,768]{2,1,0:T(8,128)(2,1)} %copy-done.4, ...), custom_call_target="tpu_custom_call" | custom-call | tf_op jit(solution)/shard_map/pallas_call | solution.py:261
  (4 shorter events, 0.1 us)
Async XLA Ops:
  1.9 60.3 %copy-start = (bf16[3,48,768]{2,1,0:T(8,128)(2,1)}, bf16[3,48,768]{2,1,0:T(8,128)(2,1)S(1)}, u32[]{:S(2)}) copy-start(bf16[3,48,768]{2,1,0:T(8,128)(2,1)S(1)} %pad_maximum_fusion.own_ref) | copy-start | bytes 663556
  2.0 64.4 %collective-permute-start = (bf16[3,48,768]{2,1,0:T(8,128)(2,1)S(1)}, bf16[3,48,768]{2,1,0:T(8,128)(2,1)S(1)}, u32[]{:S(2)}, u32[]{:S(2)}) collective-permute-start(bf16[3,48,768]{2,1,0:T(8,128)(2,1)S(1)} %pad_maximum_fusion.own_ref), channel_id=1, source_target_pairs={{0,1},{1,2},{2,3},{4,5},{5,6},{6,7},{8,9},{9,10},{10,11},{12,13},{... | collective-permute-start | bytes 663560 | tf_op jit(solution)/shard_map/ppermute | solution.py:41
  6.8 59.6 %collective-permute-start.1 = (bf16[3,48,768]{2,1,0:T(8,128)(2,1)S(1)}, bf16[3,48,768]{2,1,0:T(8,128)(2,1)S(1)}, u32[]{:S(2)}, u32[]{:S(2)}) collective-permute-start(bf16[3,48,768]{2,1,0:T(8,128)(2,1)S(1)} %pad_maximum_fusion.own_ref), channel_id=1, source_target_pairs={{1,0},{2,1},{3,2},{5,4},{6,5},{7,6},{9,8},{10,9},{11,10},{13,12},{... | collective-permute-start | bytes 663560 | tf_op jit(solution)/shard_map/ppermute | solution.py:42
  15.7 47.8 %copy-start.5 = (f32[4]{0:T(128)S(1)}, f32[4]{0:T(128)}, u32[]{:S(2)}) copy-start(f32[4]{0:T(128)} %constant.23.clone) | copy-start | bytes 52
  66.4 0.7 copy-start.1
  67.1 0.7 copy-start.2
  94.4 9.5 %collective-permute-start.2 = (bf16[3,48,768]{2,1,0:T(8,128)(2,1)}, bf16[3,48,768]{2,1,0:T(8,128)(2,1)S(1)}, u32[]{:S(2)}, u32[]{:S(2)}) collective-permute-start(bf16[3,48,768]{2,1,0:T(8,128)(2,1)} %shard_map.83.own_ref), channel_id=1, source_target_pairs={{0,1},{1,2},{2,3},{4,5},{5,6},{6,7},{8,9},{9,10},{10,11},{12,13},{... | collective-permute-start | bytes 663560 | tf_op jit(solution)/shard_map/ppermute | solution.py:41
  98.4 13.0 %collective-permute-start.3 = (bf16[3,48,768]{2,1,0:T(8,128)(2,1)}, bf16[3,48,768]{2,1,0:T(8,128)(2,1)S(1)}, u32[]{:S(2)}, u32[]{:S(2)}) collective-permute-start(bf16[3,48,768]{2,1,0:T(8,128)(2,1)} %shard_map.83.own_ref), channel_id=1, source_target_pairs={{1,0},{2,1},{3,2},{5,4},{6,5},{7,6},{9,8},{10,9},{11,10},{13,12},{... | collective-permute-start | bytes 663560 | tf_op jit(solution)/shard_map/ppermute | solution.py:42
  103.8 7.5 %copy-start.3 = (bf16[3,48,768]{2,1,0:T(8,128)(2,1)}, bf16[3,48,768]{2,1,0:T(8,128)(2,1)S(1)}, u32[]{:S(2)}) copy-start(bf16[3,48,768]{2,1,0:T(8,128)(2,1)S(1)} %collective-permute-done.2.prev_ref) | copy-start | bytes 663556
  111.3 0.7 copy-start.4

commit v3 on v2

--- a/solution.py
+++ b/solution.py
@@ -110,43 +110,61 @@
         coarse = jnp.dot(
             proj_ref[...], activated, preferred_element_type=jnp.float32
         ).astype(jnp.bfloat16)
-        fc_ref[i] = jnp.dot(
+        forecast = jnp.dot(
             sub_ref[...], coarse, preferred_element_type=jnp.float32
         ).astype(jnp.bfloat16)
-
-
-def score_kernel(sub_ref, weight_ref, fc_ref, truth_ref, filt_ref, proj_t_ref, out_ref):
-    members, rows, cells, width_p = fc_ref.shape
+        blocks, block = fc_ref.shape[0], fc_ref.shape[3]
+        for q in range(blocks):
+            fc_ref[q, i] = forecast[:, q * block : (q + 1) * block]
+
+
+def score_kernel(sub_ref, weight_ref, fc_ref, truth_ref, out_ref):
+    members, rows, cells, block = fc_ref.shape
+    vp = out_ref.shape[2]
     variables = sub_ref.shape[0] // cells
     subcells = cells // variables
-    vp = proj_t_ref.shape[1]
     total_rows = weight_ref.shape[0] // subcells
-    me = lax.axis_index("member")
     first = lax.axis_index("lat") * rows
     cell_sub = lax.broadcasted_iota(jnp.int32, (cells, 1), 0) // variables
     for i in range(rows):
         g = first + i
-        mine = fc_ref[me, i].astype(jnp.float32)
-        spread = None
-        for n in range(members):
-            term = softened_sign(mine - fc_ref[n, i].astype(jnp.float32))
-            spread = term if spread is None else spread + term
         scale = jnp.zeros((cells, 1), jnp.float32)
         for s in range(subcells):
             scale = jnp.where(cell_sub == s, weight_ref[s * total_rows + g], scale)
-        grad = scale * (softened_sign(mine - truth_ref[i]) - spread / members)
-        coarse = []
-        for u in range(vp):
-            if u >= variables:
-                coarse.append(jnp.zeros((1, width_p), jnp.float32))
-                continue
-            acc = None
-            for r in range(cells):
-                term = sub_ref[r * variables + u] * grad[r : r + 1]
-                acc = term if acc is None else acc + term
-            coarse.append(acc)
-        grad_coarse = jnp.concatenate(coarse, axis=0).astype(jnp.bfloat16)
-        grad_act = jnp.dot(proj_t_ref[...], grad_coarse, preferred_element_type=jnp.float32)
+        truth = truth_ref[i]
+        values = [fc_ref[n, i].astype(jnp.float32) for n in range(members)]
+        spread = [jnp.zeros((cells, block), jnp.float32) for _ in range(members)]
+        for m in range(members):
+            for n in range(m + 1, members):
+                term = softened_sign(values[m] - values[n])
+                spread[m] = spread[m] + term
+                spread[n] = spread[n] - term
+        for m in range(members):
+            grad = scale * (softened_sign(values[m] - truth) - spread[m] / members)
+            coarse = []
+            for u in range(vp):
+                if u >= variables:
+                    coarse.append(jnp.zeros((1, block), jnp.float32))
+                    continue
+                acc = None
+                for r in range(cells):
+                    term = sub_ref[r * variables + u] * grad[r : r + 1]
+                    acc = term if acc is None else acc + term
+                coarse.append(acc)
+            out_ref[m, i] = jnp.concatenate(coarse, axis=0).astype(out_ref.dtype)
+
+
+def grad_filtered_kernel(gc_ref, filt_ref, proj_t_ref, out_ref):
+    blocks, rows = gc_ref.shape[0], gc_ref.shape[1]
+    width_p = filt_ref.shape[2]
+    for i in range(rows):
+        row = jnp.concatenate([gc_ref[q, i] for q in range(blocks)], axis=1)
+        width = row.shape[1]
+        extra = width_p - width
+        lo = extra // 2
+        hi = extra - lo
+        ring = jnp.concatenate([row, row[:, :lo], row[:, width - hi :]], axis=1)
+        grad_act = jnp.dot(proj_t_ref[...], ring, preferred_element_type=jnp.float32)
         out_ref[i] = (grad_act * gelu_grad(filt_ref[i])).astype(jnp.bfloat16)
 
 
@@ -222,10 +240,9 @@
     quad_all = latitude_rows(total_rows, total_rows)
     weight_all = subcell_weight(0, total_rows, total_rows).reshape(-1)
     sub_flat = subcell_maps.astype(jnp.float32).reshape(-1)
-    truth_all = lax.all_gather(verifying_truth, "member", axis=3, tiled=True)
-    truth_ring = to_ring(
-        truth_all.reshape(subcells * variables, rows, width).transpose(1, 0, 2), width_p
-    )
+    blocks = lax.axis_size("member")
+    block = width // blocks
+    truth = verifying_truth.reshape(subcells * variables, rows, block).transpose(1, 0, 2)
 
     table = jnp.concatenate([filters, jnp.zeros((1,) + filters.shape[1:], filters.dtype)], 0)
     table = pad_axis(pad_axis(table, 1, cp), 2, cp)
@@ -242,20 +259,27 @@
         forward_kernel,
         out_shape=(
             jax.ShapeDtypeStruct((rows, cp, width_p), jnp.float32),
-            jax.ShapeDtypeStruct((rows, svp, width_p), jnp.bfloat16),
+            jax.ShapeDtypeStruct((blocks, rows, svp, block), jnp.bfloat16),
         ),
         in_specs=[smem(), smem(), smem()] + [vmem()] * 6,
         out_specs=(vmem(), vmem()),
     )(basis_flat, step_rows, quad_all, low, own, high, tables, proj_p, sub_p)
 
-    gathered = lax.all_gather(fc, "member", axis=0, tiled=False)
+    fc_owned = lax.all_to_all(fc, "member", split_axis=0, concat_axis=0, tiled=True)
+    gc_owned = pl.pallas_call(
+        score_kernel,
+        out_shape=jax.ShapeDtypeStruct((blocks, rows, vp, block), jnp.bfloat16),
+        in_specs=[smem(), smem()] + [vmem()] * 2,
+        out_specs=vmem(),
+    )(sub_flat, weight_all, fc_owned, truth)
+    gc_home = lax.all_to_all(gc_owned, "member", split_axis=0, concat_axis=0, tiled=True)
     proj_t = pad_axis(pad_axis(project.T, 0, cp), 1, vp)
     grad_filtered = pl.pallas_call(
-        score_kernel,
+        grad_filtered_kernel,
         out_shape=jax.ShapeDtypeStruct((rows, cp, width_p), jnp.bfloat16),
-        in_specs=[smem(), smem()] + [vmem()] * 4,
+        in_specs=[vmem()] * 3,
         out_specs=vmem(),
-    )(sub_flat, weight_all, gathered, truth_ring, filtered, proj_t)
+    )(gc_home, filtered, proj_t)
 
     g_low, g_high = halo(grad_filtered, "lat", HALF)
     result = pl.pallas_call(

time: 117 us -> 70 us (0.60)
  blocking collectives: 59.4 us -> 0 us
  waiting for transfers between devices: 11.7 us -> 25.2 us
  local copies, waits for them, and re-layouts: 18.3 us -> 9.26 us
  starting transfers between devices: 11.4 us -> 19.2 us
  Pallas kernels: 12.7 us -> 14.2 us
    all_gather x2 -> x0, blocking collectives: 59.4 us -> none  [the longest x1 41.7 us: on_device(): truth_all = lax.all_gather(verifying_truth, 'member', axis=3, tiled=True)]
    all_to_all x0 -> x2, waiting for transfers between devices: none -> 11.7 us  [the longest x1 6.2 us: on_device(): lax.all_to_all(fc, 'member', split_axis=0, concat_axis=0, tiled=True)]
    all_to_all x0 -> x2, starting transfers between devices: none -> 8.37 us  [the longest x1 5.01 us: on_device(): lax.all_to_all(fc, 'member', split_axis=0, concat_axis=0, tiled=True)]
    all_gather x1 -> x0, local copies, waits for them, and re-layouts: 4.8 us -> none  [on_device(): truth_all = lax.all_gather(verifying_truth, 'member', axis=3, tiled=True)]
    ppermute x2, waiting for transfers between devices: 7.46 us -> 9.96 us  [halo(): high = lax.ppermute(block[:width], axis_name, backward)]
    pad x4, local copies, waits for them, and re-layouts: 3.45 us -> 1.83 us  [pad_axis(): return jnp.pad(block, pads)]
    pallas_call x1 -> x2, Pallas kernels: 4.42 us -> 5.72 us  [the longest x1 3.56 us: on_device(): pl.pallas_call(score_kernel, out_shape=jax.ShapeDtypeStruct((blocks, rows...]
    unnamed x15 -> x31, local copies, waits for them, and re-layouts: 4.88 us -> 3.7 us
  transfers between devices with their start and end apart: 4 -> 6, of which waited for: 2 -> 5; matrix products, arithmetic and copies ran while one was open for 14% -> 9% of each run, Pallas kernels for 0% -> 0%
where the time goes in v3:
time: 70 us; the launch traced here: 69.4 us
  waiting for transfers between devices  25.2 us (36%)
  starting transfers between devices  19.2 us (27%)
  Pallas kernels  14.2 us (20%)
  local copies, waits for them, and re-layouts  9.26 us (13%)
  other arithmetic  1.49 us (2%)
    ppermute x2, waiting for transfers between devices, halo(): high = lax.ppermute(block[:width], axis_name, backward)  9.96 us
    ppermute x2, starting transfers between devices, halo(): low = lax.ppermute(block[block.shape[0] - width:], axis_name, forward)  8.25 us
    all_to_all x1, waiting for transfers between devices, on_device(): lax.all_to_all(fc, 'member', split_axis=0, concat_axis=0, tiled=True)  6.2 us
    all_to_all x1, waiting for transfers between devices, on_device(): lax.all_to_all(gc_owned, 'member', split_axis=0, concat_axis=0, tiled=True)  5.54 us
    all_to_all x1, starting transfers between devices, on_device(): lax.all_to_all(fc, 'member', split_axis=0, concat_axis=0, tiled=True)  5.01 us
    pallas_call x1, Pallas kernels, on_device(): pl.pallas_call(forward_kernel, out_shape=(jax.ShapeDtypeStruct((rows, cp,...  4.59 us
    pallas_call x1, Pallas kernels, on_device(): pl.pallas_call(backward_kernel, out_shape=jax.ShapeDtypeStruct((rows, cha...  3.84 us
    unnamed x31, local copies, waits for them, and re-layouts  3.7 us
  transfers between devices with their start and end apart: 6, of which 5 were waited for; matrix products, arithmetic and copies ran while one was open for 9% of the time, Pallas kernels for 0%

profile of v3, /device:TPU:0, one launch (start us, length us, event | category | flops | bytes accessed | tf_op | source)
XLA Modules:
  0.0 69.4 jit_solution(5299806500597577536)
XLA Ops:
  0.0 0.9 %pad_slice_fusion.1 = (bf16[3,48,24]{2,1,0:T(8,128)(2,1)S(1)}, bf16[3,48,24]{2,1,0:T(8,128)(2,1)S(1)}) fusion(bf16[3,45,720]{2,1,0:T(8,128)(2,1)} %bitcast.13), kind=kLoop, calls=%fused_computation.9 | loop fusion | bytes 208224 | tf_op jit(solution)/shard_map/slice | solution.py:27
  0.9 0.0 copy-done.1
  1.0 0.0 copy-start.10
  1.0 0.0 copy-start.8
  1.0 0.1 pad_maximum_fusion.own_ref
  1.1 0.0 copy-start
  1.1 4.9 %collective-permute-start = (bf16[3,48,768]{2,1,0:T(8,128)(2,1)S(1)}, bf16[3,48,768]{2,1,0:T(8,128)(2,1)S(1)}, u32[]{:S(2)}, u32[]{:S(2)}) collective-permute-start(bf16[3,48,768]{2,1,0:T(8,128)(2,1)S(1)} %pad_maximum_fusion.own_ref), channel_id=1, source_target_pairs={{0,1},{1,2},{2,3},{4,5},{5,6},{6,7},{8,9},{9,10},{10,11},{12,13},{... | collective-permute-start | bytes 663560 | tf_op jit(solution)/shard_map/ppermute | solution.py:41
  6.0 1.3 %collective-permute-start.1 = (bf16[3,48,768]{2,1,0:T(8,128)(2,1)S(1)}, bf16[3,48,768]{2,1,0:T(8,128)(2,1)S(1)}, u32[]{:S(2)}, u32[]{:S(2)}) collective-permute-start(bf16[3,48,768]{2,1,0:T(8,128)(2,1)S(1)} %pad_maximum_fusion.own_ref), channel_id=1, source_target_pairs={{1,0},{2,1},{3,2},{5,4},{6,5},{7,6},{9,8},{10,9},{11,10},{13,12},{... | collective-permute-start | bytes 663560 | tf_op jit(solution)/shard_map/ppermute | solution.py:42
  7.3 0.6 multiply_cosine_fusion.1.quad_ref
  7.9 0.0 copy-done.10
  7.9 0.0 copy-done.8
  7.9 0.1 copy.17
  8.1 0.0 copy-start.12
  8.1 0.1 copy.18
  8.2 0.0 copy-done
  8.2 0.6 copy-done.12
  8.8 0.7 reshape.31.basis_ref
  9.5 0.6 pad.38.sub_ref
  10.1 0.1 copy-done.11
  10.2 0.6 pad.48.proj_ref
  10.8 0.0 copy-done.9
  10.8 0.6 copy.27
  11.4 0.7 reshape.37.sub_ref
  12.1 0.7 pad_maximum_fusion.1.table_ref
  12.8 0.0 collective-permute-done.prev_ref
  12.8 4.6 %collective-permute-done.1.next_ref = bf16[3,48,768]{2,1,0:T(8,128)(2,1)S(1)} collective-permute-done((bf16[3,48,768]{2,1,0:T(8,128)(2,1)S(1)}, bf16[3,48,768]{2,1,0:T(8,128)(2,1)S(1)}, u32[]{:S(2)}, u32[]{:S(2)}) %collective-permute-start.1) | collective-permute-done | bytes 221216 | tf_op jit(solution)/shard_map/ppermute | solution.py:42
  17.3 0.0 copy-done.4
  17.3 0.7 %copy-done.5 = bf16[3,48,768]{2,1,0:T(8,128)(2,1)} copy-done((bf16[3,48,768]{2,1,0:T(8,128)(2,1)}, bf16[3,48,768]{2,1,0:T(8,128)(2,1)S(1)}, u32[]{:S(2)}) %copy-start.5) | copy-done | bytes 221208
  18.0 4.6 %shard_map.82 = (f32[3,48,768]{2,1,0:T(8,128)}, bf16[8,3,20,90]{3,2,1,0:T(8,128)(2,1)}) custom-call(s32[588]{0:T(1024)} %reshape.31.basis_ref, s32[12]{0:T(128)} %step_ref.3, f32[12]{0:T(128)} %multiply_cosine_fusion.1.quad_ref, bf16[3,48,768]{2,1,0:T(8,128)(2,1)} %copy-done.4, bf16[3,48,768]{2,1,0:T(8,128)(2,1)} %copy-done, bf16[3,48,768]{2,1,0:T(8,128)(2,1)} %copy-done.5, ...), custom_call_target="tpu_custom_call" | custom-call | tf_op jit(solution)/shard_map/pallas_call | solution.py:258
  22.6 5.0 %all-to-all-start = ((bf16[8,3,20,90]{3,2,1,0:T(8,128)(2,1)}), bf16[8,3,20,90]{3,2,1,0:T(8,128)(2,1)S(1)}, u32[]{:S(2)}, u32[]{:S(2)}) async-start(bf16[8,3,20,90]{3,2,1,0:T(8,128)(2,1)} %get-tuple-element.7), calls=%async_computation | async-start | bytes 294912 | tf_op jit(solution)/shard_map/all_to_all | solution.py:268
  27.7 0.1 multiply_cosine_fusion
  27.8 0.7 reshape.40.weight_ref
  28.4 6.2 %all-to-all-done.fc_ref = bf16[8,3,20,90]{3,2,1,0:T(8,128)(2,1)S(1)} async-done(((bf16[8,3,20,90]{3,2,1,0:T(8,128)(2,1)}), bf16[8,3,20,90]{3,2,1,0:T(8,128)(2,1)S(1)}, u32[]{:S(2)}, u32[]{:S(2)}) %all-to-all-start) | async-done | bytes 86432 | tf_op jit(solution)/shard_map/all_to_all | solution.py:268
  34.7 0.7 copy-done.2
  35.3 3.6 %shard_map.83 = bf16[8,3,16,90]{3,2,1,0:T(8,128)(2,1)} custom-call(f32[100]{0:T(128)} %reshape.37.sub_ref, f32[48]{0:T(128)} %reshape.40.weight_ref, bf16[8,3,20,90]{3,2,1,0:T(8,128)(2,1)} %copy-done.2, f32[3,20,90]{2,1,0:T(8,128)} %bitcast.16), custom_call_target="tpu_custom_call" | custom-call | tf_op jit(solution)/shard_map/pallas_call | solution.py:269
  38.9 3.4 %all-to-all-start.1 = ((bf16[8,3,16,90]{3,2,1,0:T(8,128)(2,1)}), bf16[8,3,16,90]{3,2,1,0:T(8,128)(2,1)S(1)}, u32[]{:S(2)}, u32[]{:S(2)}) async-start(bf16[8,3,16,90]{3,2,1,0:T(8,128)(2,1)} %shard_map.83), calls=%async_computation.1 | async-start | bytes 196608 | tf_op jit(solution)/shard_map/all_to_all | solution.py:275
  42.2 0.1 copy.23
  42.4 0.6 pad.49.proj_t_ref
  43.0 5.5 %all-to-all-done.1.gc_ref = bf16[8,3,16,90]{3,2,1,0:T(8,128)(2,1)S(1)} async-done(((bf16[8,3,16,90]{3,2,1,0:T(8,128)(2,1)}), bf16[8,3,16,90]{3,2,1,0:T(8,128)(2,1)S(1)}, u32[]{:S(2)}, u32[]{:S(2)}) %all-to-all-start.1) | async-done | bytes 69152 | tf_op jit(solution)/shard_map/all_to_all | solution.py:275
  48.5 0.6 copy-done.3
  49.2 2.2 %shard_map.84.own_ref = bf16[3,48,768]{2,1,0:T(8,128)(2,1)} custom-call(bf16[8,3,16,90]{3,2,1,0:T(8,128)(2,1)} %copy-done.3, f32[3,48,768]{2,1,0:T(8,128)} %get-tuple-element.8.filt_ref, bf16[48,16]{1,0:T(8,128)(2,1)} %pad.49.proj_t_ref), custom_call_target="tpu_custom_call" | custom-call | tf_op jit(solution)/shard_map/pallas_call | solution.py:277
  51.3 3.4 %collective-permute-start.2 = (bf16[3,48,768]{2,1,0:T(8,128)(2,1)}, bf16[3,48,768]{2,1,0:T(8,128)(2,1)S(1)}, u32[]{:S(2)}, u32[]{:S(2)}) collective-permute-start(bf16[3,48,768]{2,1,0:T(8,128)(2,1)} %shard_map.84.own_ref), channel_id=1, source_target_pairs={{0,1},{1,2},{2,3},{4,5},{5,6},{6,7},{8,9},{9,10},{10,11},{12,13},{... | collective-permute-start | bytes 663560 | tf_op jit(solution)/shard_map/ppermute | solution.py:41
  54.7 1.3 %collective-permute-start.3 = (bf16[3,48,768]{2,1,0:T(8,128)(2,1)}, bf16[3,48,768]{2,1,0:T(8,128)(2,1)S(1)}, u32[]{:S(2)}, u32[]{:S(2)}) collective-permute-start(bf16[3,48,768]{2,1,0:T(8,128)(2,1)} %shard_map.84.own_ref), channel_id=1, source_target_pairs={{1,0},{2,1},{3,2},{5,4},{6,5},{7,6},{9,8},{10,9},{11,10},{13,12},{... | collective-permute-start | bytes 663560 | tf_op jit(solution)/shard_map/ppermute | solution.py:42
  56.0 3.5 %collective-permute-done.2.prev_ref = bf16[3,48,768]{2,1,0:T(8,128)(2,1)S(1)} collective-permute-done((bf16[3,48,768]{2,1,0:T(8,128)(2,1)}, bf16[3,48,768]{2,1,0:T(8,128)(2,1)S(1)}, u32[]{:S(2)}, u32[]{:S(2)}) %collective-permute-start.2) | collective-permute-done | bytes 221216 | tf_op jit(solution)/shard_map/ppermute | solution.py:41
  59.5 5.4 %collective-permute-done.3.next_ref = bf16[3,48,768]{2,1,0:T(8,128)(2,1)S(1)} collective-permute-done((bf16[3,48,768]{2,1,0:T(8,128)(2,1)}, bf16[3,48,768]{2,1,0:T(8,128)(2,1)S(1)}, u32[]{:S(2)}, u32[]{:S(2)}) %collective-permute-start.3) | collective-permute-done | bytes 221216 | tf_op jit(solution)/shard_map/ppermute | solution.py:42
  64.9 0.0 copy-done.6
  64.9 0.7 %copy-done.7 = bf16[3,48,768]{2,1,0:T(8,128)(2,1)} copy-done((bf16[3,48,768]{2,1,0:T(8,128)(2,1)}, bf16[3,48,768]{2,1,0:T(8,128)(2,1)S(1)}, u32[]{:S(2)}) %copy-start.7) | copy-done | bytes 221208
  65.6 3.8 %shard_map.85 = bf16[3,45,720]{2,1,0:T(8,128)(2,1)} custom-call(s32[588]{0:T(1024)} %reshape.31.basis_ref, s32[12]{0:T(128)} %step_ref.3, f32[12]{0:T(128)} %multiply_cosine_fusion.1.quad_ref, bf16[3,48,768]{2,1,0:T(8,128)(2,1)} %copy-done.6, bf16[3,48,768]{2,1,0:T(8,128)(2,1)} %shard_map.84.own_ref, bf16[3,48,768]{2,1,0:T(8,128)(2,1)} %copy-done.7, ...), custom_call_target="tpu_custom_call" | custom-call | tf_op jit(solution)/shard_map/pallas_call | solution.py:285
  (18 shorter events, 0.1 us)
Async XLA Ops:
  0.0 1.0 %copy-start.1 = (bf16[1,3,45,720]{3,2,1,0:T(8,128)(2,1)S(1)}, bf16[1,3,45,720]{3,2,1,0:T(8,128)(2,1)}, u32[]{:S(2)}) copy-start(bf16[1,3,45,720]{3,2,1,0:T(8,128)(2,1)} %param.8) | copy-start | bytes 583204
  1.0 6.9 %copy-start.10 = (bf16[4,5,5]{2,0,1:T(4,128)(2,1)S(1)}, bf16[4,5,5]{2,0,1:T(4,128)(2,1)}, u32[]{:S(2)}) copy-start(bf16[4,5,5]{2,0,1:T(4,128)(2,1)} %param.11) | copy-start | bytes 604
  1.0 6.9 %copy-start.8 = (bf16[5,45,45]{2,1,0:T(8,128)(2,1)S(1)}, bf16[5,45,45]{2,1,0:T(8,128)(2,1)}, u32[]{:S(2)}) copy-start(bf16[5,45,45]{2,1,0:T(8,128)(2,1)} %param.9) | copy-start | bytes 60754
  1.1 7.1 %copy-start = (bf16[3,48,768]{2,1,0:T(8,128)(2,1)}, bf16[3,48,768]{2,1,0:T(8,128)(2,1)S(1)}, u32[]{:S(2)}) copy-start(bf16[3,48,768]{2,1,0:T(8,128)(2,1)S(1)} %pad_maximum_fusion.own_ref) | copy-start | bytes 663556
  1.1 11.6 %collective-permute-start = (bf16[3,48,768]{2,1,0:T(8,128)(2,1)S(1)}, bf16[3,48,768]{2,1,0:T(8,128)(2,1)S(1)}, u32[]{:S(2)}, u32[]{:S(2)}) collective-permute-start(bf16[3,48,768]{2,1,0:T(8,128)(2,1)S(1)} %pad_maximum_fusion.own_ref), channel_id=1, source_target_pairs={{0,1},{1,2},{2,3},{4,5},{5,6},{6,7},{8,9},{9,10},{10,11},{12,13},{... | collective-permute-start | bytes 663560 | tf_op jit(solution)/shard_map/ppermute | solution.py:41
  6.0 11.3 %collective-permute-start.1 = (bf16[3,48,768]{2,1,0:T(8,128)(2,1)S(1)}, bf16[3,48,768]{2,1,0:T(8,128)(2,1)S(1)}, u32[]{:S(2)}, u32[]{:S(2)}) collective-permute-start(bf16[3,48,768]{2,1,0:T(8,128)(2,1)S(1)} %pad_maximum_fusion.own_ref), channel_id=1, source_target_pairs={{1,0},{2,1},{3,2},{5,4},{6,5},{7,6},{9,8},{10,9},{11,10},{13,12},{... | collective-permute-start | bytes 663560 | tf_op jit(solution)/shard_map/ppermute | solution.py:42
  8.1 0.7 %copy-start.12 = (s32[12,49]{1,0:T(8,128)S(1)}, s32[12,49]{1,0:T(8,128)}, u32[]{:S(2)}) copy-start(s32[12,49]{1,0:T(8,128)} %param.13) | copy-start | bytes 7060
  8.8 2.0 %copy-start.9 = (f32[4,5,3,90]{3,0,2,1:T(4,128)S(1)}, f32[4,5,3,90]{3,0,2,1:T(4,128)}, u32[]{:S(2)}) copy-start(f32[4,5,3,90]{3,0,2,1:T(4,128)} %param.12) | copy-start | bytes 64804
  9.5 0.7 copy-start.11
  12.8 4.6 %copy-start.4 = (bf16[3,48,768]{2,1,0:T(8,128)(2,1)}, bf16[3,48,768]{2,1,0:T(8,128)(2,1)S(1)}, u32[]{:S(2)}) copy-start(bf16[3,48,768]{2,1,0:T(8,128)(2,1)S(1)} %collective-permute-done.prev_ref) | copy-start | bytes 663556
  17.3 0.7 %copy-start.5 = (bf16[3,48,768]{2,1,0:T(8,128)(2,1)}, bf16[3,48,768]{2,1,0:T(8,128)(2,1)S(1)}, u32[]{:S(2)}) copy-start(bf16[3,48,768]{2,1,0:T(8,128)(2,1)S(1)} %collective-permute-done.1.next_ref) | copy-start | bytes 663556
  22.6 5.0 %copy-start.13 = (f32[4]{0:T(128)S(1)}, f32[4]{0:T(128)}, u32[]{:S(2)}) copy-start(f32[4]{0:T(128)} %constant.23.clone) | copy-start | bytes 52
  22.6 12.0 %all-to-all-start = ((bf16[8,3,20,90]{3,2,1,0:T(8,128)(2,1)}), bf16[8,3,20,90]{3,2,1,0:T(8,128)(2,1)S(1)}, u32[]{:S(2)}, u32[]{:S(2)}) async-start(bf16[8,3,20,90]{3,2,1,0:T(8,128)(2,1)} %get-tuple-element.7), calls=%async_computation | async-start | bytes 294912 | tf_op jit(solution)/shard_map/all_to_all | solution.py:268
  34.6 0.7 copy-start.2
  38.9 9.6 %all-to-all-start.1 = ((bf16[8,3,16,90]{3,2,1,0:T(8,128)(2,1)}), bf16[8,3,16,90]{3,2,1,0:T(8,128)(2,1)S(1)}, u32[]{:S(2)}, u32[]{:S(2)}) async-start(bf16[8,3,16,90]{3,2,1,0:T(8,128)(2,1)} %shard_map.83), calls=%async_computation.1 | async-start | bytes 196608 | tf_op jit(solution)/shard_map/all_to_all | solution.py:275
  48.5 0.6 copy-start.3
  51.3 8.2 %collective-permute-start.2 = (bf16[3,48,768]{2,1,0:T(8,128)(2,1)}, bf16[3,48,768]{2,1,0:T(8,128)(2,1)S(1)}, u32[]{:S(2)}, u32[]{:S(2)}) collective-permute-start(bf16[3,48,768]{2,1,0:T(8,128)(2,1)} %shard_map.84.own_ref), channel_id=1, source_target_pairs={{0,1},{1,2},{2,3},{4,5},{5,6},{6,7},{8,9},{9,10},{10,11},{12,13},{... | collective-permute-start | bytes 663560 | tf_op jit(solution)/shard_map/ppermute | solution.py:41
  54.7 10.2 %collective-permute-start.3 = (bf16[3,48,768]{2,1,0:T(8,128)(2,1)}, bf16[3,48,768]{2,1,0:T(8,128)(2,1)S(1)}, u32[]{:S(2)}, u32[]{:S(2)}) collective-permute-start(bf16[3,48,768]{2,1,0:T(8,128)(2,1)} %shard_map.84.own_ref), channel_id=1, source_target_pairs={{1,0},{2,1},{3,2},{5,4},{6,5},{7,6},{9,8},{10,9},{11,10},{13,12},{... | collective-permute-start | bytes 663560 | tf_op jit(solution)/shard_map/ppermute | solution.py:42
  59.5 5.4 %copy-start.6 = (bf16[3,48,768]{2,1,0:T(8,128)(2,1)}, bf16[3,48,768]{2,1,0:T(8,128)(2,1)S(1)}, u32[]{:S(2)}) copy-start(bf16[3,48,768]{2,1,0:T(8,128)(2,1)S(1)} %collective-permute-done.2.prev_ref) | copy-start | bytes 663556
  64.9 0.7 %copy-start.7 = (bf16[3,48,768]{2,1,0:T(8,128)(2,1)}, bf16[3,48,768]{2,1,0:T(8,128)(2,1)S(1)}, u32[]{:S(2)}) copy-start(bf16[3,48,768]{2,1,0:T(8,128)(2,1)S(1)} %collective-permute-done.3.next_ref) | copy-start | bytes 663556

commit v4 on v3

--- a/solution.py
+++ b/solution.py
@@ -34,12 +34,13 @@
     return jnp.pad(block, pads)
 
 
-def halo(block, axis_name, width):
+def halo(block, axis_name, width, axis=0):
     count = lax.axis_size(axis_name)
     forward = [(i, i + 1) for i in range(count - 1)]
     backward = [(target, source) for source, target in forward]
-    low = lax.ppermute(block[block.shape[0] - width :], axis_name, forward)
-    high = lax.ppermute(block[:width], axis_name, backward)
+    size = block.shape[axis]
+    low = lax.ppermute(lax.slice_in_dim(block, size - width, size, axis=axis), axis_name, forward)
+    high = lax.ppermute(lax.slice_in_dim(block, 0, width, axis=axis), axis_name, backward)
     return low, high
 
 
@@ -75,7 +76,7 @@
 
 
 def forward_kernel(basis_ref, step_ref, quad_ref, prev_ref, own_ref, next_ref, table_ref,
-                   proj_ref, sub_ref, filt_ref, fc_ref):
+                   proj_ref, sub_ref, slope_ref, fc_ref):
     rows, cp, width_p = own_ref.shape
     first = lax.axis_index("lat") * rows
     ext = (
@@ -105,7 +106,7 @@
             shift = lax.rem((HALF - b) * step + width_p, width_p)
             total = total + pltpu.roll(taps[b * cp : (b + 1) * cp], shift, 1)
         filtered = total * quad_ref[g]
-        filt_ref[i] = filtered
+        slope_ref[i] = gelu_grad(filtered)
         activated = gelu(filtered).astype(jnp.bfloat16)
         coarse = jnp.dot(
             proj_ref[...], activated, preferred_element_type=jnp.float32
@@ -154,30 +155,25 @@
             out_ref[m, i] = jnp.concatenate(coarse, axis=0).astype(out_ref.dtype)
 
 
-def grad_filtered_kernel(gc_ref, filt_ref, proj_t_ref, out_ref):
-    blocks, rows = gc_ref.shape[0], gc_ref.shape[1]
-    width_p = filt_ref.shape[2]
-    for i in range(rows):
-        row = jnp.concatenate([gc_ref[q, i] for q in range(blocks)], axis=1)
-        width = row.shape[1]
-        extra = width_p - width
-        lo = extra // 2
-        hi = extra - lo
-        ring = jnp.concatenate([row, row[:, :lo], row[:, width - hi :]], axis=1)
-        grad_act = jnp.dot(proj_t_ref[...], ring, preferred_element_type=jnp.float32)
-        out_ref[i] = (grad_act * gelu_grad(filt_ref[i])).astype(jnp.bfloat16)
-
-
-def backward_kernel(basis_ref, step_ref, quad_ref, prev_ref, own_ref, next_ref, table_ref,
-                    out_ref):
-    rows, cp, width_p = own_ref.shape
+def ring_row(blocks_ref, i, width_p):
+    row = jnp.concatenate([blocks_ref[q, i] for q in range(blocks_ref.shape[0])], axis=1)
+    width = row.shape[1]
+    extra = width_p - width
+    lo = extra // 2
+    hi = extra - lo
+    return jnp.concatenate([row, row[:, :lo], row[:, width - hi :]], axis=1)
+
+
+def backward_kernel(basis_ref, step_ref, quad_ref, gc_prev_ref, gc_own_ref, gc_next_ref,
+                    sl_prev_ref, sl_own_ref, sl_next_ref, proj_t_ref, table_ref, out_ref):
+    rows, cp, width_p = sl_own_ref.shape
     channels, width = out_ref.shape[1], out_ref.shape[2]
     total_rows = step_ref.shape[0]
     first = lax.axis_index("lat") * rows
-    ext = (
-        [prev_ref[e] for e in range(HALF)]
-        + [own_ref[e] for e in range(rows)]
-        + [next_ref[e] for e in range(HALF)]
+    sources = (
+        [(gc_prev_ref, sl_prev_ref, e) for e in range(HALF)]
+        + [(gc_own_ref, sl_own_ref, e) for e in range(rows)]
+        + [(gc_next_ref, sl_next_ref, e) for e in range(HALF)]
     )
     acc = [None] * rows
     for e in range(rows + 2 * HALF):
@@ -197,7 +193,12 @@
             ],
             axis=0,
         )
-        source = ext[e]
+        gc_ref, sl_ref, r = sources[e]
+        grad_act = jnp.dot(
+            proj_t_ref[...], ring_row(gc_ref, r, width_p).astype(jnp.bfloat16),
+            preferred_element_type=jnp.float32,
+        )
+        source = (grad_act * sl_ref[r]).astype(jnp.bfloat16)
         rolled = []
         for b in range(TAPS):
             if b == HALF:
@@ -255,7 +256,7 @@
     own = to_ring(pad_axis(latents[0], 1, cp), width_p)
     low, high = halo(own, "lat", HALF)
 
-    filtered, fc = pl.pallas_call(
+    slope, fc = pl.pallas_call(
         forward_kernel,
         out_shape=(
             jax.ShapeDtypeStruct((rows, cp, width_p), jnp.float32),
@@ -274,20 +275,15 @@
     )(sub_flat, weight_all, fc_owned, truth)
     gc_home = lax.all_to_all(gc_owned, "member", split_axis=0, concat_axis=0, tiled=True)
     proj_t = pad_axis(pad_axis(project.T, 0, cp), 1, vp)
-    grad_filtered = pl.pallas_call(
-        grad_filtered_kernel,
-        out_shape=jax.ShapeDtypeStruct((rows, cp, width_p), jnp.bfloat16),
-        in_specs=[vmem()] * 3,
-        out_specs=vmem(),
-    )(gc_home, filtered, proj_t)
-
-    g_low, g_high = halo(grad_filtered, "lat", HALF)
+    sl_low, sl_high = halo(slope, "lat", HALF)
+    gc_low, gc_high = halo(gc_home, "lat", HALF, axis=1)
     result = pl.pallas_call(
         backward_kernel,
         out_shape=jax.ShapeDtypeStruct((rows, channels, width), jnp.bfloat16),
-        in_specs=[smem(), smem(), smem()] + [vmem()] * 4,
+        in_specs=[smem(), smem(), smem()] + [vmem()] * 8,
         out_specs=vmem(),
-    )(basis_flat, step_rows, quad_all, g_low, grad_filtered, g_high, tables)
+    )(basis_flat, step_rows, quad_all, gc_low, gc_home, gc_high, sl_low, slope, sl_high,
+      proj_t, tables)
     return result[None]
 
 

time: 70 us -> 70.4 us (level)
  the two profiles are of different devices: /device:TPU:0 before, /device:TPU:4 now
where the time goes in v4:
time: 70.4 us; the launch traced here: 69.8 us
  starting transfers between devices  22.8 us (32%)
  Pallas kernels  14.1 us (20%)
  waiting for transfers between devices  12.7 us (18%)
  blocking collectives  9.61 us (14%)
  local copies, waits for them, and re-layouts  8.8 us (12%)
  other arithmetic  1.53 us (2%)
    all_to_all x1, blocking collectives, on_device(): lax.all_to_all(gc_owned, 'member', split_axis=0, concat_axis=0, tiled=True)  9.61 us
    ppermute x3, starting transfers between devices, halo(): lax.ppermute(lax.slice_in_dim(block, size - width, size, axis=axis), axis...  9.5 us
    ppermute x3, starting transfers between devices, halo(): lax.ppermute(lax.slice_in_dim(block, 0, width, axis=axis), axis_name, bac...  8.17 us
    ppermute x3, waiting for transfers between devices, halo(): lax.ppermute(lax.slice_in_dim(block, size - width, size, axis=axis), axis...  7.63 us
    pallas_call x1, Pallas kernels, on_device(): pl.pallas_call(backward_kernel, out_shape=jax.ShapeDtypeStruct((rows, cha...  5.87 us
    all_to_all x1, starting transfers between devices, on_device(): lax.all_to_all(fc, 'member', split_axis=0, concat_axis=0, tiled=True)  5.13 us
    all_to_all x1, waiting for transfers between devices, on_device(): lax.all_to_all(fc, 'member', split_axis=0, concat_axis=0, tiled=True)  5.05 us
    pallas_call x1, Pallas kernels, on_device(): pl.pallas_call(forward_kernel, out_shape=(jax.ShapeDtypeStruct((rows, cp,...  4.71 us
  transfers between devices with their start and end apart: 7, of which 3 were waited for; matrix products, arithmetic and copies ran while one was open for 9% of the time, Pallas kernels for 5%

profile of v4, /device:TPU:4, one launch (start us, length us, event | category | flops | bytes accessed | tf_op | source)
XLA Modules:
  0.0 69.8 jit_solution(17938554932644547210)
XLA Ops:
  0.0 0.9 %pad_slice_fusion.1 = (bf16[3,48,24]{2,1,0:T(8,128)(2,1)S(1)}, bf16[3,48,24]{2,1,0:T(8,128)(2,1)S(1)}) fusion(bf16[3,45,720]{2,1,0:T(8,128)(2,1)} %bitcast.13), kind=kLoop, calls=%fused_computation.9 | loop fusion | bytes 208224 | tf_op jit(solution)/shard_map/slice | solution.py:27
  0.9 0.0 copy-done.1
  1.0 0.0 copy-start.14
  1.0 0.0 copy-start.10
  1.0 0.1 pad_maximum_fusion.own_ref
  1.1 0.0 copy-start
  1.1 0.0 copy-start.13
  1.1 3.5 %collective-permute-start.1 = (bf16[3,48,768]{2,1,0:T(8,128)(2,1)S(1)}, bf16[3,48,768]{2,1,0:T(8,128)(2,1)S(1)}, u32[]{:S(2)}, u32[]{:S(2)}) collective-permute-start(bf16[3,48,768]{2,1,0:T(8,128)(2,1)S(1)} %pad_maximum_fusion.own_ref), channel_id=1, source_target_pairs={{1,0},{2,1},{3,2},{5,4},{6,5},{7,6},{9,8},{10,9},{11,10},{13,12},{... | collective-permute-start | bytes 663560 | tf_op jit(solution)/shard_map/ppermute | solution.py:43
  4.6 2.5 %collective-permute-start = (bf16[3,48,768]{2,1,0:T(8,128)(2,1)S(1)}, bf16[3,48,768]{2,1,0:T(8,128)(2,1)S(1)}, u32[]{:S(2)}, u32[]{:S(2)}) collective-permute-start(bf16[3,48,768]{2,1,0:T(8,128)(2,1)S(1)} %pad_maximum_fusion.own_ref), channel_id=1, source_target_pairs={{0,1},{1,2},{2,3},{4,5},{5,6},{6,7},{8,9},{9,10},{10,11},{12,13},{... | collective-permute-start | bytes 663560 | tf_op jit(solution)/shard_map/ppermute | solution.py:42
  7.2 0.7 reshape.31.basis_ref
  7.8 0.6 pad.48.proj_ref
  8.4 0.1 copy-done.12
  8.6 0.6 pad.38.sub_ref
  9.2 0.1 copy.17
  9.3 0.1 copy.18
  9.4 0.6 multiply_cosine_fusion.1.quad_ref
  10.1 0.7 pad_maximum_fusion.1.table_ref
  10.8 0.0 collective-permute-done.1.next_ref
  10.8 4.0 %collective-permute-done.prev_ref = bf16[3,48,768]{2,1,0:T(8,128)(2,1)S(1)} collective-permute-done((bf16[3,48,768]{2,1,0:T(8,128)(2,1)S(1)}, bf16[3,48,768]{2,1,0:T(8,128)(2,1)S(1)}, u32[]{:S(2)}, u32[]{:S(2)}) %collective-permute-start) | collective-permute-done | bytes 221216 | tf_op jit(solution)/shard_map/ppermute | solution.py:42
  14.8 0.7 copy-done.7
  15.5 4.7 %shard_map.82 = (f32[3,48,768]{2,1,0:T(8,128)}, bf16[8,3,20,90]{3,2,1,0:T(8,128)(2,1)}) custom-call(s32[588]{0:T(1024)} %reshape.31.basis_ref, s32[12]{0:T(128)} %step_ref.3, f32[12]{0:T(128)} %multiply_cosine_fusion.1.quad_ref, bf16[3,48,768]{2,1,0:T(8,128)(2,1)} %copy-done.7, bf16[3,48,768]{2,1,0:T(8,128)(2,1)} %copy-done, bf16[3,48,768]{2,1,0:T(8,128)(2,1)} %copy-done.6, ...), custom_call_target="tpu_custom_call" | custom-call | tf_op jit(solution)/shard_map/pallas_call | solution.py:259
  20.2 1.9 %collective-permute-start.5 = (f32[3,48,768]{2,1,0:T(8,128)}, f32[3,48,768]{2,1,0:T(8,128)S(1)}, u32[]{:S(2)}, u32[]{:S(2)}) collective-permute-start(f32[3,48,768]{2,1,0:T(8,128)} %get-tuple-element.8.sl_own_ref), channel_id=1, source_target_pairs={{1,0},{2,1},{3,2},{5,4},{6,5},{7,6},{9,8},{10,9},{11,10},{13,12},{... | collective-permute-start | bytes 1327112 | tf_op jit(solution)/shard_map/ppermute | solution.py:43
  22.1 3.9 %collective-permute-start.4 = (f32[3,48,768]{2,1,0:T(8,128)}, f32[3,48,768]{2,1,0:T(8,128)S(1)}, u32[]{:S(2)}, u32[]{:S(2)}) collective-permute-start(f32[3,48,768]{2,1,0:T(8,128)} %get-tuple-element.8.sl_own_ref), channel_id=1, source_target_pairs={{0,1},{1,2},{2,3},{4,5},{5,6},{6,7},{8,9},{9,10},{10,11},{12,13},{... | collective-permute-start | bytes 1327112 | tf_op jit(solution)/shard_map/ppermute | solution.py:42
  26.1 0.0 copy-start.15
  26.1 0.0 copy-start.11
  26.1 5.1 %all-to-all-start = ((bf16[8,3,20,90]{3,2,1,0:T(8,128)(2,1)}), bf16[8,3,20,90]{3,2,1,0:T(8,128)(2,1)S(1)}, u32[]{:S(2)}, u32[]{:S(2)}) async-start(bf16[8,3,20,90]{3,2,1,0:T(8,128)(2,1)} %get-tuple-element.7), calls=%async_computation | async-start | bytes 294912 | tf_op jit(solution)/shard_map/all_to_all | solution.py:269
  31.2 0.0 copy-done.15
  31.2 0.1 multiply_cosine_fusion
  31.4 0.6 reshape.40.weight_ref
  31.9 0.6 reshape.37.sub_ref
  32.6 0.6 copy.27
  33.2 5.0 %all-to-all-done.fc_ref = bf16[8,3,20,90]{3,2,1,0:T(8,128)(2,1)S(1)} async-done(((bf16[8,3,20,90]{3,2,1,0:T(8,128)(2,1)}), bf16[8,3,20,90]{3,2,1,0:T(8,128)(2,1)S(1)}, u32[]{:S(2)}, u32[]{:S(2)}) %all-to-all-start) | async-done | bytes 86432 | tf_op jit(solution)/shard_map/all_to_all | solution.py:269
  38.2 0.7 copy-done.2
  38.9 3.6 %shard_map.83 = bf16[8,3,16,90]{3,2,1,0:T(8,128)(2,1)} custom-call(f32[100]{0:T(128)} %reshape.37.sub_ref, f32[48]{0:T(128)} %reshape.40.weight_ref, bf16[8,3,20,90]{3,2,1,0:T(8,128)(2,1)} %copy-done.2, f32[3,20,90]{2,1,0:T(8,128)} %bitcast.16), custom_call_target="tpu_custom_call" | custom-call | tf_op jit(solution)/shard_map/pallas_call | solution.py:270
  42.5 9.6 %all_to_all.10.gc_own_ref = bf16[8,3,16,90]{3,2,1,0:T(8,128)(2,1)S(1)} all-to-all(bf16[8,3,16,90]{3,2,1,0:T(8,128)(2,1)} %shard_map.83), channel_id=1, replica_groups=mesh['member'=8,'lat'=4] {'member'}, dimensions={0} | all-to-all | bytes 138240 | tf_op jit(solution)/shard_map/all_to_all | solution.py:276
  52.1 2.8 %collective-permute-start.3 = (bf16[8,3,16,90]{3,2,1,0:T(8,128)(2,1)S(1)}, bf16[8,3,16,90]{3,2,1,0:T(8,128)(2,1)S(1)}, u32[]{:S(2)}, u32[]{:S(2)}) collective-permute-start(bf16[8,3,16,90]{3,2,1,0:T(8,128)(2,1)S(1)} %all_to_all.10.gc_own_ref), channel_id=1, source_target_pairs={{1,0},{2,1},{3,2},{5,4},{6,5},{7,6},{9,8},{10,9},{11,10},{13,12},{... | collective-permute-start | bytes 207368 | tf_op jit(solution)/shard_map/ppermute | solution.py:43
  54.9 3.0 %collective-permute-start.2 = (bf16[8,3,16,90]{3,2,1,0:T(8,128)(2,1)S(1)}, bf16[8,3,16,90]{3,2,1,0:T(8,128)(2,1)S(1)}, u32[]{:S(2)}, u32[]{:S(2)}) collective-permute-start(bf16[8,3,16,90]{3,2,1,0:T(8,128)(2,1)S(1)} %all_to_all.10.gc_own_ref), channel_id=1, source_target_pairs={{0,1},{1,2},{2,3},{4,5},{5,6},{6,7},{8,9},{9,10},{10,11},{12,13},{... | collective-permute-start | bytes 207368 | tf_op jit(solution)/shard_map/ppermute | solution.py:42
  57.9 0.1 copy.23
  58.0 0.6 pad.49.proj_t_ref
  58.6 0.0 collective-permute-done.3.gc_next_ref
  58.6 3.6 %collective-permute-done.2.gc_prev_ref = bf16[8,3,16,90]{3,2,1,0:T(8,128)(2,1)S(1)} collective-permute-done((bf16[8,3,16,90]{3,2,1,0:T(8,128)(2,1)S(1)}, bf16[8,3,16,90]{3,2,1,0:T(8,128)(2,1)S(1)}, u32[]{:S(2)}, u32[]{:S(2)}) %collective-permute-start.2) | collective-permute-done | bytes 69152 | tf_op jit(solution)/shard_map/ppermute | solution.py:42
  62.3 0.0 collective-permute-done.5.sl_next_ref
  62.3 0.0 collective-permute-done.4.sl_prev_ref
  62.3 0.0 copy-done.5
  62.3 0.6 copy-done.9
  62.9 0.2 copy-done.3
  63.1 0.8 %copy-done.4 = f32[3,48,768]{2,1,0:T(8,128)} copy-done((f32[3,48,768]{2,1,0:T(8,128)}, f32[3,48,768]{2,1,0:T(8,128)S(1)}, u32[]{:S(2)}) %copy-start.4) | copy-done | bytes 442392
  63.9 5.9 %shard_map.84 = bf16[3,45,720]{2,1,0:T(8,128)(2,1)} custom-call(s32[588]{0:T(1024)} %reshape.31.basis_ref, s32[12]{0:T(128)} %step_ref.3, f32[12]{0:T(128)} %multiply_cosine_fusion.1.quad_ref, bf16[8,3,16,90]{3,2,1,0:T(8,128)(2,1)} %copy-done.9, bf16[8,3,16,90]{3,2,1,0:T(8,128)(2,1)} %copy-done.5, bf16[8,3,16,90]{3,2,1,0:T(8,128)(2,1)} %copy-done.8, ...), custom_call_target="tpu_custom_call" | custom-call | tf_op jit(solution)/shard_map/pallas_call | solution.py:280
  (24 shorter events, 0.1 us)
Async XLA Ops:
  0.0 1.0 %copy-start.1 = (bf16[1,3,45,720]{3,2,1,0:T(8,128)(2,1)S(1)}, bf16[1,3,45,720]{3,2,1,0:T(8,128)(2,1)}, u32[]{:S(2)}) copy-start(bf16[1,3,45,720]{3,2,1,0:T(8,128)(2,1)} %param.8) | copy-start | bytes 583204
  1.0 6.1 %copy-start.14 = (s32[12,49]{1,0:T(8,128)S(1)}, s32[12,49]{1,0:T(8,128)}, u32[]{:S(2)}) copy-start(s32[12,49]{1,0:T(8,128)} %param.13) | copy-start | bytes 7060
  1.0 8.1 %copy-start.10 = (bf16[5,45,45]{2,1,0:T(8,128)(2,1)S(1)}, bf16[5,45,45]{2,1,0:T(8,128)(2,1)}, u32[]{:S(2)}) copy-start(bf16[5,45,45]{2,1,0:T(8,128)(2,1)} %param.9) | copy-start | bytes 60754
  1.1 8.3 %copy-start = (bf16[3,48,768]{2,1,0:T(8,128)(2,1)}, bf16[3,48,768]{2,1,0:T(8,128)(2,1)S(1)}, u32[]{:S(2)}) copy-start(bf16[3,48,768]{2,1,0:T(8,128)(2,1)S(1)} %pad_maximum_fusion.own_ref) | copy-start | bytes 663556
  1.1 6.7 %copy-start.13 = (bf16[5,45]{1,0:T(8,128)(2,1)S(1)}, bf16[5,45]{1,0:T(8,128)(2,1)}, u32[]{:S(2)}) copy-start(bf16[5,45]{1,0:T(8,128)(2,1)} %param.10) | copy-start | bytes 1354
  1.1 9.6 %collective-permute-start.1 = (bf16[3,48,768]{2,1,0:T(8,128)(2,1)S(1)}, bf16[3,48,768]{2,1,0:T(8,128)(2,1)S(1)}, u32[]{:S(2)}, u32[]{:S(2)}) collective-permute-start(bf16[3,48,768]{2,1,0:T(8,128)(2,1)S(1)} %pad_maximum_fusion.own_ref), channel_id=1, source_target_pairs={{1,0},{2,1},{3,2},{5,4},{6,5},{7,6},{9,8},{10,9},{11,10},{13,12},{... | collective-permute-start | bytes 663560 | tf_op jit(solution)/shard_map/ppermute | solution.py:43
  4.6 10.2 %collective-permute-start = (bf16[3,48,768]{2,1,0:T(8,128)(2,1)S(1)}, bf16[3,48,768]{2,1,0:T(8,128)(2,1)S(1)}, u32[]{:S(2)}, u32[]{:S(2)}) collective-permute-start(bf16[3,48,768]{2,1,0:T(8,128)(2,1)S(1)} %pad_maximum_fusion.own_ref), channel_id=1, source_target_pairs={{0,1},{1,2},{2,3},{4,5},{5,6},{6,7},{8,9},{9,10},{10,11},{12,13},{... | collective-permute-start | bytes 663560 | tf_op jit(solution)/shard_map/ppermute | solution.py:42
  7.8 0.7 copy-start.12
  10.8 4.0 %copy-start.6 = (bf16[3,48,768]{2,1,0:T(8,128)(2,1)}, bf16[3,48,768]{2,1,0:T(8,128)(2,1)S(1)}, u32[]{:S(2)}) copy-start(bf16[3,48,768]{2,1,0:T(8,128)(2,1)S(1)} %collective-permute-done.1.next_ref) | copy-start | bytes 663556
  14.8 0.7 copy-start.7
  20.2 42.1 %collective-permute-start.5 = (f32[3,48,768]{2,1,0:T(8,128)}, f32[3,48,768]{2,1,0:T(8,128)S(1)}, u32[]{:S(2)}, u32[]{:S(2)}) collective-permute-start(f32[3,48,768]{2,1,0:T(8,128)} %get-tuple-element.8.sl_own_ref), channel_id=1, source_target_pairs={{1,0},{2,1},{3,2},{5,4},{6,5},{7,6},{9,8},{10,9},{11,10},{13,12},{... | collective-permute-start | bytes 1327112 | tf_op jit(solution)/shard_map/ppermute | solution.py:43
  22.1 40.2 %collective-permute-start.4 = (f32[3,48,768]{2,1,0:T(8,128)}, f32[3,48,768]{2,1,0:T(8,128)S(1)}, u32[]{:S(2)}, u32[]{:S(2)}) collective-permute-start(f32[3,48,768]{2,1,0:T(8,128)} %get-tuple-element.8.sl_own_ref), channel_id=1, source_target_pairs={{0,1},{1,2},{2,3},{4,5},{5,6},{6,7},{8,9},{9,10},{10,11},{12,13},{... | collective-permute-start | bytes 1327112 | tf_op jit(solution)/shard_map/ppermute | solution.py:42
  26.1 5.2 %copy-start.15 = (f32[4]{0:T(128)S(1)}, f32[4]{0:T(128)}, u32[]{:S(2)}) copy-start(f32[4]{0:T(128)} %constant.23.clone) | copy-start | bytes 52
  26.1 6.5 %copy-start.11 = (f32[4,5,3,90]{3,0,2,1:T(4,128)S(1)}, f32[4,5,3,90]{3,0,2,1:T(4,128)}, u32[]{:S(2)}) copy-start(f32[4,5,3,90]{3,0,2,1:T(4,128)} %param.12) | copy-start | bytes 64804
  26.1 12.1 %all-to-all-start = ((bf16[8,3,20,90]{3,2,1,0:T(8,128)(2,1)}), bf16[8,3,20,90]{3,2,1,0:T(8,128)(2,1)S(1)}, u32[]{:S(2)}, u32[]{:S(2)}) async-start(bf16[8,3,20,90]{3,2,1,0:T(8,128)(2,1)} %get-tuple-element.7), calls=%async_computation | async-start | bytes 294912 | tf_op jit(solution)/shard_map/all_to_all | solution.py:269
  38.2 0.7 copy-start.2
  52.1 10.2 %copy-start.5 = (bf16[8,3,16,90]{3,2,1,0:T(8,128)(2,1)}, bf16[8,3,16,90]{3,2,1,0:T(8,128)(2,1)S(1)}, u32[]{:S(2)}) copy-start(bf16[8,3,16,90]{3,2,1,0:T(8,128)(2,1)S(1)} %all_to_all.10.gc_own_ref) | copy-start | bytes 207364
  52.1 6.6 %collective-permute-start.3 = (bf16[8,3,16,90]{3,2,1,0:T(8,128)(2,1)S(1)}, bf16[8,3,16,90]{3,2,1,0:T(8,128)(2,1)S(1)}, u32[]{:S(2)}, u32[]{:S(2)}) collective-permute-start(bf16[8,3,16,90]{3,2,1,0:T(8,128)(2,1)S(1)} %all_to_all.10.gc_own_ref), channel_id=1, source_target_pairs={{1,0},{2,1},{3,2},{5,4},{6,5},{7,6},{9,8},{10,9},{11,10},{13,12},{... | collective-permute-start | bytes 207368 | tf_op jit(solution)/shard_map/ppermute | solution.py:43
  54.9 7.4 %collective-permute-start.2 = (bf16[8,3,16,90]{3,2,1,0:T(8,128)(2,1)S(1)}, bf16[8,3,16,90]{3,2,1,0:T(8,128)(2,1)S(1)}, u32[]{:S(2)}, u32[]{:S(2)}) collective-permute-start(bf16[8,3,16,90]{3,2,1,0:T(8,128)(2,1)S(1)} %all_to_all.10.gc_own_ref), channel_id=1, source_target_pairs={{0,1},{1,2},{2,3},{4,5},{5,6},{6,7},{8,9},{9,10},{10,11},{12,13},{... | collective-permute-start | bytes 207368 | tf_op jit(solution)/shard_map/ppermute | solution.py:42
  58.6 3.7 %copy-start.8 = (bf16[8,3,16,90]{3,2,1,0:T(8,128)(2,1)}, bf16[8,3,16,90]{3,2,1,0:T(8,128)(2,1)S(1)}, u32[]{:S(2)}) copy-start(bf16[8,3,16,90]{3,2,1,0:T(8,128)(2,1)S(1)} %collective-permute-done.3.gc_next_ref) | copy-start | bytes 207364
  62.3 0.6 copy-start.9
  62.3 0.8 %copy-start.3 = (f32[3,48,768]{2,1,0:T(8,128)}, f32[3,48,768]{2,1,0:T(8,128)S(1)}, u32[]{:S(2)}) copy-start(f32[3,48,768]{2,1,0:T(8,128)S(1)} %collective-permute-done.5.sl_next_ref) | copy-start | bytes 1327108
  63.1 0.8 %copy-start.4 = (f32[3,48,768]{2,1,0:T(8,128)}, f32[3,48,768]{2,1,0:T(8,128)S(1)}, u32[]{:S(2)}) copy-start(f32[3,48,768]{2,1,0:T(8,128)S(1)} %collective-permute-done.4.sl_prev_ref) | copy-start | bytes 1327108

commit v5 on v4

--- a/solution.py
+++ b/solution.py
@@ -121,7 +121,8 @@
 
 def score_kernel(sub_ref, weight_ref, fc_ref, truth_ref, out_ref):
     members, rows, cells, block = fc_ref.shape
-    vp = out_ref.shape[2]
+    bands, vp = out_ref.shape[1], out_ref.shape[3]
+    band = lax.axis_index("lat")
     variables = sub_ref.shape[0] // cells
     subcells = cells // variables
     total_rows = weight_ref.shape[0] // subcells
@@ -152,11 +153,16 @@
                     term = sub_ref[r * variables + u] * grad[r : r + 1]
                     acc = term if acc is None else acc + term
                 coarse.append(acc)
-            out_ref[m, i] = jnp.concatenate(coarse, axis=0).astype(out_ref.dtype)
-
-
-def ring_row(blocks_ref, i, width_p):
-    row = jnp.concatenate([blocks_ref[q, i] for q in range(blocks_ref.shape[0])], axis=1)
+            coarse = jnp.concatenate(coarse, axis=0).astype(out_ref.dtype)
+            for lp in range(bands):
+                near = jnp.abs(lp - band) <= 1
+                out_ref[m, lp, i] = jnp.where(near, coarse, jnp.zeros_like(coarse))
+
+
+def ring_row(blocks_ref, band, i, width_p):
+    row = jnp.concatenate(
+        [blocks_ref[q, band, i] for q in range(blocks_ref.shape[0])], axis=1
+    )
     width = row.shape[1]
     extra = width_p - width
     lo = extra // 2
@@ -164,16 +170,20 @@
     return jnp.concatenate([row, row[:, :lo], row[:, width - hi :]], axis=1)
 
 
-def backward_kernel(basis_ref, step_ref, quad_ref, gc_prev_ref, gc_own_ref, gc_next_ref,
-                    sl_prev_ref, sl_own_ref, sl_next_ref, proj_t_ref, table_ref, out_ref):
+def backward_kernel(basis_ref, step_ref, quad_ref, gc_ref, sl_prev_ref, sl_own_ref,
+                    sl_next_ref, proj_t_ref, table_ref, out_ref):
     rows, cp, width_p = sl_own_ref.shape
+    bands = gc_ref.shape[1]
     channels, width = out_ref.shape[1], out_ref.shape[2]
     total_rows = step_ref.shape[0]
-    first = lax.axis_index("lat") * rows
+    band = lax.axis_index("lat")
+    first = band * rows
+    below = jnp.maximum(band - 1, 0)
+    above = jnp.minimum(band + 1, bands - 1)
     sources = (
-        [(gc_prev_ref, sl_prev_ref, e) for e in range(HALF)]
-        + [(gc_own_ref, sl_own_ref, e) for e in range(rows)]
-        + [(gc_next_ref, sl_next_ref, e) for e in range(HALF)]
+        [(below, sl_prev_ref, rows - HALF + e, e) for e in range(HALF)]
+        + [(band, sl_own_ref, e, e) for e in range(rows)]
+        + [(above, sl_next_ref, e, e) for e in range(HALF)]
     )
     acc = [None] * rows
     for e in range(rows + 2 * HALF):
@@ -193,12 +203,12 @@
             ],
             axis=0,
         )
-        gc_ref, sl_ref, r = sources[e]
+        src_band, sl_ref, r, rs = sources[e]
         grad_act = jnp.dot(
-            proj_t_ref[...], ring_row(gc_ref, r, width_p).astype(jnp.bfloat16),
+            proj_t_ref[...], ring_row(gc_ref, src_band, r, width_p).astype(jnp.bfloat16),
             preferred_element_type=jnp.float32,
         )
-        source = (grad_act * sl_ref[r]).astype(jnp.bfloat16)
+        source = (grad_act * sl_ref[rs]).astype(jnp.bfloat16)
         rolled = []
         for b in range(TAPS):
             if b == HALF:
@@ -242,6 +252,7 @@
     weight_all = subcell_weight(0, total_rows, total_rows).reshape(-1)
     sub_flat = subcell_maps.astype(jnp.float32).reshape(-1)
     blocks = lax.axis_size("member")
+    bands = lax.axis_size("lat")
     block = width // blocks
     truth = verifying_truth.reshape(subcells * variables, rows, block).transpose(1, 0, 2)
 
@@ -269,21 +280,22 @@
     fc_owned = lax.all_to_all(fc, "member", split_axis=0, concat_axis=0, tiled=True)
     gc_owned = pl.pallas_call(
         score_kernel,
-        out_shape=jax.ShapeDtypeStruct((blocks, rows, vp, block), jnp.bfloat16),
+        out_shape=jax.ShapeDtypeStruct((blocks, bands, rows, vp, block), jnp.bfloat16),
         in_specs=[smem(), smem()] + [vmem()] * 2,
         out_specs=vmem(),
     )(sub_flat, weight_all, fc_owned, truth)
-    gc_home = lax.all_to_all(gc_owned, "member", split_axis=0, concat_axis=0, tiled=True)
+    gc_home = lax.all_to_all(
+        gc_owned.reshape((blocks * bands,) + gc_owned.shape[2:]),
+        ("member", "lat"), split_axis=0, concat_axis=0, tiled=True,
+    ).reshape(gc_owned.shape)
     proj_t = pad_axis(pad_axis(project.T, 0, cp), 1, vp)
     sl_low, sl_high = halo(slope, "lat", HALF)
-    gc_low, gc_high = halo(gc_home, "lat", HALF, axis=1)
     result = pl.pallas_call(
         backward_kernel,
         out_shape=jax.ShapeDtypeStruct((rows, channels, width), jnp.bfloat16),
-        in_specs=[smem(), smem(), smem()] + [vmem()] * 8,
+        in_specs=[smem(), smem(), smem()] + [vmem()] * 6,
         out_specs=vmem(),
-    )(basis_flat, step_rows, quad_all, gc_low, gc_home, gc_high, sl_low, slope, sl_high,
-      proj_t, tables)
+    )(basis_flat, step_rows, quad_all, gc_home, sl_low, slope, sl_high, proj_t, tables)
     return result[None]
 
 

time: 70.4 us -> 74.3 us (1.055)
  waiting for transfers between devices: 12.7 us -> 28.6 us
  blocking collectives: 9.61 us -> 0 us
  starting transfers between devices: 22.8 us -> 21.2 us
    ppermute x3 -> x2, waiting for transfers between devices: 0.01 us -> 10 us  [halo(): lax.ppermute(lax.slice_in_dim(block, 0, width, axis=axis), axis_name, bac...]
    all_to_all x1 -> x0, blocking collectives: 9.61 us -> none  [on_device(): lax.all_to_all(gc_owned, 'member', split_axis=0, concat_axis=0, tiled=True)]
    ppermute x3 -> x2, waiting for transfers between devices: 7.63 us -> 13.6 us  [halo(): lax.ppermute(lax.slice_in_dim(block, size - width, size, axis=axis), axis...]
    ppermute x3 -> x2, starting transfers between devices: 9.5 us -> 5.01 us  [halo(): lax.ppermute(lax.slice_in_dim(block, size - width, size, axis=axis), axis...]
    all_to_all x0 -> x1, starting transfers between devices: none -> 4.05 us  [on_device(): lax.all_to_all(gc_owned.reshape((blocks * bands,) + gc_owned.shape[2:]),...]
    ppermute x3 -> x2, starting transfers between devices: 8.17 us -> 6.84 us  [halo(): lax.ppermute(lax.slice_in_dim(block, 0, width, axis=axis), axis_name, bac...]
    unnamed x35 -> x33, local copies, waits for them, and re-layouts: 3.39 us -> 2.6 us
  transfers between devices with their start and end apart: 7 -> 6, of which waited for: 3 -> 4; matrix products, arithmetic and copies ran while one was open for 9% -> 8% of each run, Pallas kernels for 5% -> 0%
where the time goes in v5:
time: 74.3 us; the launch traced here: 73.8 us
  waiting for transfers between devices  28.6 us (38%)
  starting transfers between devices  21.2 us (29%)
  Pallas kernels  14.3 us (19%)
  local copies, waits for them, and re-layouts  8.09 us (11%)
  other arithmetic  1.5 us (2%)
    ppermute x2, waiting for transfers between devices, halo(): lax.ppermute(lax.slice_in_dim(block, size - width, size, axis=axis), axis...  13.6 us
    ppermute x2, waiting for transfers between devices, halo(): lax.ppermute(lax.slice_in_dim(block, 0, width, axis=axis), axis_name, bac...  10 us
    ppermute x2, starting transfers between devices, halo(): lax.ppermute(lax.slice_in_dim(block, 0, width, axis=axis), axis_name, bac...  6.84 us
    pallas_call x1, Pallas kernels, on_device(): pl.pallas_call(backward_kernel, out_shape=jax.ShapeDtypeStruct((rows, cha...  5.88 us
    all_to_all x1, starting transfers between devices, on_device(): lax.all_to_all(fc, 'member', split_axis=0, concat_axis=0, tiled=True)  5.26 us
    ppermute x2, starting transfers between devices, halo(): lax.ppermute(lax.slice_in_dim(block, size - width, size, axis=axis), axis...  5.01 us
    all_to_all x1, waiting for transfers between devices, on_device(): lax.all_to_all(fc, 'member', split_axis=0, concat_axis=0, tiled=True)  4.95 us
    pallas_call x1, Pallas kernels, on_device(): pl.pallas_call(forward_kernel, out_shape=(jax.ShapeDtypeStruct((rows, cp,...  4.7 us
  transfers between devices with their start and end apart: 6, of which 4 were waited for; matrix products, arithmetic and copies ran while one was open for 8% of the time, Pallas kernels for 0%

profile of v5, /device:TPU:4, one launch (start us, length us, event | category | flops | bytes accessed | tf_op | source)
XLA Modules:
  0.0 73.8 jit_solution(46571809170091641)
XLA Ops:
  0.0 0.9 %pad_slice_fusion.1 = (bf16[3,48,24]{2,1,0:T(8,128)(2,1)S(1)}, bf16[3,48,24]{2,1,0:T(8,128)(2,1)S(1)}) fusion(bf16[3,45,720]{2,1,0:T(8,128)(2,1)} %bitcast.17), kind=kLoop, calls=%fused_computation.9 | loop fusion | bytes 208224 | tf_op jit(solution)/shard_map/slice | solution.py:27
  0.9 0.0 copy-done.2
  1.0 0.0 copy-start.11
  1.0 0.0 copy-start.13
  1.0 0.0 copy-start.12
  1.0 0.1 pad_maximum_fusion.own_ref
  1.1 0.0 copy-start.1
  1.1 0.0 copy-start.9
  1.2 3.5 %collective-permute-start.1 = (bf16[3,48,768]{2,1,0:T(8,128)(2,1)S(1)}, bf16[3,48,768]{2,1,0:T(8,128)(2,1)S(1)}, u32[]{:S(2)}, u32[]{:S(2)}) collective-permute-start(bf16[3,48,768]{2,1,0:T(8,128)(2,1)S(1)} %pad_maximum_fusion.own_ref), channel_id=1, source_target_pairs={{1,0},{2,1},{3,2},{5,4},{6,5},{7,6},{9,8},{10,9},{11,10},{13,12},{... | collective-permute-start | bytes 663560 | tf_op jit(solution)/shard_map/ppermute | solution.py:43
  4.6 2.5 %collective-permute-start = (bf16[3,48,768]{2,1,0:T(8,128)(2,1)S(1)}, bf16[3,48,768]{2,1,0:T(8,128)(2,1)S(1)}, u32[]{:S(2)}, u32[]{:S(2)}) collective-permute-start(bf16[3,48,768]{2,1,0:T(8,128)(2,1)S(1)} %pad_maximum_fusion.own_ref), channel_id=1, source_target_pairs={{0,1},{1,2},{2,3},{4,5},{5,6},{6,7},{8,9},{9,10},{10,11},{12,13},{... | collective-permute-start | bytes 663560 | tf_op jit(solution)/shard_map/ppermute | solution.py:42
  7.2 0.6 multiply_cosine_fusion.1.quad_ref
  7.7 0.0 copy-done.11
  7.8 0.0 copy-done.13
  7.8 0.7 reshape.37.basis_ref
  8.4 0.0 copy-done.12
  8.4 0.6 pad.48.proj_ref
  9.0 0.6 pad.38.sub_ref
  9.6 0.0 copy-done.9
  9.7 0.1 copy.17
  9.8 0.1 copy.18
  9.9 0.0 copy-done.1
  10.0 0.7 pad_maximum_fusion.1.table_ref
  10.7 0.0 collective-permute-done.1.next_ref
  10.7 4.1 %collective-permute-done.prev_ref = bf16[3,48,768]{2,1,0:T(8,128)(2,1)S(1)} collective-permute-done((bf16[3,48,768]{2,1,0:T(8,128)(2,1)S(1)}, bf16[3,48,768]{2,1,0:T(8,128)(2,1)S(1)}, u32[]{:S(2)}, u32[]{:S(2)}) %collective-permute-start) | collective-permute-done | bytes 221216 | tf_op jit(solution)/shard_map/ppermute | solution.py:42
  14.8 0.0 copy-done.7
  14.8 0.7 copy-done.8
  15.5 4.7 %shard_map.82 = (f32[3,48,768]{2,1,0:T(8,128)}, bf16[8,3,20,90]{3,2,1,0:T(8,128)(2,1)}) custom-call(s32[588]{0:T(1024)} %reshape.37.basis_ref, s32[12]{0:T(128)} %step_ref.3, f32[12]{0:T(128)} %multiply_cosine_fusion.1.quad_ref, bf16[3,48,768]{2,1,0:T(8,128)(2,1)} %copy-done.8, bf16[3,48,768]{2,1,0:T(8,128)(2,1)} %copy-done.1, ...), custom_call_target="tpu_custom_call" | custom-call | tf_op jit(solution)/shard_map/pallas_call | solution.py:270
  20.2 5.3 %all-to-all-start = ((bf16[8,3,20,90]{3,2,1,0:T(8,128)(2,1)}), bf16[8,3,20,90]{3,2,1,0:T(8,128)(2,1)S(1)}, u32[]{:S(2)}, u32[]{:S(2)}) async-start(bf16[8,3,20,90]{3,2,1,0:T(8,128)(2,1)} %get-tuple-element.7), calls=%async_computation | async-start | bytes 294912 | tf_op jit(solution)/shard_map/all_to_all | solution.py:280
  25.4 0.0 copy-done.14
  25.5 0.1 multiply_cosine_fusion
  25.6 0.6 reshape.48.weight_ref
  26.2 0.7 reshape.45.sub_ref
  26.9 0.6 copy.27
  27.5 5.0 %all-to-all-done.fc_ref = bf16[8,3,20,90]{3,2,1,0:T(8,128)(2,1)S(1)} async-done(((bf16[8,3,20,90]{3,2,1,0:T(8,128)(2,1)}), bf16[8,3,20,90]{3,2,1,0:T(8,128)(2,1)S(1)}, u32[]{:S(2)}, u32[]{:S(2)}) %all-to-all-start) | async-done | bytes 86432 | tf_op jit(solution)/shard_map/all_to_all | solution.py:280
  32.5 0.7 copy-done.3
  33.1 3.8 %shard_map.83 = bf16[8,4,3,16,90]{4,3,2,1,0:T(8,128)(2,1)} custom-call(f32[100]{0:T(128)} %reshape.45.sub_ref, f32[48]{0:T(128)} %reshape.48.weight_ref, bf16[8,3,20,90]{3,2,1,0:T(8,128)(2,1)} %copy-done.3, f32[3,20,90]{2,1,0:T(8,128)} %bitcast.20), custom_call_target="tpu_custom_call" | custom-call | tf_op jit(solution)/shard_map/pallas_call | solution.py:281
  36.9 4.0 %all-to-all-start.1 = ((bf16[32,3,16,90]{3,2,1,0:T(8,128)(2,1)}), bf16[32,3,16,90]{3,2,1,0:T(8,128)(2,1)S(1)}, u32[]{:S(2)}, u32[]{:S(2)}) async-start(bf16[32,3,16,90]{3,2,1,0:T(8,128)(2,1)} %bitcast.15), calls=%async_computation.1 | async-start | bytes 786432 | tf_op jit(solution)/shard_map/all_to_all | solution.py:287
  40.9 3.4 %collective-permute-start.3 = (f32[3,48,768]{2,1,0:T(8,128)S(1)}, f32[3,48,768]{2,1,0:T(8,128)S(1)}, u32[]{:S(2)}, u32[]{:S(2)}) collective-permute-start(f32[3,48,768]{2,1,0:T(8,128)S(1)} %copy-done.4), channel_id=1, source_target_pairs={{1,0},{2,1},{3,2},{5,4},{6,5},{7,6},{9,8},{10,9},{11,10},{13,12},{... | collective-permute-start | bytes 1327112 | tf_op jit(solution)/shard_map/ppermute | solution.py:43
  44.3 2.5 %collective-permute-start.2 = (f32[3,48,768]{2,1,0:T(8,128)S(1)}, f32[3,48,768]{2,1,0:T(8,128)S(1)}, u32[]{:S(2)}, u32[]{:S(2)}) collective-permute-start(f32[3,48,768]{2,1,0:T(8,128)S(1)} %copy-done.4), channel_id=1, source_target_pairs={{0,1},{1,2},{2,3},{4,5},{5,6},{6,7},{8,9},{9,10},{10,11},{12,13},{... | collective-permute-start | bytes 1327112 | tf_op jit(solution)/shard_map/ppermute | solution.py:42
  46.8 0.1 copy.23
  46.9 0.6 pad.49.proj_t_ref
  47.5 10.0 %collective-permute-done.3.sl_next_ref = f32[3,48,768]{2,1,0:T(8,128)S(1)} collective-permute-done((f32[3,48,768]{2,1,0:T(8,128)S(1)}, f32[3,48,768]{2,1,0:T(8,128)S(1)}, u32[]{:S(2)}, u32[]{:S(2)}) %collective-permute-start.3) | collective-permute-done | bytes 442400 | tf_op jit(solution)/shard_map/ppermute | solution.py:43
  57.6 9.4 %collective-permute-done.2.sl_prev_ref = f32[3,48,768]{2,1,0:T(8,128)S(1)} collective-permute-done((f32[3,48,768]{2,1,0:T(8,128)S(1)}, f32[3,48,768]{2,1,0:T(8,128)S(1)}, u32[]{:S(2)}, u32[]{:S(2)}) %collective-permute-start.2) | collective-permute-done | bytes 442400 | tf_op jit(solution)/shard_map/ppermute | solution.py:42
  67.0 0.0 all-to-all-done.1
  67.0 0.0 copy-done.5
  67.0 0.8 %copy-done.6 = f32[3,48,768]{2,1,0:T(8,128)} copy-done((f32[3,48,768]{2,1,0:T(8,128)}, f32[3,48,768]{2,1,0:T(8,128)S(1)}, u32[]{:S(2)}) %copy-start.6) | copy-done | bytes 442392
  67.8 0.1 copy-done
  67.9 5.9 %shard_map.84 = bf16[3,45,720]{2,1,0:T(8,128)(2,1)} custom-call(s32[588]{0:T(1024)} %reshape.37.basis_ref, s32[12]{0:T(128)} %step_ref.3, f32[12]{0:T(128)} %multiply_cosine_fusion.1.quad_ref, bf16[8,4,3,16,90]{4,3,2,1,0:T(8,128)(2,1)} %bitcast.16, f32[3,48,768]{2,1,0:T(8,128)} %copy-done.6, f32[3,48,768]{2,1,0:T(8,128)} %get-tuple-element.8.sl_own_ref, ...), custom_call_target="tpu_custom_call" | custom-call | tf_op jit(solution)/shard_map/pallas_call | solution.py:293
  (19 shorter events, 0.1 us)
Async XLA Ops:
  0.0 1.0 %copy-start.2 = (bf16[1,3,45,720]{3,2,1,0:T(8,128)(2,1)S(1)}, bf16[1,3,45,720]{3,2,1,0:T(8,128)(2,1)}, u32[]{:S(2)}) copy-start(bf16[1,3,45,720]{3,2,1,0:T(8,128)(2,1)} %param.8) | copy-start | bytes 583204
  1.0 6.7 %copy-start.11 = (bf16[4,5,5]{2,0,1:T(4,128)(2,1)S(1)}, bf16[4,5,5]{2,0,1:T(4,128)(2,1)}, u32[]{:S(2)}) copy-start(bf16[4,5,5]{2,0,1:T(4,128)(2,1)} %param.11) | copy-start | bytes 604
  1.0 6.7 %copy-start.13 = (s32[12,49]{1,0:T(8,128)S(1)}, s32[12,49]{1,0:T(8,128)}, u32[]{:S(2)}) copy-start(s32[12,49]{1,0:T(8,128)} %param.13) | copy-start | bytes 7060
  1.0 7.4 %copy-start.12 = (bf16[5,45]{1,0:T(8,128)(2,1)S(1)}, bf16[5,45]{1,0:T(8,128)(2,1)}, u32[]{:S(2)}) copy-start(bf16[5,45]{1,0:T(8,128)(2,1)} %param.10) | copy-start | bytes 1354
  1.1 8.8 %copy-start.1 = (bf16[3,48,768]{2,1,0:T(8,128)(2,1)}, bf16[3,48,768]{2,1,0:T(8,128)(2,1)S(1)}, u32[]{:S(2)}) copy-start(bf16[3,48,768]{2,1,0:T(8,128)(2,1)S(1)} %pad_maximum_fusion.own_ref) | copy-start | bytes 663556
  1.1 8.5 %copy-start.9 = (bf16[5,45,45]{2,1,0:T(8,128)(2,1)S(1)}, bf16[5,45,45]{2,1,0:T(8,128)(2,1)}, u32[]{:S(2)}) copy-start(bf16[5,45,45]{2,1,0:T(8,128)(2,1)} %param.9) | copy-start | bytes 60754
  1.2 9.5 %collective-permute-start.1 = (bf16[3,48,768]{2,1,0:T(8,128)(2,1)S(1)}, bf16[3,48,768]{2,1,0:T(8,128)(2,1)S(1)}, u32[]{:S(2)}, u32[]{:S(2)}) collective-permute-start(bf16[3,48,768]{2,1,0:T(8,128)(2,1)S(1)} %pad_maximum_fusion.own_ref), channel_id=1, source_target_pairs={{1,0},{2,1},{3,2},{5,4},{6,5},{7,6},{9,8},{10,9},{11,10},{13,12},{... | collective-permute-start | bytes 663560 | tf_op jit(solution)/shard_map/ppermute | solution.py:43
  4.6 10.2 %collective-permute-start = (bf16[3,48,768]{2,1,0:T(8,128)(2,1)S(1)}, bf16[3,48,768]{2,1,0:T(8,128)(2,1)S(1)}, u32[]{:S(2)}, u32[]{:S(2)}) collective-permute-start(bf16[3,48,768]{2,1,0:T(8,128)(2,1)S(1)} %pad_maximum_fusion.own_ref), channel_id=1, source_target_pairs={{0,1},{1,2},{2,3},{4,5},{5,6},{6,7},{8,9},{9,10},{10,11},{12,13},{... | collective-permute-start | bytes 663560 | tf_op jit(solution)/shard_map/ppermute | solution.py:42
  10.7 4.1 %copy-start.7 = (bf16[3,48,768]{2,1,0:T(8,128)(2,1)}, bf16[3,48,768]{2,1,0:T(8,128)(2,1)S(1)}, u32[]{:S(2)}) copy-start(bf16[3,48,768]{2,1,0:T(8,128)(2,1)S(1)} %collective-permute-done.1.next_ref) | copy-start | bytes 663556
  14.8 0.7 copy-start.8
  20.2 5.3 %copy-start.14 = (f32[4]{0:T(128)S(1)}, f32[4]{0:T(128)}, u32[]{:S(2)}) copy-start(f32[4]{0:T(128)} %constant.23.clone) | copy-start | bytes 52
  20.2 6.7 %copy-start.10 = (f32[4,5,3,90]{3,0,2,1:T(4,128)S(1)}, f32[4,5,3,90]{3,0,2,1:T(4,128)}, u32[]{:S(2)}) copy-start(f32[4,5,3,90]{3,0,2,1:T(4,128)} %param.12) | copy-start | bytes 64804
  20.2 12.3 %all-to-all-start = ((bf16[8,3,20,90]{3,2,1,0:T(8,128)(2,1)}), bf16[8,3,20,90]{3,2,1,0:T(8,128)(2,1)S(1)}, u32[]{:S(2)}, u32[]{:S(2)}) async-start(bf16[8,3,20,90]{3,2,1,0:T(8,128)(2,1)} %get-tuple-element.7), calls=%async_computation | async-start | bytes 294912 | tf_op jit(solution)/shard_map/all_to_all | solution.py:280
  32.4 0.7 copy-start.3
  36.9 4.1 %copy-start.4 = (f32[3,48,768]{2,1,0:T(8,128)S(1)}, f32[3,48,768]{2,1,0:T(8,128)}, u32[]{:S(2)}) copy-start(f32[3,48,768]{2,1,0:T(8,128)} %get-tuple-element.8.sl_own_ref) | copy-start | bytes 1327108
  36.9 30.1 %all-to-all-start.1 = ((bf16[32,3,16,90]{3,2,1,0:T(8,128)(2,1)}), bf16[32,3,16,90]{3,2,1,0:T(8,128)(2,1)S(1)}, u32[]{:S(2)}, u32[]{:S(2)}) async-start(bf16[32,3,16,90]{3,2,1,0:T(8,128)(2,1)} %bitcast.15), calls=%async_computation.1 | async-start | bytes 786432 | tf_op jit(solution)/shard_map/all_to_all | solution.py:287
  40.9 16.6 %collective-permute-start.3 = (f32[3,48,768]{2,1,0:T(8,128)S(1)}, f32[3,48,768]{2,1,0:T(8,128)S(1)}, u32[]{:S(2)}, u32[]{:S(2)}) collective-permute-start(f32[3,48,768]{2,1,0:T(8,128)S(1)} %copy-done.4), channel_id=1, source_target_pairs={{1,0},{2,1},{3,2},{5,4},{6,5},{7,6},{9,8},{10,9},{11,10},{13,12},{... | collective-permute-start | bytes 1327112 | tf_op jit(solution)/shard_map/ppermute | solution.py:43
  44.3 22.7 %collective-permute-start.2 = (f32[3,48,768]{2,1,0:T(8,128)S(1)}, f32[3,48,768]{2,1,0:T(8,128)S(1)}, u32[]{:S(2)}, u32[]{:S(2)}) collective-permute-start(f32[3,48,768]{2,1,0:T(8,128)S(1)} %copy-done.4), channel_id=1, source_target_pairs={{0,1},{1,2},{2,3},{4,5},{5,6},{6,7},{8,9},{9,10},{10,11},{12,13},{... | collective-permute-start | bytes 1327112 | tf_op jit(solution)/shard_map/ppermute | solution.py:42
  57.6 9.4 %copy-start.5 = (f32[3,48,768]{2,1,0:T(8,128)}, f32[3,48,768]{2,1,0:T(8,128)S(1)}, u32[]{:S(2)}) copy-start(f32[3,48,768]{2,1,0:T(8,128)S(1)} %collective-permute-done.3.sl_next_ref) | copy-start | bytes 1327108
  67.0 0.8 %copy-start.6 = (f32[3,48,768]{2,1,0:T(8,128)}, f32[3,48,768]{2,1,0:T(8,128)S(1)}, u32[]{:S(2)}) copy-start(f32[3,48,768]{2,1,0:T(8,128)S(1)} %collective-permute-done.2.sl_prev_ref) | copy-start | bytes 1327108
  67.0 0.9 %copy-start = (bf16[32,3,16,90]{3,2,1,0:T(8,128)(2,1)}, bf16[32,3,16,90]{3,2,1,0:T(8,128)(2,1)S(1)}, u32[]{:S(2)}) copy-start(bf16[32,3,16,90]{3,2,1,0:T(8,128)(2,1)S(1)} %all-to-all-done.1) | copy-start | bytes 829444

commit v6 on v3

--- a/solution.py
+++ b/solution.py
@@ -1,3 +1,5 @@
+import functools
+
 import jax
 import jax.numpy as jnp
 from jax import lax
@@ -74,8 +76,16 @@
     return 0.5 * (1.0 + t) + x * (0.5 * (1.0 - t * t)) * d_inner
 
 
+def gelu_and_grad(x):
+    inner = SQRT_2_OVER_PI * (x + 0.044715 * (x * x * x))
+    t = jnp.tanh(inner)
+    d_inner = SQRT_2_OVER_PI * (1.0 + 3.0 * 0.044715 * (x * x))
+    half = 0.5 * (1.0 + t)
+    return x * half, half + x * (0.5 * (1.0 - t * t)) * d_inner
+
+
 def forward_kernel(basis_ref, step_ref, quad_ref, prev_ref, own_ref, next_ref, table_ref,
-                   proj_ref, sub_ref, filt_ref, fc_ref):
+                   proj_ref, sub_ref, slope_ref, fc_ref):
     rows, cp, width_p = own_ref.shape
     first = lax.axis_index("lat") * rows
     ext = (
@@ -105,8 +115,9 @@
             shift = lax.rem((HALF - b) * step + width_p, width_p)
             total = total + pltpu.roll(taps[b * cp : (b + 1) * cp], shift, 1)
         filtered = total * quad_ref[g]
-        filt_ref[i] = filtered
-        activated = gelu(filtered).astype(jnp.bfloat16)
+        gelu_value, gelu_slope = gelu_and_grad(filtered)
+        slope_ref[i] = gelu_slope
+        activated = gelu_value.astype(jnp.bfloat16)
         coarse = jnp.dot(
             proj_ref[...], activated, preferred_element_type=jnp.float32
         ).astype(jnp.bfloat16)
@@ -118,45 +129,58 @@
             fc_ref[q, i] = forecast[:, q * block : (q + 1) * block]
 
 
-def score_kernel(sub_ref, weight_ref, fc_ref, truth_ref, out_ref):
+def split3(x):
+    hi = x.astype(jnp.bfloat16)
+    rest = x - hi.astype(jnp.float32)
+    mid = rest.astype(jnp.bfloat16)
+    lo = (rest - mid.astype(jnp.float32)).astype(jnp.bfloat16)
+    return hi, mid, lo
+
+
+def score_kernel(subcells, weight_ref, sub_t_ref, fc_ref, truth_ref, out_ref):
     members, rows, cells, block = fc_ref.shape
-    vp = out_ref.shape[2]
-    variables = sub_ref.shape[0] // cells
-    subcells = cells // variables
     total_rows = weight_ref.shape[0] // subcells
+    slot = 128
+    lanes = members * slot
     first = lax.axis_index("lat") * rows
+    variables = cells // subcells
     cell_sub = lax.broadcasted_iota(jnp.int32, (cells, 1), 0) // variables
+    pad = jnp.zeros((cells, slot - block), jnp.float32)
     for i in range(rows):
         g = first + i
         scale = jnp.zeros((cells, 1), jnp.float32)
         for s in range(subcells):
             scale = jnp.where(cell_sub == s, weight_ref[s * total_rows + g], scale)
-        truth = truth_ref[i]
-        values = [fc_ref[n, i].astype(jnp.float32) for n in range(members)]
-        spread = [jnp.zeros((cells, block), jnp.float32) for _ in range(members)]
+        values = jnp.concatenate(
+            [
+                jnp.concatenate([fc_ref[n, i].astype(jnp.float32), pad], axis=1)
+                for n in range(members)
+            ],
+            axis=1,
+        )
+        truth_slot = jnp.concatenate([truth_ref[i], pad], axis=1)
+        truth = jnp.concatenate([truth_slot] * members, axis=1)
+        spread = jnp.zeros((cells, lanes), jnp.float32)
+        for k in range(1, (members + 1) // 2):
+            term = softened_sign(values - pltpu.roll(values, k * slot, 1))
+            spread = spread + term - pltpu.roll(term, lanes - k * slot, 1)
+        if members % 2 == 0:
+            spread = spread + softened_sign(
+                values - pltpu.roll(values, (members // 2) * slot, 1)
+            )
+        grad = scale * (softened_sign(values - truth) - spread / members)
+        coarse = None
+        for part in split3(grad):
+            term = jnp.dot(sub_t_ref[...], part, preferred_element_type=jnp.float32)
+            coarse = term if coarse is None else coarse + term
+        coarse = coarse.astype(out_ref.dtype)
         for m in range(members):
-            for n in range(m + 1, members):
-                term = softened_sign(values[m] - values[n])
-                spread[m] = spread[m] + term
-                spread[n] = spread[n] - term
-        for m in range(members):
-            grad = scale * (softened_sign(values[m] - truth) - spread[m] / members)
-            coarse = []
-            for u in range(vp):
-                if u >= variables:
-                    coarse.append(jnp.zeros((1, block), jnp.float32))
-                    continue
-                acc = None
-                for r in range(cells):
-                    term = sub_ref[r * variables + u] * grad[r : r + 1]
-                    acc = term if acc is None else acc + term
-                coarse.append(acc)
-            out_ref[m, i] = jnp.concatenate(coarse, axis=0).astype(out_ref.dtype)
-
-
-def grad_filtered_kernel(gc_ref, filt_ref, proj_t_ref, out_ref):
+            out_ref[m, i] = coarse[:, m * slot : m * slot + block]
+
+
+def grad_filtered_kernel(gc_ref, slope_ref, proj_t_ref, out_ref):
     blocks, rows = gc_ref.shape[0], gc_ref.shape[1]
-    width_p = filt_ref.shape[2]
+    width_p = slope_ref.shape[2]
     for i in range(rows):
         row = jnp.concatenate([gc_ref[q, i] for q in range(blocks)], axis=1)
         width = row.shape[1]
@@ -165,7 +189,7 @@
         hi = extra - lo
         ring = jnp.concatenate([row, row[:, :lo], row[:, width - hi :]], axis=1)
         grad_act = jnp.dot(proj_t_ref[...], ring, preferred_element_type=jnp.float32)
-        out_ref[i] = (grad_act * gelu_grad(filt_ref[i])).astype(jnp.bfloat16)
+        out_ref[i] = (grad_act * slope_ref[i]).astype(jnp.bfloat16)
 
 
 def backward_kernel(basis_ref, step_ref, quad_ref, prev_ref, own_ref, next_ref, table_ref,
@@ -239,7 +263,7 @@
 
     quad_all = latitude_rows(total_rows, total_rows)
     weight_all = subcell_weight(0, total_rows, total_rows).reshape(-1)
-    sub_flat = subcell_maps.astype(jnp.float32).reshape(-1)
+    sub_t = pad_axis(subcell_maps.reshape(subcells * variables, variables).T, 0, vp)
     blocks = lax.axis_size("member")
     block = width // blocks
     truth = verifying_truth.reshape(subcells * variables, rows, block).transpose(1, 0, 2)
@@ -255,7 +279,7 @@
     own = to_ring(pad_axis(latents[0], 1, cp), width_p)
     low, high = halo(own, "lat", HALF)
 
-    filtered, fc = pl.pallas_call(
+    slope, fc = pl.pallas_call(
         forward_kernel,
         out_shape=(
             jax.ShapeDtypeStruct((rows, cp, width_p), jnp.float32),
@@ -267,11 +291,11 @@
 
     fc_owned = lax.all_to_all(fc, "member", split_axis=0, concat_axis=0, tiled=True)
     gc_owned = pl.pallas_call(
-        score_kernel,
+        functools.partial(score_kernel, subcells),
         out_shape=jax.ShapeDtypeStruct((blocks, rows, vp, block), jnp.bfloat16),
-        in_specs=[smem(), smem()] + [vmem()] * 2,
+        in_specs=[smem()] + [vmem()] * 3,
         out_specs=vmem(),
-    )(sub_flat, weight_all, fc_owned, truth)
+    )(weight_all, sub_t, fc_owned, truth)
     gc_home = lax.all_to_all(gc_owned, "member", split_axis=0, concat_axis=0, tiled=True)
     proj_t = pad_axis(pad_axis(project.T, 0, cp), 1, vp)
     grad_filtered = pl.pallas_call(
@@ -279,7 +303,7 @@
         out_shape=jax.ShapeDtypeStruct((rows, cp, width_p), jnp.bfloat16),
         in_specs=[vmem()] * 3,
         out_specs=vmem(),
-    )(gc_home, filtered, proj_t)
+    )(gc_home, slope, proj_t)
 
     g_low, g_high = halo(grad_filtered, "lat", HALF)
     result = pl.pallas_call(

time: 70 us -> 69 us (0.986)
  Pallas kernels: 14.2 us -> 13.2 us
    pallas_call x1, Pallas kernels: 3.56 us -> 2.6 us  [on_device(): pl.pallas_call(functools.partial(score_kernel, subcells), out_shape=jax.S...]
    pad x4 -> x5, local copies, waits for them, and re-layouts: 1.83 us -> 2.43 us  [pad_axis(): return jnp.pad(block, pads)]
    unnamed x31 -> x32, local copies, waits for them, and re-layouts: 3.7 us -> 3.73 us
  transfers between devices with their start and end apart: 6 -> 6, of which waited for: 5 -> 5; matrix products, arithmetic and copies ran while one was open for 9% -> 10% of each run, Pallas kernels for 0% -> 0%
where the time goes in v6:
time: 69 us; the launch traced here: 68.5 us
  waiting for transfers between devices  25 us (36%)
  starting transfers between devices  19.2 us (28%)
  Pallas kernels  13.2 us (19%)
  local copies, waits for them, and re-layouts  9.4 us (14%)
  other arithmetic  1.53 us (2%)
    ppermute x2, waiting for transfers between devices, halo(): high = lax.ppermute(block[:width], axis_name, backward)  9.77 us
    ppermute x2, starting transfers between devices, halo(): low = lax.ppermute(block[block.shape[0] - width:], axis_name, forward)  8.25 us
    all_to_all x1, waiting for transfers between devices, on_device(): lax.all_to_all(fc, 'member', split_axis=0, concat_axis=0, tiled=True)  6.2 us
    all_to_all x1, waiting for transfers between devices, on_device(): lax.all_to_all(gc_owned, 'member', split_axis=0, concat_axis=0, tiled=True)  5.54 us
    all_to_all x1, starting transfers between devices, on_device(): lax.all_to_all(fc, 'member', split_axis=0, concat_axis=0, tiled=True)  5.01 us
    pallas_call x1, Pallas kernels, on_device(): pl.pallas_call(forward_kernel, out_shape=(jax.ShapeDtypeStruct((rows, cp,...  4.71 us
    pallas_call x1, Pallas kernels, on_device(): pl.pallas_call(backward_kernel, out_shape=jax.ShapeDtypeStruct((rows, cha...  3.84 us
    unnamed x32, local copies, waits for them, and re-layouts  3.73 us
  transfers between devices with their start and end apart: 6, of which 5 were waited for; matrix products, arithmetic and copies ran while one was open for 10% of the time, Pallas kernels for 0%

profile of v6, /device:TPU:0, one launch (start us, length us, event | category | flops | bytes accessed | tf_op | source)
XLA Modules:
  0.0 68.5 jit_solution(2738340684225380850)
XLA Ops:
  0.0 0.9 %pad_slice_fusion.1 = (bf16[3,48,24]{2,1,0:T(8,128)(2,1)S(1)}, bf16[3,48,24]{2,1,0:T(8,128)(2,1)S(1)}) fusion(bf16[3,45,720]{2,1,0:T(8,128)(2,1)} %bitcast.16), kind=kLoop, calls=%fused_computation.9 | loop fusion | bytes 208224 | tf_op jit(solution)/shard_map/slice | solution.py:29
  0.9 0.0 copy-done.1
  1.0 0.0 copy-start.8
  1.0 0.1 pad_maximum_fusion.own_ref
  1.1 4.9 %collective-permute-start = (bf16[3,48,768]{2,1,0:T(8,128)(2,1)S(1)}, bf16[3,48,768]{2,1,0:T(8,128)(2,1)S(1)}, u32[]{:S(2)}, u32[]{:S(2)}) collective-permute-start(bf16[3,48,768]{2,1,0:T(8,128)(2,1)S(1)} %pad_maximum_fusion.own_ref), channel_id=1, source_target_pairs={{0,1},{1,2},{2,3},{4,5},{5,6},{6,7},{8,9},{9,10},{10,11},{12,13},{... | collective-permute-start | bytes 663560 | tf_op jit(solution)/shard_map/ppermute | solution.py:43
  6.0 1.3 %collective-permute-start.1 = (bf16[3,48,768]{2,1,0:T(8,128)(2,1)S(1)}, bf16[3,48,768]{2,1,0:T(8,128)(2,1)S(1)}, u32[]{:S(2)}, u32[]{:S(2)}) collective-permute-start(bf16[3,48,768]{2,1,0:T(8,128)(2,1)S(1)} %pad_maximum_fusion.own_ref), channel_id=1, source_target_pairs={{1,0},{2,1},{3,2},{5,4},{6,5},{7,6},{9,8},{10,9},{11,10},{13,12},{... | collective-permute-start | bytes 663560 | tf_op jit(solution)/shard_map/ppermute | solution.py:44
  7.3 0.6 multiply_cosine_fusion.1.quad_ref
  7.9 0.0 copy-done.8
  7.9 0.1 copy.16
  8.1 0.0 copy-start.12
  8.1 0.0 copy-start.11
  8.1 0.1 copy.17
  8.2 0.5 copy-done.12
  8.8 0.1 copy.15
  8.9 0.1 reshape.28
  9.0 0.1 copy.18
  9.1 0.6 pad.43.sub_ref
  9.7 0.0 copy-done.11
  9.7 0.7 reshape.27.basis_ref
  10.4 0.0 copy-done.10
  10.4 0.6 pad.53.proj_ref
  11.0 0.6 pad.37.sub_t_ref
  11.6 0.0 copy-done.9
  11.6 0.6 copy.23
  12.2 0.7 %pad_maximum_fusion.1.table_ref = bf16[2,6,48,48]{3,2,1,0:T(8,128)(2,1)} fusion(bf16[1,6,48,48]{3,2,1,0:T(8,128)(2,1)S(1)} %get-tuple-element.12, bf16[1,6,48,48]{3,2,1,0:T(8,128)(2,1)S(1)} %copy.17), kind=kLoop, calls=%fused_computation.1 | loop fusion | flops 27648 | bytes 110592 | tf_op jit(solution)/shard_map/stack | solution.py:273
  12.9 0.0 collective-permute-done.prev_ref
  12.9 4.4 %collective-permute-done.1.next_ref = bf16[3,48,768]{2,1,0:T(8,128)(2,1)S(1)} collective-permute-done((bf16[3,48,768]{2,1,0:T(8,128)(2,1)S(1)}, bf16[3,48,768]{2,1,0:T(8,128)(2,1)S(1)}, u32[]{:S(2)}, u32[]{:S(2)}) %collective-permute-start.1) | collective-permute-done | bytes 221216 | tf_op jit(solution)/shard_map/ppermute | solution.py:44
  17.3 0.0 copy-done.4
  17.3 0.7 %copy-done.5 = bf16[3,48,768]{2,1,0:T(8,128)(2,1)} copy-done((bf16[3,48,768]{2,1,0:T(8,128)(2,1)}, bf16[3,48,768]{2,1,0:T(8,128)(2,1)S(1)}, u32[]{:S(2)}) %copy-start.5) | copy-done | bytes 221208
  18.0 4.7 %shard_map.82 = (f32[3,48,768]{2,1,0:T(8,128)}, bf16[8,3,20,90]{3,2,1,0:T(8,128)(2,1)}) custom-call(s32[588]{0:T(1024)} %reshape.27.basis_ref, s32[12]{0:T(128)} %step_ref.3, f32[12]{0:T(128)} %multiply_cosine_fusion.1.quad_ref, bf16[3,48,768]{2,1,0:T(8,128)(2,1)} %copy-done.4, bf16[3,48,768]{2,1,0:T(8,128)(2,1)} %copy-done, bf16[3,48,768]{2,1,0:T(8,128)(2,1)} %copy-done.5, ...), custom_call_target="tpu_custom_call" | custom-call | tf_op jit(solution)/shard_map/pallas_call | solution.py:282
  22.7 5.0 %all-to-all-start = ((bf16[8,3,20,90]{3,2,1,0:T(8,128)(2,1)}), bf16[8,3,20,90]{3,2,1,0:T(8,128)(2,1)S(1)}, u32[]{:S(2)}, u32[]{:S(2)}) async-start(bf16[8,3,20,90]{3,2,1,0:T(8,128)(2,1)} %get-tuple-element.7), calls=%async_computation | async-start | bytes 294912 | tf_op jit(solution)/shard_map/all_to_all | solution.py:292
  27.8 0.1 multiply_cosine_fusion
  27.9 0.7 reshape.32.weight_ref
  28.6 6.2 %all-to-all-done.fc_ref = bf16[8,3,20,90]{3,2,1,0:T(8,128)(2,1)S(1)} async-done(((bf16[8,3,20,90]{3,2,1,0:T(8,128)(2,1)}), bf16[8,3,20,90]{3,2,1,0:T(8,128)(2,1)S(1)}, u32[]{:S(2)}, u32[]{:S(2)}) %all-to-all-start) | async-done | bytes 86432 | tf_op jit(solution)/shard_map/all_to_all | solution.py:292
  34.8 0.7 copy-done.2
  35.4 2.6 %shard_map.83 = bf16[8,3,16,90]{3,2,1,0:T(8,128)(2,1)} custom-call(f32[48]{0:T(128)} %reshape.32.weight_ref, bf16[16,20]{1,0:T(8,128)(2,1)} %pad.37.sub_t_ref, bf16[8,3,20,90]{3,2,1,0:T(8,128)(2,1)} %copy-done.2, f32[3,20,90]{2,1,0:T(8,128)} %bitcast.19), custom_call_target="tpu_custom_call" | custom-call | tf_op jit(solution)/shard_map/pallas_call | solution.py:293
  38.0 3.4 %all-to-all-start.1 = ((bf16[8,3,16,90]{3,2,1,0:T(8,128)(2,1)}), bf16[8,3,16,90]{3,2,1,0:T(8,128)(2,1)S(1)}, u32[]{:S(2)}, u32[]{:S(2)}) async-start(bf16[8,3,16,90]{3,2,1,0:T(8,128)(2,1)} %shard_map.83), calls=%async_computation.1 | async-start | bytes 196608 | tf_op jit(solution)/shard_map/all_to_all | solution.py:299
  41.4 0.1 copy.21
  41.5 0.6 pad.54.proj_t_ref
  42.1 5.5 %all-to-all-done.1.gc_ref = bf16[8,3,16,90]{3,2,1,0:T(8,128)(2,1)S(1)} async-done(((bf16[8,3,16,90]{3,2,1,0:T(8,128)(2,1)}), bf16[8,3,16,90]{3,2,1,0:T(8,128)(2,1)S(1)}, u32[]{:S(2)}, u32[]{:S(2)}) %all-to-all-start.1) | async-done | bytes 69152 | tf_op jit(solution)/shard_map/all_to_all | solution.py:299
  47.7 0.6 copy-done.3
  48.3 2.1 %shard_map.84.own_ref = bf16[3,48,768]{2,1,0:T(8,128)(2,1)} custom-call(bf16[8,3,16,90]{3,2,1,0:T(8,128)(2,1)} %copy-done.3, f32[3,48,768]{2,1,0:T(8,128)} %get-tuple-element.8.slope_ref, bf16[48,16]{1,0:T(8,128)(2,1)} %pad.54.proj_t_ref), custom_call_target="tpu_custom_call" | custom-call | tf_op jit(solution)/shard_map/pallas_call | solution.py:301
  50.4 3.4 %collective-permute-start.2 = (bf16[3,48,768]{2,1,0:T(8,128)(2,1)}, bf16[3,48,768]{2,1,0:T(8,128)(2,1)S(1)}, u32[]{:S(2)}, u32[]{:S(2)}) collective-permute-start(bf16[3,48,768]{2,1,0:T(8,128)(2,1)} %shard_map.84.own_ref), channel_id=1, source_target_pairs={{0,1},{1,2},{2,3},{4,5},{5,6},{6,7},{8,9},{9,10},{10,11},{12,13},{... | collective-permute-start | bytes 663560 | tf_op jit(solution)/shard_map/ppermute | solution.py:43
  53.8 1.3 %collective-permute-start.3 = (bf16[3,48,768]{2,1,0:T(8,128)(2,1)}, bf16[3,48,768]{2,1,0:T(8,128)(2,1)S(1)}, u32[]{:S(2)}, u32[]{:S(2)}) collective-permute-start(bf16[3,48,768]{2,1,0:T(8,128)(2,1)} %shard_map.84.own_ref), channel_id=1, source_target_pairs={{1,0},{2,1},{3,2},{5,4},{6,5},{7,6},{9,8},{10,9},{11,10},{13,12},{... | collective-permute-start | bytes 663560 | tf_op jit(solution)/shard_map/ppermute | solution.py:44
  55.1 3.5 %collective-permute-done.2.prev_ref = bf16[3,48,768]{2,1,0:T(8,128)(2,1)S(1)} collective-permute-done((bf16[3,48,768]{2,1,0:T(8,128)(2,1)}, bf16[3,48,768]{2,1,0:T(8,128)(2,1)S(1)}, u32[]{:S(2)}, u32[]{:S(2)}) %collective-permute-start.2) | collective-permute-done | bytes 221216 | tf_op jit(solution)/shard_map/ppermute | solution.py:43
  58.5 5.4 %collective-permute-done.3.next_ref = bf16[3,48,768]{2,1,0:T(8,128)(2,1)S(1)} collective-permute-done((bf16[3,48,768]{2,1,0:T(8,128)(2,1)}, bf16[3,48,768]{2,1,0:T(8,128)(2,1)S(1)}, u32[]{:S(2)}, u32[]{:S(2)}) %collective-permute-start.3) | collective-permute-done | bytes 221216 | tf_op jit(solution)/shard_map/ppermute | solution.py:44
  63.9 0.7 %copy-done.7 = bf16[3,48,768]{2,1,0:T(8,128)(2,1)} copy-done((bf16[3,48,768]{2,1,0:T(8,128)(2,1)}, bf16[3,48,768]{2,1,0:T(8,128)(2,1)S(1)}, u32[]{:S(2)}) %copy-start.7) | copy-done | bytes 221208
  64.6 3.8 %shard_map.85 = bf16[3,45,720]{2,1,0:T(8,128)(2,1)} custom-call(s32[588]{0:T(1024)} %reshape.27.basis_ref, s32[12]{0:T(128)} %step_ref.3, f32[12]{0:T(128)} %multiply_cosine_fusion.1.quad_ref, bf16[3,48,768]{2,1,0:T(8,128)(2,1)} %copy-done.6, bf16[3,48,768]{2,1,0:T(8,128)(2,1)} %shard_map.84.own_ref, bf16[3,48,768]{2,1,0:T(8,128)(2,1)} %copy-done.7, ...), custom_call_target="tpu_custom_call" | custom-call | tf_op jit(solution)/shard_map/pallas_call | solution.py:309
  (18 shorter events, 0.1 us)
Async XLA Ops:
  0.0 1.0 %copy-start.1 = (bf16[1,3,45,720]{3,2,1,0:T(8,128)(2,1)S(1)}, bf16[1,3,45,720]{3,2,1,0:T(8,128)(2,1)}, u32[]{:S(2)}) copy-start(bf16[1,3,45,720]{3,2,1,0:T(8,128)(2,1)} %param.8) | copy-start | bytes 583204
  1.0 6.9 %copy-start.8 = (bf16[5,45,45]{2,1,0:T(8,128)(2,1)S(1)}, bf16[5,45,45]{2,1,0:T(8,128)(2,1)}, u32[]{:S(2)}) copy-start(bf16[5,45,45]{2,1,0:T(8,128)(2,1)} %param.9) | copy-start | bytes 60754
  1.1 7.1 %copy-start = (bf16[3,48,768]{2,1,0:T(8,128)(2,1)}, bf16[3,48,768]{2,1,0:T(8,128)(2,1)S(1)}, u32[]{:S(2)}) copy-start(bf16[3,48,768]{2,1,0:T(8,128)(2,1)S(1)} %pad_maximum_fusion.own_ref) | copy-start | bytes 663556
  1.1 11.8 %collective-permute-start = (bf16[3,48,768]{2,1,0:T(8,128)(2,1)S(1)}, bf16[3,48,768]{2,1,0:T(8,128)(2,1)S(1)}, u32[]{:S(2)}, u32[]{:S(2)}) collective-permute-start(bf16[3,48,768]{2,1,0:T(8,128)(2,1)S(1)} %pad_maximum_fusion.own_ref), channel_id=1, source_target_pairs={{0,1},{1,2},{2,3},{4,5},{5,6},{6,7},{8,9},{9,10},{10,11},{12,13},{... | collective-permute-start | bytes 663560 | tf_op jit(solution)/shard_map/ppermute | solution.py:43
  6.0 11.3 %collective-permute-start.1 = (bf16[3,48,768]{2,1,0:T(8,128)(2,1)S(1)}, bf16[3,48,768]{2,1,0:T(8,128)(2,1)S(1)}, u32[]{:S(2)}, u32[]{:S(2)}) collective-permute-start(bf16[3,48,768]{2,1,0:T(8,128)(2,1)S(1)} %pad_maximum_fusion.own_ref), channel_id=1, source_target_pairs={{1,0},{2,1},{3,2},{5,4},{6,5},{7,6},{9,8},{10,9},{11,10},{13,12},{... | collective-permute-start | bytes 663560 | tf_op jit(solution)/shard_map/ppermute | solution.py:44
  8.1 0.7 %copy-start.12 = (bf16[4,5,5]{2,0,1:T(4,128)(2,1)S(1)}, bf16[4,5,5]{2,0,1:T(4,128)(2,1)}, u32[]{:S(2)}) copy-start(bf16[4,5,5]{2,0,1:T(4,128)(2,1)} %param.11) | copy-start | bytes 604
  8.1 1.6 %copy-start.11 = (s32[12,49]{1,0:T(8,128)S(1)}, s32[12,49]{1,0:T(8,128)}, u32[]{:S(2)}) copy-start(s32[12,49]{1,0:T(8,128)} %param.13) | copy-start | bytes 7060
  8.8 2.8 %copy-start.9 = (f32[4,5,3,90]{3,0,2,1:T(4,128)S(1)}, f32[4,5,3,90]{3,0,2,1:T(4,128)}, u32[]{:S(2)}) copy-start(f32[4,5,3,90]{3,0,2,1:T(4,128)} %param.12) | copy-start | bytes 64804
  9.7 0.7 copy-start.10
  12.9 4.4 %copy-start.4 = (bf16[3,48,768]{2,1,0:T(8,128)(2,1)}, bf16[3,48,768]{2,1,0:T(8,128)(2,1)S(1)}, u32[]{:S(2)}) copy-start(bf16[3,48,768]{2,1,0:T(8,128)(2,1)S(1)} %collective-permute-done.prev_ref) | copy-start | bytes 663556
  17.3 0.7 %copy-start.5 = (bf16[3,48,768]{2,1,0:T(8,128)(2,1)}, bf16[3,48,768]{2,1,0:T(8,128)(2,1)S(1)}, u32[]{:S(2)}) copy-start(bf16[3,48,768]{2,1,0:T(8,128)(2,1)S(1)} %collective-permute-done.1.next_ref) | copy-start | bytes 663556
  22.7 5.0 %copy-start.13 = (f32[4]{0:T(128)S(1)}, f32[4]{0:T(128)}, u32[]{:S(2)}) copy-start(f32[4]{0:T(128)} %constant.23.clone) | copy-start | bytes 52
  22.7 12.0 %all-to-all-start = ((bf16[8,3,20,90]{3,2,1,0:T(8,128)(2,1)}), bf16[8,3,20,90]{3,2,1,0:T(8,128)(2,1)S(1)}, u32[]{:S(2)}, u32[]{:S(2)}) async-start(bf16[8,3,20,90]{3,2,1,0:T(8,128)(2,1)} %get-tuple-element.7), calls=%async_computation | async-start | bytes 294912 | tf_op jit(solution)/shard_map/all_to_all | solution.py:292
  34.8 0.7 copy-start.2
  38.0 9.6 %all-to-all-start.1 = ((bf16[8,3,16,90]{3,2,1,0:T(8,128)(2,1)}), bf16[8,3,16,90]{3,2,1,0:T(8,128)(2,1)S(1)}, u32[]{:S(2)}, u32[]{:S(2)}) async-start(bf16[8,3,16,90]{3,2,1,0:T(8,128)(2,1)} %shard_map.83), calls=%async_computation.1 | async-start | bytes 196608 | tf_op jit(solution)/shard_map/all_to_all | solution.py:299
  47.7 0.6 copy-start.3
  50.4 8.2 %collective-permute-start.2 = (bf16[3,48,768]{2,1,0:T(8,128)(2,1)}, bf16[3,48,768]{2,1,0:T(8,128)(2,1)S(1)}, u32[]{:S(2)}, u32[]{:S(2)}) collective-permute-start(bf16[3,48,768]{2,1,0:T(8,128)(2,1)} %shard_map.84.own_ref), channel_id=1, source_target_pairs={{0,1},{1,2},{2,3},{4,5},{5,6},{6,7},{8,9},{9,10},{10,11},{12,13},{... | collective-permute-start | bytes 663560 | tf_op jit(solution)/shard_map/ppermute | solution.py:43
  53.8 10.2 %collective-permute-start.3 = (bf16[3,48,768]{2,1,0:T(8,128)(2,1)}, bf16[3,48,768]{2,1,0:T(8,128)(2,1)S(1)}, u32[]{:S(2)}, u32[]{:S(2)}) collective-permute-start(bf16[3,48,768]{2,1,0:T(8,128)(2,1)} %shard_map.84.own_ref), channel_id=1, source_target_pairs={{1,0},{2,1},{3,2},{5,4},{6,5},{7,6},{9,8},{10,9},{11,10},{13,12},{... | collective-permute-start | bytes 663560 | tf_op jit(solution)/shard_map/ppermute | solution.py:44
  58.5 5.4 %copy-start.6 = (bf16[3,48,768]{2,1,0:T(8,128)(2,1)}, bf16[3,48,768]{2,1,0:T(8,128)(2,1)S(1)}, u32[]{:S(2)}) copy-start(bf16[3,48,768]{2,1,0:T(8,128)(2,1)S(1)} %collective-permute-done.2.prev_ref) | copy-start | bytes 663556
  63.9 0.7 %copy-start.7 = (bf16[3,48,768]{2,1,0:T(8,128)(2,1)}, bf16[3,48,768]{2,1,0:T(8,128)(2,1)S(1)}, u32[]{:S(2)}) copy-start(bf16[3,48,768]{2,1,0:T(8,128)(2,1)S(1)} %collective-permute-done.3.next_ref) | copy-start | bytes 663556

commit v7 on v6

--- a/solution.py
+++ b/solution.py
@@ -192,19 +192,11 @@
         out_ref[i] = (grad_act * slope_ref[i]).astype(jnp.bfloat16)
 
 
-def backward_kernel(basis_ref, step_ref, quad_ref, prev_ref, own_ref, next_ref, table_ref,
-                    out_ref):
-    rows, cp, width_p = own_ref.shape
-    channels, width = out_ref.shape[1], out_ref.shape[2]
+def backward_terms(basis_ref, step_ref, quad_ref, table_ref, rows, sources, acc):
     total_rows = step_ref.shape[0]
     first = lax.axis_index("lat") * rows
-    ext = (
-        [prev_ref[e] for e in range(HALF)]
-        + [own_ref[e] for e in range(rows)]
-        + [next_ref[e] for e in range(HALF)]
-    )
-    acc = [None] * rows
-    for e in range(rows + 2 * HALF):
+    for e, src_ref, r in sources:
+        cp, width_p = src_ref.shape[1], src_ref.shape[2]
         a_lo = max(0, 2 * HALF - e)
         a_hi = min(TAPS - 1, rows - 1 + 2 * HALF - e)
         if a_lo > a_hi:
@@ -221,7 +213,7 @@
             ],
             axis=0,
         )
-        source = ext[e]
+        source = src_ref[r]
         rolled = []
         for b in range(TAPS):
             if b == HALF:
@@ -236,6 +228,29 @@
             i2 = e + a - 2 * HALF
             piece = part[(a - a_lo) * cp : (a - a_lo + 1) * cp] * scale
             acc[i2] = piece if acc[i2] is None else acc[i2] + piece
+    return acc
+
+
+def backward_own_kernel(basis_ref, step_ref, quad_ref, own_ref, table_ref, acc_ref):
+    rows = own_ref.shape[0]
+    acc = backward_terms(
+        basis_ref, step_ref, quad_ref, table_ref, rows,
+        [(HALF + r, own_ref, r) for r in range(rows)], [None] * rows,
+    )
+    for i2 in range(rows):
+        acc_ref[i2] = acc[i2]
+
+
+def backward_halo_kernel(basis_ref, step_ref, quad_ref, prev_ref, next_ref, acc_in_ref,
+                         table_ref, out_ref):
+    rows = acc_in_ref.shape[0]
+    channels, width = out_ref.shape[1], out_ref.shape[2]
+    acc = backward_terms(
+        basis_ref, step_ref, quad_ref, table_ref, rows,
+        [(e, prev_ref, e) for e in range(HALF)]
+        + [(HALF + rows + e, next_ref, e) for e in range(HALF)],
+        [acc_in_ref[i2] for i2 in range(rows)],
+    )
     for i2 in range(rows):
         out_ref[i2] = acc[i2][:channels, :width].astype(out_ref.dtype)
 
@@ -306,12 +321,23 @@
     )(gc_home, slope, proj_t)
 
     g_low, g_high = halo(grad_filtered, "lat", HALF)
+    own_terms = pl.pallas_call(
+        backward_own_kernel,
+        out_shape=jax.ShapeDtypeStruct((rows, cp, width_p), jnp.float32),
+        in_specs=[smem(), smem(), smem()] + [vmem()] * 2,
+        out_specs=vmem(),
+        cost_estimate=pl.CostEstimate(
+            flops=2 * rows * rows * cp * TAPS * cp * width_p,
+            transcendentals=0,
+            bytes_accessed=rows * cp * width_p * 6,
+        ),
+    )(basis_flat, step_rows, quad_all, grad_filtered, tables)
     result = pl.pallas_call(
-        backward_kernel,
+        backward_halo_kernel,
         out_shape=jax.ShapeDtypeStruct((rows, channels, width), jnp.bfloat16),
         in_specs=[smem(), smem(), smem()] + [vmem()] * 4,
         out_specs=vmem(),
-    )(basis_flat, step_rows, quad_all, g_low, grad_filtered, g_high, tables)
+    )(basis_flat, step_rows, quad_all, g_low, g_high, own_terms, tables)
     return result[None]
 
 

time: 69 us -> 68.5 us (level)
  waiting for transfers between devices: 25 us -> 22.2 us
  Pallas kernels: 13.2 us -> 15.3 us
    ppermute x2, waiting for transfers between devices: 3.48 us -> 0.81 us  [halo(): low = lax.ppermute(block[block.shape[0] - width:], axis_name, forward)]
    pallas_call x1 -> x2, Pallas kernels: 3.84 us -> 5.93 us  [the longest x1 3.26 us: on_device(): pl.pallas_call(backward_halo_kernel, out_shape=jax.ShapeDtypeStruct((rows...]
  transfers between devices with their start and end apart: 6 -> 6, of which waited for: 5 -> 5; matrix products, arithmetic and copies ran while one was open for 10% -> 10% of each run, Pallas kernels for 0% -> 4%
where the time goes in v7:
time: 68.5 us; the launch traced here: 67.9 us
  waiting for transfers between devices  22.2 us (32%)
  starting transfers between devices  19.2 us (28%)
  Pallas kernels  15.3 us (22%)
  local copies, waits for them, and re-layouts  9.47 us (14%)
  other arithmetic  1.53 us (2%)
    ppermute x2, waiting for transfers between devices, halo(): high = lax.ppermute(block[:width], axis_name, backward)  9.69 us
    ppermute x2, starting transfers between devices, halo(): low = lax.ppermute(block[block.shape[0] - width:], axis_name, forward)  8.24 us
    all_to_all x1, waiting for transfers between devices, on_device(): lax.all_to_all(fc, 'member', split_axis=0, concat_axis=0, tiled=True)  6.2 us
    all_to_all x1, waiting for transfers between devices, on_device(): lax.all_to_all(gc_owned, 'member', split_axis=0, concat_axis=0, tiled=True)  5.55 us
    all_to_all x1, starting transfers between devices, on_device(): lax.all_to_all(fc, 'member', split_axis=0, concat_axis=0, tiled=True)  5.01 us
    pallas_call x1, Pallas kernels, on_device(): pl.pallas_call(forward_kernel, out_shape=(jax.ShapeDtypeStruct((rows, cp,...  4.71 us
    unnamed x32, local copies, waits for them, and re-layouts  3.81 us
    all_to_all x1, starting transfers between devices, on_device(): lax.all_to_all(gc_owned, 'member', split_axis=0, concat_axis=0, tiled=True)  3.36 us
  transfers between devices with their start and end apart: 6, of which 5 were waited for; matrix products, arithmetic and copies ran while one was open for 10% of the time, Pallas kernels for 4%

profile of v7, /device:TPU:0, one launch (start us, length us, event | category | flops | bytes accessed | tf_op | source)
XLA Modules:
  0.0 67.9 jit_solution(9072846403761613484)
XLA Ops:
  0.0 0.9 %pad_slice_fusion.1 = (bf16[3,48,24]{2,1,0:T(8,128)(2,1)S(1)}, bf16[3,48,24]{2,1,0:T(8,128)(2,1)S(1)}) fusion(bf16[3,45,720]{2,1,0:T(8,128)(2,1)} %bitcast.16), kind=kLoop, calls=%fused_computation.9 | loop fusion | bytes 208224 | tf_op jit(solution)/shard_map/slice | solution.py:29
  0.9 0.0 copy-done.1
  1.0 0.0 copy-start.8
  1.0 0.1 pad_maximum_fusion.own_ref
  1.1 4.9 %collective-permute-start = (bf16[3,48,768]{2,1,0:T(8,128)(2,1)S(1)}, bf16[3,48,768]{2,1,0:T(8,128)(2,1)S(1)}, u32[]{:S(2)}, u32[]{:S(2)}) collective-permute-start(bf16[3,48,768]{2,1,0:T(8,128)(2,1)S(1)} %pad_maximum_fusion.own_ref), channel_id=1, source_target_pairs={{0,1},{1,2},{2,3},{4,5},{5,6},{6,7},{8,9},{9,10},{10,11},{12,13},{... | collective-permute-start | bytes 663560 | tf_op jit(solution)/shard_map/ppermute | solution.py:43
  6.0 1.3 %collective-permute-start.1 = (bf16[3,48,768]{2,1,0:T(8,128)(2,1)S(1)}, bf16[3,48,768]{2,1,0:T(8,128)(2,1)S(1)}, u32[]{:S(2)}, u32[]{:S(2)}) collective-permute-start(bf16[3,48,768]{2,1,0:T(8,128)(2,1)S(1)} %pad_maximum_fusion.own_ref), channel_id=1, source_target_pairs={{1,0},{2,1},{3,2},{5,4},{6,5},{7,6},{9,8},{10,9},{11,10},{13,12},{... | collective-permute-start | bytes 663560 | tf_op jit(solution)/shard_map/ppermute | solution.py:44
  7.3 0.6 multiply_cosine_fusion.1.quad_ref
  7.9 0.0 copy-done.8
  7.9 0.1 copy.16
  8.1 0.0 copy-start.11
  8.1 0.0 copy-start.12
  8.1 0.1 copy.17
  8.2 0.6 copy-done.11
  8.8 0.7 reshape.27.basis_ref
  9.5 0.1 copy.15
  9.6 0.1 reshape.28
  9.7 0.1 copy.18
  9.8 0.6 pad.43.sub_ref
  10.4 0.1 copy-done.10
  10.5 0.6 pad.53.proj_ref
  11.1 0.6 pad.37.sub_t_ref
  11.7 0.0 copy-done.9
  11.7 0.6 copy.23
  12.3 0.7 %pad_maximum_fusion.1.table_ref = bf16[2,6,48,48]{3,2,1,0:T(8,128)(2,1)} fusion(bf16[1,6,48,48]{3,2,1,0:T(8,128)(2,1)S(1)} %get-tuple-element.12, bf16[1,6,48,48]{3,2,1,0:T(8,128)(2,1)S(1)} %copy.17), kind=kLoop, calls=%fused_computation.1 | loop fusion | flops 27648 | bytes 110592 | tf_op jit(solution)/shard_map/stack | solution.py:288
  13.0 0.0 collective-permute-done.prev_ref
  13.0 4.3 %collective-permute-done.1.next_ref = bf16[3,48,768]{2,1,0:T(8,128)(2,1)S(1)} collective-permute-done((bf16[3,48,768]{2,1,0:T(8,128)(2,1)S(1)}, bf16[3,48,768]{2,1,0:T(8,128)(2,1)S(1)}, u32[]{:S(2)}, u32[]{:S(2)}) %collective-permute-start.1) | collective-permute-done | bytes 221216 | tf_op jit(solution)/shard_map/ppermute | solution.py:44
  17.3 0.0 copy-done.4
  17.3 0.7 %copy-done.5 = bf16[3,48,768]{2,1,0:T(8,128)(2,1)} copy-done((bf16[3,48,768]{2,1,0:T(8,128)(2,1)}, bf16[3,48,768]{2,1,0:T(8,128)(2,1)S(1)}, u32[]{:S(2)}) %copy-start.5) | copy-done | bytes 221208
  18.0 4.7 %shard_map.82 = (f32[3,48,768]{2,1,0:T(8,128)}, bf16[8,3,20,90]{3,2,1,0:T(8,128)(2,1)}) custom-call(s32[588]{0:T(1024)} %reshape.27.basis_ref, s32[12]{0:T(128)} %step_ref.5, f32[12]{0:T(128)} %multiply_cosine_fusion.1.quad_ref, bf16[3,48,768]{2,1,0:T(8,128)(2,1)} %copy-done.4, bf16[3,48,768]{2,1,0:T(8,128)(2,1)} %copy-done, bf16[3,48,768]{2,1,0:T(8,128)(2,1)} %copy-done.5, ...), custom_call_target="tpu_custom_call" | custom-call | tf_op jit(solution)/shard_map/pallas_call | solution.py:297
  22.7 5.0 %all-to-all-start = ((bf16[8,3,20,90]{3,2,1,0:T(8,128)(2,1)}), bf16[8,3,20,90]{3,2,1,0:T(8,128)(2,1)S(1)}, u32[]{:S(2)}, u32[]{:S(2)}) async-start(bf16[8,3,20,90]{3,2,1,0:T(8,128)(2,1)} %get-tuple-element.7), calls=%async_computation | async-start | bytes 294912 | tf_op jit(solution)/shard_map/all_to_all | solution.py:307
  27.8 0.1 multiply_cosine_fusion
  27.9 0.7 %reshape.32.weight_ref = f32[48]{0:T(128)} reshape(f32[4,12]{1,0:T(4,128)S(1)} %multiply_cosine_fusion) | data formatting | bytes 384 | tf_op jit(solution)/shard_map/cos | solution.py:57
  28.6 6.2 %all-to-all-done.fc_ref = bf16[8,3,20,90]{3,2,1,0:T(8,128)(2,1)S(1)} async-done(((bf16[8,3,20,90]{3,2,1,0:T(8,128)(2,1)}), bf16[8,3,20,90]{3,2,1,0:T(8,128)(2,1)S(1)}, u32[]{:S(2)}, u32[]{:S(2)}) %all-to-all-start) | async-done | bytes 86432 | tf_op jit(solution)/shard_map/all_to_all | solution.py:307
  34.8 0.7 copy-done.2
  35.4 2.6 %shard_map.83 = bf16[8,3,16,90]{3,2,1,0:T(8,128)(2,1)} custom-call(f32[48]{0:T(128)} %reshape.32.weight_ref, bf16[16,20]{1,0:T(8,128)(2,1)} %pad.37.sub_t_ref, bf16[8,3,20,90]{3,2,1,0:T(8,128)(2,1)} %copy-done.2, f32[3,20,90]{2,1,0:T(8,128)} %bitcast.19), custom_call_target="tpu_custom_call" | custom-call | tf_op jit(solution)/shard_map/pallas_call | solution.py:308
  38.0 3.4 %all-to-all-start.1 = ((bf16[8,3,16,90]{3,2,1,0:T(8,128)(2,1)}), bf16[8,3,16,90]{3,2,1,0:T(8,128)(2,1)S(1)}, u32[]{:S(2)}, u32[]{:S(2)}) async-start(bf16[8,3,16,90]{3,2,1,0:T(8,128)(2,1)} %shard_map.83), calls=%async_computation.1 | async-start | bytes 196608 | tf_op jit(solution)/shard_map/all_to_all | solution.py:314
  41.4 0.1 copy.21
  41.5 0.6 pad.54.proj_t_ref
  42.1 5.5 %all-to-all-done.1.gc_ref = bf16[8,3,16,90]{3,2,1,0:T(8,128)(2,1)S(1)} async-done(((bf16[8,3,16,90]{3,2,1,0:T(8,128)(2,1)}), bf16[8,3,16,90]{3,2,1,0:T(8,128)(2,1)S(1)}, u32[]{:S(2)}, u32[]{:S(2)}) %all-to-all-start.1) | async-done | bytes 69152 | tf_op jit(solution)/shard_map/all_to_all | solution.py:314
  47.7 0.6 copy-done.3
  48.3 2.1 %shard_map.84.own_ref = bf16[3,48,768]{2,1,0:T(8,128)(2,1)} custom-call(bf16[8,3,16,90]{3,2,1,0:T(8,128)(2,1)} %copy-done.3, f32[3,48,768]{2,1,0:T(8,128)} %get-tuple-element.8.slope_ref, bf16[48,16]{1,0:T(8,128)(2,1)} %pad.54.proj_t_ref), custom_call_target="tpu_custom_call" | custom-call | tf_op jit(solution)/shard_map/pallas_call | solution.py:316
  50.4 3.4 %collective-permute-start.2 = (bf16[3,48,768]{2,1,0:T(8,128)(2,1)}, bf16[3,48,768]{2,1,0:T(8,128)(2,1)S(1)}, u32[]{:S(2)}, u32[]{:S(2)}) collective-permute-start(bf16[3,48,768]{2,1,0:T(8,128)(2,1)} %shard_map.84.own_ref), channel_id=1, source_target_pairs={{0,1},{1,2},{2,3},{4,5},{5,6},{6,7},{8,9},{9,10},{10,11},{12,13},{... | collective-permute-start | bytes 663560 | tf_op jit(solution)/shard_map/ppermute | solution.py:43
  53.7 1.3 %collective-permute-start.3 = (bf16[3,48,768]{2,1,0:T(8,128)(2,1)}, bf16[3,48,768]{2,1,0:T(8,128)(2,1)S(1)}, u32[]{:S(2)}, u32[]{:S(2)}) collective-permute-start(bf16[3,48,768]{2,1,0:T(8,128)(2,1)} %shard_map.84.own_ref), channel_id=1, source_target_pairs={{1,0},{2,1},{3,2},{5,4},{6,5},{7,6},{9,8},{10,9},{11,10},{13,12},{... | collective-permute-start | bytes 663560 | tf_op jit(solution)/shard_map/ppermute | solution.py:44
  55.0 2.7 %shard_map.85.acc_in_ref = f32[3,48,768]{2,1,0:T(8,128)} custom-call(s32[588]{0:T(1024)} %reshape.27.basis_ref, s32[12]{0:T(128)} %step_ref.5, f32[12]{0:T(128)} %multiply_cosine_fusion.1.quad_ref, bf16[3,48,768]{2,1,0:T(8,128)(2,1)} %shard_map.84.own_ref, bf16[2,6,48,48]{3,2,1,0:T(8,128)(2,1)} %pad_maximum_fusion.1.table_ref), custom_call_target="tpu_custom_call" | custom-call | flops 222953472 | bytes 663552 | tf_op jit(solution)/shard_map/pallas_call | solution.py:324
  57.7 0.8 %collective-permute-done.2.prev_ref = bf16[3,48,768]{2,1,0:T(8,128)(2,1)S(1)} collective-permute-done((bf16[3,48,768]{2,1,0:T(8,128)(2,1)}, bf16[3,48,768]{2,1,0:T(8,128)(2,1)S(1)}, u32[]{:S(2)}, u32[]{:S(2)}) %collective-permute-start.2) | collective-permute-done | bytes 221216 | tf_op jit(solution)/shard_map/ppermute | solution.py:43
  58.5 5.4 %collective-permute-done.3.next_ref = bf16[3,48,768]{2,1,0:T(8,128)(2,1)S(1)} collective-permute-done((bf16[3,48,768]{2,1,0:T(8,128)(2,1)}, bf16[3,48,768]{2,1,0:T(8,128)(2,1)S(1)}, u32[]{:S(2)}, u32[]{:S(2)}) %collective-permute-start.3) | collective-permute-done | bytes 221216 | tf_op jit(solution)/shard_map/ppermute | solution.py:44
  63.9 0.7 %copy-done.7 = bf16[3,48,768]{2,1,0:T(8,128)(2,1)} copy-done((bf16[3,48,768]{2,1,0:T(8,128)(2,1)}, bf16[3,48,768]{2,1,0:T(8,128)(2,1)S(1)}, u32[]{:S(2)}) %copy-start.7) | copy-done | bytes 221208
  64.6 3.3 %shard_map.86 = bf16[3,45,720]{2,1,0:T(8,128)(2,1)} custom-call(s32[588]{0:T(1024)} %reshape.27.basis_ref, s32[12]{0:T(128)} %step_ref.5, f32[12]{0:T(128)} %multiply_cosine_fusion.1.quad_ref, bf16[3,48,768]{2,1,0:T(8,128)(2,1)} %copy-done.6, bf16[3,48,768]{2,1,0:T(8,128)(2,1)} %copy-done.7, f32[3,48,768]{2,1,0:T(8,128)} %shard_map.85.acc_in_ref, ...), custom_call_target="tpu_custom_call" | custom-call | tf_op jit(solution)/shard_map/pallas_call | solution.py:335
  (19 shorter events, 0.1 us)
Async XLA Ops:
  0.0 1.0 %copy-start.1 = (bf16[1,3,45,720]{3,2,1,0:T(8,128)(2,1)S(1)}, bf16[1,3,45,720]{3,2,1,0:T(8,128)(2,1)}, u32[]{:S(2)}) copy-start(bf16[1,3,45,720]{3,2,1,0:T(8,128)(2,1)} %param.8) | copy-start | bytes 583204
  1.0 6.9 %copy-start.8 = (bf16[5,45,45]{2,1,0:T(8,128)(2,1)S(1)}, bf16[5,45,45]{2,1,0:T(8,128)(2,1)}, u32[]{:S(2)}) copy-start(bf16[5,45,45]{2,1,0:T(8,128)(2,1)} %param.9) | copy-start | bytes 60754
  1.1 7.1 %copy-start = (bf16[3,48,768]{2,1,0:T(8,128)(2,1)}, bf16[3,48,768]{2,1,0:T(8,128)(2,1)S(1)}, u32[]{:S(2)}) copy-start(bf16[3,48,768]{2,1,0:T(8,128)(2,1)S(1)} %pad_maximum_fusion.own_ref) | copy-start | bytes 663556
  1.1 11.9 %collective-permute-start = (bf16[3,48,768]{2,1,0:T(8,128)(2,1)S(1)}, bf16[3,48,768]{2,1,0:T(8,128)(2,1)S(1)}, u32[]{:S(2)}, u32[]{:S(2)}) collective-permute-start(bf16[3,48,768]{2,1,0:T(8,128)(2,1)S(1)} %pad_maximum_fusion.own_ref), channel_id=1, source_target_pairs={{0,1},{1,2},{2,3},{4,5},{5,6},{6,7},{8,9},{9,10},{10,11},{12,13},{... | collective-permute-start | bytes 663560 | tf_op jit(solution)/shard_map/ppermute | solution.py:43
  6.0 11.3 %collective-permute-start.1 = (bf16[3,48,768]{2,1,0:T(8,128)(2,1)S(1)}, bf16[3,48,768]{2,1,0:T(8,128)(2,1)S(1)}, u32[]{:S(2)}, u32[]{:S(2)}) collective-permute-start(bf16[3,48,768]{2,1,0:T(8,128)(2,1)S(1)} %pad_maximum_fusion.own_ref), channel_id=1, source_target_pairs={{1,0},{2,1},{3,2},{5,4},{6,5},{7,6},{9,8},{10,9},{11,10},{13,12},{... | collective-permute-start | bytes 663560 | tf_op jit(solution)/shard_map/ppermute | solution.py:44
  8.1 0.7 %copy-start.11 = (s32[12,49]{1,0:T(8,128)S(1)}, s32[12,49]{1,0:T(8,128)}, u32[]{:S(2)}) copy-start(s32[12,49]{1,0:T(8,128)} %param.13) | copy-start | bytes 7060
  8.1 1.4 %copy-start.12 = (bf16[4,5,5]{2,0,1:T(4,128)(2,1)S(1)}, bf16[4,5,5]{2,0,1:T(4,128)(2,1)}, u32[]{:S(2)}) copy-start(bf16[4,5,5]{2,0,1:T(4,128)(2,1)} %param.11) | copy-start | bytes 604
  8.8 2.9 %copy-start.9 = (f32[4,5,3,90]{3,0,2,1:T(4,128)S(1)}, f32[4,5,3,90]{3,0,2,1:T(4,128)}, u32[]{:S(2)}) copy-start(f32[4,5,3,90]{3,0,2,1:T(4,128)} %param.12) | copy-start | bytes 64804
  9.8 0.7 %copy-start.10 = (bf16[5,45]{1,0:T(8,128)(2,1)S(1)}, bf16[5,45]{1,0:T(8,128)(2,1)}, u32[]{:S(2)}) copy-start(bf16[5,45]{1,0:T(8,128)(2,1)} %param.10) | copy-start | bytes 1354
  13.0 4.3 %copy-start.4 = (bf16[3,48,768]{2,1,0:T(8,128)(2,1)}, bf16[3,48,768]{2,1,0:T(8,128)(2,1)S(1)}, u32[]{:S(2)}) copy-start(bf16[3,48,768]{2,1,0:T(8,128)(2,1)S(1)} %collective-permute-done.prev_ref) | copy-start | bytes 663556
  17.3 0.7 %copy-start.5 = (bf16[3,48,768]{2,1,0:T(8,128)(2,1)}, bf16[3,48,768]{2,1,0:T(8,128)(2,1)S(1)}, u32[]{:S(2)}) copy-start(bf16[3,48,768]{2,1,0:T(8,128)(2,1)S(1)} %collective-permute-done.1.next_ref) | copy-start | bytes 663556
  22.7 5.0 %copy-start.13 = (f32[4]{0:T(128)S(1)}, f32[4]{0:T(128)}, u32[]{:S(2)}) copy-start(f32[4]{0:T(128)} %constant.23.clone) | copy-start | bytes 52
  22.7 12.0 %all-to-all-start = ((bf16[8,3,20,90]{3,2,1,0:T(8,128)(2,1)}), bf16[8,3,20,90]{3,2,1,0:T(8,128)(2,1)S(1)}, u32[]{:S(2)}, u32[]{:S(2)}) async-start(bf16[8,3,20,90]{3,2,1,0:T(8,128)(2,1)} %get-tuple-element.7), calls=%async_computation | async-start | bytes 294912 | tf_op jit(solution)/shard_map/all_to_all | solution.py:307
  34.8 0.7 copy-start.2
  38.0 9.6 %all-to-all-start.1 = ((bf16[8,3,16,90]{3,2,1,0:T(8,128)(2,1)}), bf16[8,3,16,90]{3,2,1,0:T(8,128)(2,1)S(1)}, u32[]{:S(2)}, u32[]{:S(2)}) async-start(bf16[8,3,16,90]{3,2,1,0:T(8,128)(2,1)} %shard_map.83), calls=%async_computation.1 | async-start | bytes 196608 | tf_op jit(solution)/shard_map/all_to_all | solution.py:314
  47.7 0.6 copy-start.3
  50.4 8.2 %collective-permute-start.2 = (bf16[3,48,768]{2,1,0:T(8,128)(2,1)}, bf16[3,48,768]{2,1,0:T(8,128)(2,1)S(1)}, u32[]{:S(2)}, u32[]{:S(2)}) collective-permute-start(bf16[3,48,768]{2,1,0:T(8,128)(2,1)} %shard_map.84.own_ref), channel_id=1, source_target_pairs={{0,1},{1,2},{2,3},{4,5},{5,6},{6,7},{8,9},{9,10},{10,11},{12,13},{... | collective-permute-start | bytes 663560 | tf_op jit(solution)/shard_map/ppermute | solution.py:43
  53.7 10.2 %collective-permute-start.3 = (bf16[3,48,768]{2,1,0:T(8,128)(2,1)}, bf16[3,48,768]{2,1,0:T(8,128)(2,1)S(1)}, u32[]{:S(2)}, u32[]{:S(2)}) collective-permute-start(bf16[3,48,768]{2,1,0:T(8,128)(2,1)} %shard_map.84.own_ref), channel_id=1, source_target_pairs={{1,0},{2,1},{3,2},{5,4},{6,5},{7,6},{9,8},{10,9},{11,10},{13,12},{... | collective-permute-start | bytes 663560 | tf_op jit(solution)/shard_map/ppermute | solution.py:44
  58.5 5.4 %copy-start.6 = (bf16[3,48,768]{2,1,0:T(8,128)(2,1)}, bf16[3,48,768]{2,1,0:T(8,128)(2,1)S(1)}, u32[]{:S(2)}) copy-start(bf16[3,48,768]{2,1,0:T(8,128)(2,1)S(1)} %collective-permute-done.2.prev_ref) | copy-start | bytes 663556
  63.9 0.7 %copy-start.7 = (bf16[3,48,768]{2,1,0:T(8,128)(2,1)}, bf16[3,48,768]{2,1,0:T(8,128)(2,1)S(1)}, u32[]{:S(2)}) copy-start(bf16[3,48,768]{2,1,0:T(8,128)(2,1)S(1)} %collective-permute-done.3.next_ref) | copy-start | bytes 663556

commit v8 on v7

--- a/solution.py
+++ b/solution.py
@@ -84,36 +84,58 @@
     return x * half, half + x * (0.5 * (1.0 - t * t)) * d_inner
 
 
-def forward_kernel(basis_ref, step_ref, quad_ref, prev_ref, own_ref, next_ref, table_ref,
+def forward_taps(basis_ref, step_ref, table_ref, g, taps_a, sources):
+    cp, width_p = sources[0].shape
+    step = step_ref[g]
+    weights = jnp.concatenate(
+        [
+            jnp.concatenate(
+                [table_ref[0, basis_ref[g * TAPS * TAPS + a * TAPS + b]] for a in taps_a],
+                axis=1,
+            )
+            for b in range(TAPS)
+        ],
+        axis=0,
+    )
+    stacked = jnp.concatenate(sources, axis=0)
+    taps = jnp.dot(weights, stacked, preferred_element_type=jnp.float32)
+    total = taps[HALF * cp : (HALF + 1) * cp]
+    for b in range(TAPS):
+        if b == HALF:
+            continue
+        shift = lax.rem((HALF - b) * step + width_p, width_p)
+        total = total + pltpu.roll(taps[b * cp : (b + 1) * cp], shift, 1)
+    return total
+
+
+def own_taps(i, rows):
+    return [a for a in range(TAPS) if HALF <= i + a < HALF + rows]
+
+
+def forward_own_kernel(basis_ref, step_ref, own_ref, table_ref, part_ref):
+    rows = own_ref.shape[0]
+    first = lax.axis_index("lat") * rows
+    for i in range(rows):
+        taps_a = own_taps(i, rows)
+        part_ref[i] = forward_taps(
+            basis_ref, step_ref, table_ref, first + i, taps_a,
+            [own_ref[i + a - HALF] for a in taps_a],
+        )
+
+
+def forward_kernel(basis_ref, step_ref, quad_ref, prev_ref, next_ref, part_ref, table_ref,
                    proj_ref, sub_ref, slope_ref, fc_ref):
-    rows, cp, width_p = own_ref.shape
-    first = lax.axis_index("lat") * rows
-    ext = (
-        [prev_ref[e] for e in range(HALF)]
-        + [own_ref[e] for e in range(rows)]
-        + [next_ref[e] for e in range(HALF)]
-    )
+    rows = part_ref.shape[0]
+    first = lax.axis_index("lat") * rows
     for i in range(rows):
         g = first + i
-        step = step_ref[g]
-        weights = jnp.concatenate(
-            [
-                jnp.concatenate(
-                    [table_ref[0, basis_ref[g * TAPS * TAPS + a * TAPS + b]] for a in range(TAPS)],
-                    axis=1,
-                )
-                for b in range(TAPS)
-            ],
-            axis=0,
-        )
-        stacked = jnp.concatenate(ext[i : i + TAPS], axis=0)
-        taps = jnp.dot(weights, stacked, preferred_element_type=jnp.float32)
-        total = taps[HALF * cp : (HALF + 1) * cp]
-        for b in range(TAPS):
-            if b == HALF:
-                continue
-            shift = lax.rem((HALF - b) * step + width_p, width_p)
-            total = total + pltpu.roll(taps[b * cp : (b + 1) * cp], shift, 1)
+        own = own_taps(i, rows)
+        taps_a = [a for a in range(TAPS) if a not in own]
+        sources = [
+            prev_ref[i + a] if i + a < HALF else next_ref[i + a - HALF - rows]
+            for a in taps_a
+        ]
+        total = part_ref[i] + forward_taps(basis_ref, step_ref, table_ref, g, taps_a, sources)
         filtered = total * quad_ref[g]
         gelu_value, gelu_slope = gelu_and_grad(filtered)
         slope_ref[i] = gelu_slope
@@ -294,6 +316,17 @@
     own = to_ring(pad_axis(latents[0], 1, cp), width_p)
     low, high = halo(own, "lat", HALF)
 
+    own_part = pl.pallas_call(
+        forward_own_kernel,
+        out_shape=jax.ShapeDtypeStruct((rows, cp, width_p), jnp.float32),
+        in_specs=[smem(), smem()] + [vmem()] * 2,
+        out_specs=vmem(),
+        cost_estimate=pl.CostEstimate(
+            flops=2 * rows * TAPS * cp * rows * cp * width_p,
+            transcendentals=0,
+            bytes_accessed=rows * cp * width_p * 6,
+        ),
+    )(basis_flat, step_rows, own, tables)
     slope, fc = pl.pallas_call(
         forward_kernel,
         out_shape=(
@@ -302,7 +335,7 @@
         ),
         in_specs=[smem(), smem(), smem()] + [vmem()] * 6,
         out_specs=(vmem(), vmem()),
-    )(basis_flat, step_rows, quad_all, low, own, high, tables, proj_p, sub_p)
+    )(basis_flat, step_rows, quad_all, low, high, own_part, tables, proj_p, sub_p)
 
     fc_owned = lax.all_to_all(fc, "member", split_axis=0, concat_axis=0, tiled=True)
     gc_owned = pl.pallas_call(

time: 68.5 us -> 70.8 us (1.034)
  Pallas kernels: 15.3 us -> 18.1 us
  waiting for transfers between devices: 22.2 us -> 21.4 us
    pallas_call x0 -> x1, Pallas kernels: none -> 3.06 us  [on_device(): pl.pallas_call(forward_own_kernel, out_shape=jax.ShapeDtypeStruct((rows,...]
    ppermute x2, waiting for transfers between devices: 9.69 us -> 8.8 us  [halo(): high = lax.ppermute(block[:width], axis_name, backward)]
  transfers between devices with their start and end apart: 6 -> 6, of which waited for: 5 -> 5; matrix products, arithmetic and copies ran while one was open for 10% -> 9% of each run, Pallas kernels for 4% -> 8%
where the time goes in v8:
time: 70.8 us; the launch traced here: 70.2 us
  waiting for transfers between devices  21.4 us (30%)
  starting transfers between devices  19.7 us (28%)
  Pallas kernels  18.1 us (26%)
  local copies, waits for them, and re-layouts  9.46 us (13%)
  other arithmetic  1.45 us (2%)
    ppermute x2, waiting for transfers between devices, halo(): high = lax.ppermute(block[:width], axis_name, backward)  8.8 us
    ppermute x2, starting transfers between devices, halo(): low = lax.ppermute(block[block.shape[0] - width:], axis_name, forward)  8.75 us
    all_to_all x1, waiting for transfers between devices, on_device(): lax.all_to_all(fc, 'member', split_axis=0, concat_axis=0, tiled=True)  6.2 us
    all_to_all x1, waiting for transfers between devices, on_device(): lax.all_to_all(gc_owned, 'member', split_axis=0, concat_axis=0, tiled=True)  5.55 us
    all_to_all x1, starting transfers between devices, on_device(): lax.all_to_all(fc, 'member', split_axis=0, concat_axis=0, tiled=True)  5.01 us
    pallas_call x1, Pallas kernels, on_device(): pl.pallas_call(forward_kernel, out_shape=(jax.ShapeDtypeStruct((rows, cp,...  4.41 us
    unnamed x32, local copies, waits for them, and re-layouts  3.81 us
    all_to_all x1, starting transfers between devices, on_device(): lax.all_to_all(gc_owned, 'member', split_axis=0, concat_axis=0, tiled=True)  3.36 us
  transfers between devices with their start and end apart: 6, of which 5 were waited for; matrix products, arithmetic and copies ran while one was open for 9% of the time, Pallas kernels for 8%

profile of v8, /device:TPU:0, one launch (start us, length us, event | category | flops | bytes accessed | tf_op | source)
XLA Modules:
  0.0 70.2 jit_solution(6134558799255563091)
XLA Ops:
  0.0 0.9 %pad_slice_fusion.1 = (bf16[3,48,24]{2,1,0:T(8,128)(2,1)S(1)}, bf16[3,48,24]{2,1,0:T(8,128)(2,1)S(1)}) fusion(bf16[3,45,720]{2,1,0:T(8,128)(2,1)} %bitcast.16), kind=kLoop, calls=%fused_computation.9 | loop fusion | bytes 208224 | tf_op jit(solution)/shard_map/slice | solution.py:29
  0.9 0.0 copy-done
  1.0 0.0 copy-start.8
  1.0 0.1 pad_maximum_fusion.own_ref
  1.1 0.0 copy-start.5
  1.1 4.9 %collective-permute-start = (bf16[3,48,768]{2,1,0:T(8,128)(2,1)S(1)}, bf16[3,48,768]{2,1,0:T(8,128)(2,1)S(1)}, u32[]{:S(2)}, u32[]{:S(2)}) collective-permute-start(bf16[3,48,768]{2,1,0:T(8,128)(2,1)S(1)} %pad_maximum_fusion.own_ref), channel_id=1, source_target_pairs={{0,1},{1,2},{2,3},{4,5},{5,6},{6,7},{8,9},{9,10},{10,11},{12,13},{... | collective-permute-start | bytes 663560 | tf_op jit(solution)/shard_map/ppermute | solution.py:43
  6.0 1.3 %collective-permute-start.1 = (bf16[3,48,768]{2,1,0:T(8,128)(2,1)S(1)}, bf16[3,48,768]{2,1,0:T(8,128)(2,1)S(1)}, u32[]{:S(2)}, u32[]{:S(2)}) collective-permute-start(bf16[3,48,768]{2,1,0:T(8,128)(2,1)S(1)} %pad_maximum_fusion.own_ref), channel_id=1, source_target_pairs={{1,0},{2,1},{3,2},{5,4},{6,5},{7,6},{9,8},{10,9},{11,10},{13,12},{... | collective-permute-start | bytes 663560 | tf_op jit(solution)/shard_map/ppermute | solution.py:44
  7.3 0.0 copy-done.8
  7.3 0.1 copy.16
  7.5 0.0 copy-start.11
  7.5 0.0 copy-start.12
  7.5 0.1 copy.17
  7.6 0.6 copy-done.11
  8.2 0.7 reshape.27.basis_ref
  8.8 0.1 copy.15
  9.0 0.1 reshape.28
  9.1 0.1 copy.18
  9.2 0.6 pad.43.sub_ref
  9.8 0.1 copy-done.10
  9.9 0.6 pad.53.proj_ref
  10.5 0.6 pad.37.sub_t_ref
  11.1 0.6 copy.23
  11.7 0.7 pad_maximum_fusion.1.table_ref
  12.4 3.1 %shard_map.82.part_ref = f32[3,48,768]{2,1,0:T(8,128)} custom-call(s32[588]{0:T(1024)} %reshape.27.basis_ref, s32[12]{0:T(128)} %step_ref.7, bf16[3,48,768]{2,1,0:T(8,128)(2,1)} %copy-done.5, bf16[2,6,48,48]{3,2,1,0:T(8,128)(2,1)} %pad_maximum_fusion.1.table_ref), custom_call_target="tpu_custom_call" | custom-call | flops 222953472 | bytes 663552 | tf_op jit(solution)/shard_map/pallas_call | solution.py:319
  15.4 0.6 multiply_cosine_fusion.1.quad_ref
  16.0 0.0 collective-permute-done.prev_ref
  16.0 1.3 %collective-permute-done.1.next_ref = bf16[3,48,768]{2,1,0:T(8,128)(2,1)S(1)} collective-permute-done((bf16[3,48,768]{2,1,0:T(8,128)(2,1)S(1)}, bf16[3,48,768]{2,1,0:T(8,128)(2,1)S(1)}, u32[]{:S(2)}, u32[]{:S(2)}) %collective-permute-start.1) | collective-permute-done | bytes 221216 | tf_op jit(solution)/shard_map/ppermute | solution.py:44
  17.3 0.7 copy-done.4
  18.0 4.4 %shard_map.83 = (f32[3,48,768]{2,1,0:T(8,128)}, bf16[8,3,20,90]{3,2,1,0:T(8,128)(2,1)}) custom-call(s32[588]{0:T(1024)} %reshape.27.basis_ref, s32[12]{0:T(128)} %step_ref.7, f32[12]{0:T(128)} %multiply_cosine_fusion.1.quad_ref, bf16[3,48,768]{2,1,0:T(8,128)(2,1)} %copy-done.3, bf16[3,48,768]{2,1,0:T(8,128)(2,1)} %copy-done.4, ...), custom_call_target="tpu_custom_call" | custom-call | tf_op jit(solution)/shard_map/pallas_call | solution.py:330
  22.4 5.0 %all-to-all-start = ((bf16[8,3,20,90]{3,2,1,0:T(8,128)(2,1)}), bf16[8,3,20,90]{3,2,1,0:T(8,128)(2,1)S(1)}, u32[]{:S(2)}, u32[]{:S(2)}) async-start(bf16[8,3,20,90]{3,2,1,0:T(8,128)(2,1)} %get-tuple-element.7), calls=%async_computation | async-start | bytes 294912 | tf_op jit(solution)/shard_map/all_to_all | solution.py:340
  27.5 0.1 multiply_cosine_fusion
  27.6 0.7 reshape.32.weight_ref
  28.3 6.2 %all-to-all-done.fc_ref = bf16[8,3,20,90]{3,2,1,0:T(8,128)(2,1)S(1)} async-done(((bf16[8,3,20,90]{3,2,1,0:T(8,128)(2,1)}), bf16[8,3,20,90]{3,2,1,0:T(8,128)(2,1)S(1)}, u32[]{:S(2)}, u32[]{:S(2)}) %all-to-all-start) | async-done | bytes 86432 | tf_op jit(solution)/shard_map/all_to_all | solution.py:340
  34.5 0.7 copy-done.1
  35.1 2.6 %shard_map.84 = bf16[8,3,16,90]{3,2,1,0:T(8,128)(2,1)} custom-call(f32[48]{0:T(128)} %reshape.32.weight_ref, bf16[16,20]{1,0:T(8,128)(2,1)} %pad.37.sub_t_ref, bf16[8,3,20,90]{3,2,1,0:T(8,128)(2,1)} %copy-done.1, f32[3,20,90]{2,1,0:T(8,128)} %bitcast.19), custom_call_target="tpu_custom_call" | custom-call | tf_op jit(solution)/shard_map/pallas_call | solution.py:341
  37.7 3.4 %all-to-all-start.1 = ((bf16[8,3,16,90]{3,2,1,0:T(8,128)(2,1)}), bf16[8,3,16,90]{3,2,1,0:T(8,128)(2,1)S(1)}, u32[]{:S(2)}, u32[]{:S(2)}) async-start(bf16[8,3,16,90]{3,2,1,0:T(8,128)(2,1)} %shard_map.84), calls=%async_computation.1 | async-start | bytes 196608 | tf_op jit(solution)/shard_map/all_to_all | solution.py:347
  41.1 0.1 copy.21
  41.2 0.6 pad.54.proj_t_ref
  41.8 5.5 %all-to-all-done.1.gc_ref = bf16[8,3,16,90]{3,2,1,0:T(8,128)(2,1)S(1)} async-done(((bf16[8,3,16,90]{3,2,1,0:T(8,128)(2,1)}), bf16[8,3,16,90]{3,2,1,0:T(8,128)(2,1)S(1)}, u32[]{:S(2)}, u32[]{:S(2)}) %all-to-all-start.1) | async-done | bytes 69152 | tf_op jit(solution)/shard_map/all_to_all | solution.py:347
  47.4 0.6 copy-done.2
  48.0 2.1 %shard_map.85.own_ref = bf16[3,48,768]{2,1,0:T(8,128)(2,1)} custom-call(bf16[8,3,16,90]{3,2,1,0:T(8,128)(2,1)} %copy-done.2, f32[3,48,768]{2,1,0:T(8,128)} %get-tuple-element.8.slope_ref, bf16[48,16]{1,0:T(8,128)(2,1)} %pad.54.proj_t_ref), custom_call_target="tpu_custom_call" | custom-call | tf_op jit(solution)/shard_map/pallas_call | solution.py:349
  50.0 3.9 %collective-permute-start.2 = (bf16[3,48,768]{2,1,0:T(8,128)(2,1)}, bf16[3,48,768]{2,1,0:T(8,128)(2,1)S(1)}, u32[]{:S(2)}, u32[]{:S(2)}) collective-permute-start(bf16[3,48,768]{2,1,0:T(8,128)(2,1)} %shard_map.85.own_ref), channel_id=1, source_target_pairs={{0,1},{1,2},{2,3},{4,5},{5,6},{6,7},{8,9},{9,10},{10,11},{12,13},{... | collective-permute-start | bytes 663560 | tf_op jit(solution)/shard_map/ppermute | solution.py:43
  54.0 1.3 %collective-permute-start.3 = (bf16[3,48,768]{2,1,0:T(8,128)(2,1)}, bf16[3,48,768]{2,1,0:T(8,128)(2,1)S(1)}, u32[]{:S(2)}, u32[]{:S(2)}) collective-permute-start(bf16[3,48,768]{2,1,0:T(8,128)(2,1)} %shard_map.85.own_ref), channel_id=1, source_target_pairs={{1,0},{2,1},{3,2},{5,4},{6,5},{7,6},{9,8},{10,9},{11,10},{13,12},{... | collective-permute-start | bytes 663560 | tf_op jit(solution)/shard_map/ppermute | solution.py:44
  55.3 2.7 %shard_map.86.acc_in_ref = f32[3,48,768]{2,1,0:T(8,128)} custom-call(s32[588]{0:T(1024)} %reshape.27.basis_ref, s32[12]{0:T(128)} %step_ref.7, f32[12]{0:T(128)} %multiply_cosine_fusion.1.quad_ref, bf16[3,48,768]{2,1,0:T(8,128)(2,1)} %shard_map.85.own_ref, bf16[2,6,48,48]{3,2,1,0:T(8,128)(2,1)} %pad_maximum_fusion.1.table_ref), custom_call_target="tpu_custom_call" | custom-call | flops 222953472 | bytes 663552 | tf_op jit(solution)/shard_map/pallas_call | solution.py:357
  57.9 0.8 %collective-permute-done.2.prev_ref = bf16[3,48,768]{2,1,0:T(8,128)(2,1)S(1)} collective-permute-done((bf16[3,48,768]{2,1,0:T(8,128)(2,1)}, bf16[3,48,768]{2,1,0:T(8,128)(2,1)S(1)}, u32[]{:S(2)}, u32[]{:S(2)}) %collective-permute-start.2) | collective-permute-done | bytes 221216 | tf_op jit(solution)/shard_map/ppermute | solution.py:43
  58.7 7.5 %collective-permute-done.3.next_ref = bf16[3,48,768]{2,1,0:T(8,128)(2,1)S(1)} collective-permute-done((bf16[3,48,768]{2,1,0:T(8,128)(2,1)}, bf16[3,48,768]{2,1,0:T(8,128)(2,1)S(1)}, u32[]{:S(2)}, u32[]{:S(2)}) %collective-permute-start.3) | collective-permute-done | bytes 221216 | tf_op jit(solution)/shard_map/ppermute | solution.py:44
  66.2 0.7 copy-done.7
  66.9 3.3 %shard_map.87 = bf16[3,45,720]{2,1,0:T(8,128)(2,1)} custom-call(s32[588]{0:T(1024)} %reshape.27.basis_ref, s32[12]{0:T(128)} %step_ref.7, f32[12]{0:T(128)} %multiply_cosine_fusion.1.quad_ref, bf16[3,48,768]{2,1,0:T(8,128)(2,1)} %copy-done.6, bf16[3,48,768]{2,1,0:T(8,128)(2,1)} %copy-done.7, f32[3,48,768]{2,1,0:T(8,128)} %shard_map.86.acc_in_ref, ...), custom_call_target="tpu_custom_call" | custom-call | tf_op jit(solution)/shard_map/pallas_call | solution.py:368
  (20 shorter events, 0.1 us)
Async XLA Ops:
  0.0 1.0 %copy-start = (bf16[1,3,45,720]{3,2,1,0:T(8,128)(2,1)S(1)}, bf16[1,3,45,720]{3,2,1,0:T(8,128)(2,1)}, u32[]{:S(2)}) copy-start(bf16[1,3,45,720]{3,2,1,0:T(8,128)(2,1)} %param.8) | copy-start | bytes 583204
  1.0 6.3 %copy-start.8 = (bf16[5,45,45]{2,1,0:T(8,128)(2,1)S(1)}, bf16[5,45,45]{2,1,0:T(8,128)(2,1)}, u32[]{:S(2)}) copy-start(bf16[5,45,45]{2,1,0:T(8,128)(2,1)} %param.9) | copy-start | bytes 60754
  1.1 6.5 %copy-start.5 = (bf16[3,48,768]{2,1,0:T(8,128)(2,1)}, bf16[3,48,768]{2,1,0:T(8,128)(2,1)S(1)}, u32[]{:S(2)}) copy-start(bf16[3,48,768]{2,1,0:T(8,128)(2,1)S(1)} %pad_maximum_fusion.own_ref) | copy-start | bytes 663556
  1.1 14.9 %collective-permute-start = (bf16[3,48,768]{2,1,0:T(8,128)(2,1)S(1)}, bf16[3,48,768]{2,1,0:T(8,128)(2,1)S(1)}, u32[]{:S(2)}, u32[]{:S(2)}) collective-permute-start(bf16[3,48,768]{2,1,0:T(8,128)(2,1)S(1)} %pad_maximum_fusion.own_ref), channel_id=1, source_target_pairs={{0,1},{1,2},{2,3},{4,5},{5,6},{6,7},{8,9},{9,10},{10,11},{12,13},{... | collective-permute-start | bytes 663560 | tf_op jit(solution)/shard_map/ppermute | solution.py:43
  6.0 11.3 %collective-permute-start.1 = (bf16[3,48,768]{2,1,0:T(8,128)(2,1)S(1)}, bf16[3,48,768]{2,1,0:T(8,128)(2,1)S(1)}, u32[]{:S(2)}, u32[]{:S(2)}) collective-permute-start(bf16[3,48,768]{2,1,0:T(8,128)(2,1)S(1)} %pad_maximum_fusion.own_ref), channel_id=1, source_target_pairs={{1,0},{2,1},{3,2},{5,4},{6,5},{7,6},{9,8},{10,9},{11,10},{13,12},{... | collective-permute-start | bytes 663560 | tf_op jit(solution)/shard_map/ppermute | solution.py:44
  7.5 0.7 copy-start.11
  7.5 1.4 %copy-start.12 = (bf16[4,5,5]{2,0,1:T(4,128)(2,1)S(1)}, bf16[4,5,5]{2,0,1:T(4,128)(2,1)}, u32[]{:S(2)}) copy-start(bf16[4,5,5]{2,0,1:T(4,128)(2,1)} %param.11) | copy-start | bytes 604
  8.2 2.9 %copy-start.9 = (f32[4,5,3,90]{3,0,2,1:T(4,128)S(1)}, f32[4,5,3,90]{3,0,2,1:T(4,128)}, u32[]{:S(2)}) copy-start(f32[4,5,3,90]{3,0,2,1:T(4,128)} %param.12) | copy-start | bytes 64804
  9.2 0.7 copy-start.10
  16.0 1.3 %copy-start.3 = (bf16[3,48,768]{2,1,0:T(8,128)(2,1)}, bf16[3,48,768]{2,1,0:T(8,128)(2,1)S(1)}, u32[]{:S(2)}) copy-start(bf16[3,48,768]{2,1,0:T(8,128)(2,1)S(1)} %collective-permute-done.prev_ref) | copy-start | bytes 663556
  17.3 0.7 %copy-start.4 = (bf16[3,48,768]{2,1,0:T(8,128)(2,1)}, bf16[3,48,768]{2,1,0:T(8,128)(2,1)S(1)}, u32[]{:S(2)}) copy-start(bf16[3,48,768]{2,1,0:T(8,128)(2,1)S(1)} %collective-permute-done.1.next_ref) | copy-start | bytes 663556
  22.4 5.0 %copy-start.13 = (f32[4]{0:T(128)S(1)}, f32[4]{0:T(128)}, u32[]{:S(2)}) copy-start(f32[4]{0:T(128)} %constant.23.clone) | copy-start | bytes 52
  22.4 12.0 %all-to-all-start = ((bf16[8,3,20,90]{3,2,1,0:T(8,128)(2,1)}), bf16[8,3,20,90]{3,2,1,0:T(8,128)(2,1)S(1)}, u32[]{:S(2)}, u32[]{:S(2)}) async-start(bf16[8,3,20,90]{3,2,1,0:T(8,128)(2,1)} %get-tuple-element.7), calls=%async_computation | async-start | bytes 294912 | tf_op jit(solution)/shard_map/all_to_all | solution.py:340
  34.5 0.7 copy-start.1
  37.7 9.6 %all-to-all-start.1 = ((bf16[8,3,16,90]{3,2,1,0:T(8,128)(2,1)}), bf16[8,3,16,90]{3,2,1,0:T(8,128)(2,1)S(1)}, u32[]{:S(2)}, u32[]{:S(2)}) async-start(bf16[8,3,16,90]{3,2,1,0:T(8,128)(2,1)} %shard_map.84), calls=%async_computation.1 | async-start | bytes 196608 | tf_op jit(solution)/shard_map/all_to_all | solution.py:347
  47.4 0.6 copy-start.2
  50.0 8.7 %collective-permute-start.2 = (bf16[3,48,768]{2,1,0:T(8,128)(2,1)}, bf16[3,48,768]{2,1,0:T(8,128)(2,1)S(1)}, u32[]{:S(2)}, u32[]{:S(2)}) collective-permute-start(bf16[3,48,768]{2,1,0:T(8,128)(2,1)} %shard_map.85.own_ref), channel_id=1, source_target_pairs={{0,1},{1,2},{2,3},{4,5},{5,6},{6,7},{8,9},{9,10},{10,11},{12,13},{... | collective-permute-start | bytes 663560 | tf_op jit(solution)/shard_map/ppermute | solution.py:43
  54.0 12.2 %collective-permute-start.3 = (bf16[3,48,768]{2,1,0:T(8,128)(2,1)}, bf16[3,48,768]{2,1,0:T(8,128)(2,1)S(1)}, u32[]{:S(2)}, u32[]{:S(2)}) collective-permute-start(bf16[3,48,768]{2,1,0:T(8,128)(2,1)} %shard_map.85.own_ref), channel_id=1, source_target_pairs={{1,0},{2,1},{3,2},{5,4},{6,5},{7,6},{9,8},{10,9},{11,10},{13,12},{... | collective-permute-start | bytes 663560 | tf_op jit(solution)/shard_map/ppermute | solution.py:44
  58.7 7.5 %copy-start.6 = (bf16[3,48,768]{2,1,0:T(8,128)(2,1)}, bf16[3,48,768]{2,1,0:T(8,128)(2,1)S(1)}, u32[]{:S(2)}) copy-start(bf16[3,48,768]{2,1,0:T(8,128)(2,1)S(1)} %collective-permute-done.2.prev_ref) | copy-start | bytes 663556
  66.2 0.7 %copy-start.7 = (bf16[3,48,768]{2,1,0:T(8,128)(2,1)}, bf16[3,48,768]{2,1,0:T(8,128)(2,1)S(1)}, u32[]{:S(2)}) copy-start(bf16[3,48,768]{2,1,0:T(8,128)(2,1)S(1)} %collective-permute-done.3.next_ref) | copy-start | bytes 663556

commit v9 on v7

--- a/solution.py
+++ b/solution.py
@@ -188,7 +188,9 @@
         lo = extra // 2
         hi = extra - lo
         ring = jnp.concatenate([row, row[:, :lo], row[:, width - hi :]], axis=1)
-        grad_act = jnp.dot(proj_t_ref[...], ring, preferred_element_type=jnp.float32)
+        grad_act = jnp.dot(
+            proj_t_ref[...], ring.astype(jnp.float32), preferred_element_type=jnp.float32
+        )
         out_ref[i] = (grad_act * slope_ref[i]).astype(jnp.bfloat16)
 
 
@@ -278,7 +280,8 @@
 
     quad_all = latitude_rows(total_rows, total_rows)
     weight_all = subcell_weight(0, total_rows, total_rows).reshape(-1)
-    sub_t = pad_axis(subcell_maps.reshape(subcells * variables, variables).T, 0, vp)
+    vq = round_up(variables, 8)
+    sub_t = pad_axis(subcell_maps.reshape(subcells * variables, variables).T, 0, vq)
     blocks = lax.axis_size("member")
     block = width // blocks
     truth = verifying_truth.reshape(subcells * variables, rows, block).transpose(1, 0, 2)
@@ -307,12 +310,12 @@
     fc_owned = lax.all_to_all(fc, "member", split_axis=0, concat_axis=0, tiled=True)
     gc_owned = pl.pallas_call(
         functools.partial(score_kernel, subcells),
-        out_shape=jax.ShapeDtypeStruct((blocks, rows, vp, block), jnp.bfloat16),
+        out_shape=jax.ShapeDtypeStruct((blocks, rows, vq, block), jnp.bfloat16),
         in_specs=[smem()] + [vmem()] * 3,
         out_specs=vmem(),
     )(weight_all, sub_t, fc_owned, truth)
     gc_home = lax.all_to_all(gc_owned, "member", split_axis=0, concat_axis=0, tiled=True)
-    proj_t = pad_axis(pad_axis(project.T, 0, cp), 1, vp)
+    proj_t = pad_axis(pad_axis(project.T, 0, cp), 1, vq).astype(jnp.float32)
     grad_filtered = pl.pallas_call(
         grad_filtered_kernel,
         out_shape=jax.ShapeDtypeStruct((rows, cp, width_p), jnp.bfloat16),

time: 68.5 us -> 67.9 us (level)
  local copies, waits for them, and re-layouts: 9.47 us -> 8.75 us
    pad x5 -> x4, local copies, waits for them, and re-layouts: 2.43 us -> 1.81 us  [pad_axis(): return jnp.pad(block, pads)]
where the time goes in v9:
time: 67.9 us; the launch traced here: 67.4 us
  waiting for transfers between devices  21.9 us (32%)
  starting transfers between devices  19.2 us (28%)
  Pallas kernels  15.3 us (23%)
  local copies, waits for them, and re-layouts  8.75 us (13%)
  other arithmetic  2.15 us (3%)
    ppermute x2, waiting for transfers between devices, halo(): high = lax.ppermute(block[:width], axis_name, backward)  9.67 us
    ppermute x2, starting transfers between devices, halo(): low = lax.ppermute(block[block.shape[0] - width:], axis_name, forward)  8.25 us
    all_to_all x1, waiting for transfers between devices, on_device(): lax.all_to_all(fc, 'member', split_axis=0, concat_axis=0, tiled=True)  6.2 us
    all_to_all x1, waiting for transfers between devices, on_device(): lax.all_to_all(gc_owned, 'member', split_axis=0, concat_axis=0, tiled=True)  5.14 us
    all_to_all x1, starting transfers between devices, on_device(): lax.all_to_all(fc, 'member', split_axis=0, concat_axis=0, tiled=True)  5.01 us
    pallas_call x1, Pallas kernels, on_device(): pl.pallas_call(forward_kernel, out_shape=(jax.ShapeDtypeStruct((rows, cp,...  4.71 us
    unnamed x32, local copies, waits for them, and re-layouts  3.71 us
    all_to_all x1, starting transfers between devices, on_device(): lax.all_to_all(gc_owned, 'member', split_axis=0, concat_axis=0, tiled=True)  3.34 us
  transfers between devices with their start and end apart: 6, of which 5 were waited for; matrix products, arithmetic and copies ran while one was open for 10% of the time, Pallas kernels for 4%

profile of v9, /device:TPU:0, one launch (start us, length us, event | category | flops | bytes accessed | tf_op | source)
XLA Modules:
  0.0 67.4 jit_solution(7283273008918409411)
XLA Ops:
  0.0 0.9 %pad_slice_fusion.1 = (bf16[3,48,24]{2,1,0:T(8,128)(2,1)S(1)}, bf16[3,48,24]{2,1,0:T(8,128)(2,1)S(1)}) fusion(bf16[3,45,720]{2,1,0:T(8,128)(2,1)} %bitcast.16), kind=kLoop, calls=%fused_computation.10 | loop fusion | bytes 208224 | tf_op jit(solution)/shard_map/slice | solution.py:29
  0.9 0.0 copy-done.1
  1.0 0.0 copy-start.10
  1.0 0.0 copy-start.8
  1.0 0.1 pad_maximum_fusion.own_ref
  1.1 0.0 copy-start
  1.1 4.9 %collective-permute-start = (bf16[3,48,768]{2,1,0:T(8,128)(2,1)S(1)}, bf16[3,48,768]{2,1,0:T(8,128)(2,1)S(1)}, u32[]{:S(2)}, u32[]{:S(2)}) collective-permute-start(bf16[3,48,768]{2,1,0:T(8,128)(2,1)S(1)} %pad_maximum_fusion.own_ref), channel_id=1, source_target_pairs={{0,1},{1,2},{2,3},{4,5},{5,6},{6,7},{8,9},{9,10},{10,11},{12,13},{... | collective-permute-start | bytes 663560 | tf_op jit(solution)/shard_map/ppermute | solution.py:43
  6.0 1.3 %collective-permute-start.1 = (bf16[3,48,768]{2,1,0:T(8,128)(2,1)S(1)}, bf16[3,48,768]{2,1,0:T(8,128)(2,1)S(1)}, u32[]{:S(2)}, u32[]{:S(2)}) collective-permute-start(bf16[3,48,768]{2,1,0:T(8,128)(2,1)S(1)} %pad_maximum_fusion.own_ref), channel_id=1, source_target_pairs={{1,0},{2,1},{3,2},{5,4},{6,5},{7,6},{9,8},{10,9},{11,10},{13,12},{... | collective-permute-start | bytes 663560 | tf_op jit(solution)/shard_map/ppermute | solution.py:44
  7.3 0.6 multiply_cosine_fusion.1.quad_ref
  7.9 0.0 copy-done.10
  7.9 0.6 pad.53.proj_ref
  8.5 0.1 copy.21
  8.6 0.1 copy.16
  8.8 0.0 copy-start.11
  8.8 0.0 copy-start.12
  8.8 0.1 copy.17
  9.0 0.6 copy-done.11
  9.5 0.7 reshape.27.basis_ref
  10.2 0.1 copy.15
  10.3 0.1 reshape.28
  10.4 0.1 copy.18
  10.5 0.6 pad.43.sub_ref
  11.1 0.6 pad.37.sub_t_ref
  11.7 0.6 copy.23
  12.3 0.7 %pad_maximum_fusion.1.table_ref = bf16[2,6,48,48]{3,2,1,0:T(8,128)(2,1)} fusion(bf16[1,6,48,48]{3,2,1,0:T(8,128)(2,1)S(1)} %get-tuple-element.12, bf16[1,6,48,48]{3,2,1,0:T(8,128)(2,1)S(1)} %copy.17), kind=kLoop, calls=%fused_computation.1 | loop fusion | flops 27648 | bytes 110592 | tf_op jit(solution)/shard_map/stack | solution.py:291
  13.0 0.0 collective-permute-done.prev_ref
  13.0 4.3 %collective-permute-done.1.next_ref = bf16[3,48,768]{2,1,0:T(8,128)(2,1)S(1)} collective-permute-done((bf16[3,48,768]{2,1,0:T(8,128)(2,1)S(1)}, bf16[3,48,768]{2,1,0:T(8,128)(2,1)S(1)}, u32[]{:S(2)}, u32[]{:S(2)}) %collective-permute-start.1) | collective-permute-done | bytes 221216 | tf_op jit(solution)/shard_map/ppermute | solution.py:44
  17.3 0.7 %copy-done.4 = bf16[3,48,768]{2,1,0:T(8,128)(2,1)} copy-done((bf16[3,48,768]{2,1,0:T(8,128)(2,1)}, bf16[3,48,768]{2,1,0:T(8,128)(2,1)S(1)}, u32[]{:S(2)}) %copy-start.4) | copy-done | bytes 221208
  18.0 4.7 %shard_map.82 = (f32[3,48,768]{2,1,0:T(8,128)}, bf16[8,3,20,90]{3,2,1,0:T(8,128)(2,1)}) custom-call(s32[588]{0:T(1024)} %reshape.27.basis_ref, s32[12]{0:T(128)} %step_ref.5, f32[12]{0:T(128)} %multiply_cosine_fusion.1.quad_ref, bf16[3,48,768]{2,1,0:T(8,128)(2,1)} %copy-done.3, bf16[3,48,768]{2,1,0:T(8,128)(2,1)} %copy-done, bf16[3,48,768]{2,1,0:T(8,128)(2,1)} %copy-done.4, ...), custom_call_target="tpu_custom_call" | custom-call | tf_op jit(solution)/shard_map/pallas_call | solution.py:300
  22.8 5.0 %all-to-all-start = ((bf16[8,3,20,90]{3,2,1,0:T(8,128)(2,1)}), bf16[8,3,20,90]{3,2,1,0:T(8,128)(2,1)S(1)}, u32[]{:S(2)}, u32[]{:S(2)}) async-start(bf16[8,3,20,90]{3,2,1,0:T(8,128)(2,1)} %get-tuple-element.7), calls=%async_computation | async-start | bytes 294912 | tf_op jit(solution)/shard_map/all_to_all | solution.py:310
  27.8 0.0 copy-done.13
  27.8 0.1 multiply_cosine_fusion
  27.9 0.7 %reshape.32.weight_ref = f32[48]{0:T(128)} reshape(f32[4,12]{1,0:T(4,128)S(1)} %multiply_cosine_fusion) | data formatting | bytes 384 | tf_op jit(solution)/shard_map/cos | solution.py:57
  28.6 6.2 %all-to-all-done.fc_ref = bf16[8,3,20,90]{3,2,1,0:T(8,128)(2,1)S(1)} async-done(((bf16[8,3,20,90]{3,2,1,0:T(8,128)(2,1)}), bf16[8,3,20,90]{3,2,1,0:T(8,128)(2,1)S(1)}, u32[]{:S(2)}, u32[]{:S(2)}) %all-to-all-start) | async-done | bytes 86432 | tf_op jit(solution)/shard_map/all_to_all | solution.py:310
  34.8 0.7 copy-done.2
  35.4 2.6 %shard_map.83 = bf16[8,3,8,90]{3,2,1,0:T(8,128)(2,1)} custom-call(f32[48]{0:T(128)} %reshape.32.weight_ref, bf16[8,20]{1,0:T(8,128)(2,1)} %pad.37.sub_t_ref, bf16[8,3,20,90]{3,2,1,0:T(8,128)(2,1)} %copy-done.2, f32[3,20,90]{2,1,0:T(8,128)} %bitcast.19), custom_call_target="tpu_custom_call" | custom-call | tf_op jit(solution)/shard_map/pallas_call | solution.py:311
  38.0 3.3 %all-to-all-start.1 = ((bf16[8,3,8,90]{3,2,1,0:T(8,128)(2,1)}), bf16[8,3,8,90]{3,2,1,0:T(8,128)(2,1)S(1)}, u32[]{:S(2)}, u32[]{:S(2)}) async-start(bf16[8,3,8,90]{3,2,1,0:T(8,128)(2,1)} %shard_map.83), calls=%async_computation.1 | async-start | bytes 98304 | tf_op jit(solution)/shard_map/all_to_all | solution.py:317
  41.4 0.6 pad_convert_fusion.proj_t_ref
  42.0 5.1 %all-to-all-done.1.gc_ref = bf16[8,3,8,90]{3,2,1,0:T(8,128)(2,1)S(1)} async-done(((bf16[8,3,8,90]{3,2,1,0:T(8,128)(2,1)}), bf16[8,3,8,90]{3,2,1,0:T(8,128)(2,1)S(1)}, u32[]{:S(2)}, u32[]{:S(2)}) %all-to-all-start.1) | async-done | bytes 34592 | tf_op jit(solution)/shard_map/all_to_all | solution.py:317
  47.1 0.6 copy-done.7
  47.7 2.0 %shard_map.84.own_ref = bf16[3,48,768]{2,1,0:T(8,128)(2,1)} custom-call(bf16[8,3,8,90]{3,2,1,0:T(8,128)(2,1)} %copy-done.7, f32[3,48,768]{2,1,0:T(8,128)} %get-tuple-element.8.slope_ref, f32[48,8]{1,0:T(8,128)} %pad_convert_fusion.proj_t_ref), custom_call_target="tpu_custom_call" | custom-call | tf_op jit(solution)/shard_map/pallas_call | solution.py:319
  49.8 3.4 %collective-permute-start.2 = (bf16[3,48,768]{2,1,0:T(8,128)(2,1)}, bf16[3,48,768]{2,1,0:T(8,128)(2,1)S(1)}, u32[]{:S(2)}, u32[]{:S(2)}) collective-permute-start(bf16[3,48,768]{2,1,0:T(8,128)(2,1)} %shard_map.84.own_ref), channel_id=1, source_target_pairs={{0,1},{1,2},{2,3},{4,5},{5,6},{6,7},{8,9},{9,10},{10,11},{12,13},{... | collective-permute-start | bytes 663560 | tf_op jit(solution)/shard_map/ppermute | solution.py:43
  53.2 1.3 %collective-permute-start.3 = (bf16[3,48,768]{2,1,0:T(8,128)(2,1)}, bf16[3,48,768]{2,1,0:T(8,128)(2,1)S(1)}, u32[]{:S(2)}, u32[]{:S(2)}) collective-permute-start(bf16[3,48,768]{2,1,0:T(8,128)(2,1)} %shard_map.84.own_ref), channel_id=1, source_target_pairs={{1,0},{2,1},{3,2},{5,4},{6,5},{7,6},{9,8},{10,9},{11,10},{13,12},{... | collective-permute-start | bytes 663560 | tf_op jit(solution)/shard_map/ppermute | solution.py:44
  54.5 2.7 %shard_map.85.acc_in_ref = f32[3,48,768]{2,1,0:T(8,128)} custom-call(s32[588]{0:T(1024)} %reshape.27.basis_ref, s32[12]{0:T(128)} %step_ref.5, f32[12]{0:T(128)} %multiply_cosine_fusion.1.quad_ref, bf16[3,48,768]{2,1,0:T(8,128)(2,1)} %shard_map.84.own_ref, bf16[2,6,48,48]{3,2,1,0:T(8,128)(2,1)} %pad_maximum_fusion.1.table_ref), custom_call_target="tpu_custom_call" | custom-call | flops 222953472 | bytes 663552 | tf_op jit(solution)/shard_map/pallas_call | solution.py:327
  57.2 0.8 %collective-permute-done.2.prev_ref = bf16[3,48,768]{2,1,0:T(8,128)(2,1)S(1)} collective-permute-done((bf16[3,48,768]{2,1,0:T(8,128)(2,1)}, bf16[3,48,768]{2,1,0:T(8,128)(2,1)S(1)}, u32[]{:S(2)}, u32[]{:S(2)}) %collective-permute-start.2) | collective-permute-done | bytes 221216 | tf_op jit(solution)/shard_map/ppermute | solution.py:43
  58.0 5.4 %collective-permute-done.3.next_ref = bf16[3,48,768]{2,1,0:T(8,128)(2,1)S(1)} collective-permute-done((bf16[3,48,768]{2,1,0:T(8,128)(2,1)}, bf16[3,48,768]{2,1,0:T(8,128)(2,1)S(1)}, u32[]{:S(2)}, u32[]{:S(2)}) %collective-permute-start.3) | collective-permute-done | bytes 221216 | tf_op jit(solution)/shard_map/ppermute | solution.py:44
  63.4 0.7 %copy-done.6 = bf16[3,48,768]{2,1,0:T(8,128)(2,1)} copy-done((bf16[3,48,768]{2,1,0:T(8,128)(2,1)}, bf16[3,48,768]{2,1,0:T(8,128)(2,1)S(1)}, u32[]{:S(2)}) %copy-start.6) | copy-done | bytes 221208
  64.1 3.3 %shard_map.86 = bf16[3,45,720]{2,1,0:T(8,128)(2,1)} custom-call(s32[588]{0:T(1024)} %reshape.27.basis_ref, s32[12]{0:T(128)} %step_ref.5, f32[12]{0:T(128)} %multiply_cosine_fusion.1.quad_ref, bf16[3,48,768]{2,1,0:T(8,128)(2,1)} %copy-done.5, bf16[3,48,768]{2,1,0:T(8,128)(2,1)} %copy-done.6, f32[3,48,768]{2,1,0:T(8,128)} %shard_map.85.acc_in_ref, ...), custom_call_target="tpu_custom_call" | custom-call | tf_op jit(solution)/shard_map/pallas_call | solution.py:338
  (19 shorter events, 0.1 us)
Async XLA Ops:
  0.0 1.0 %copy-start.1 = (bf16[1,3,45,720]{3,2,1,0:T(8,128)(2,1)S(1)}, bf16[1,3,45,720]{3,2,1,0:T(8,128)(2,1)}, u32[]{:S(2)}) copy-start(bf16[1,3,45,720]{3,2,1,0:T(8,128)(2,1)} %param.8) | copy-start | bytes 583204
  1.0 6.9 %copy-start.10 = (bf16[5,45]{1,0:T(8,128)(2,1)S(1)}, bf16[5,45]{1,0:T(8,128)(2,1)}, u32[]{:S(2)}) copy-start(bf16[5,45]{1,0:T(8,128)(2,1)} %param.10) | copy-start | bytes 1354
  1.0 7.6 %copy-start.8 = (bf16[5,45,45]{2,1,0:T(8,128)(2,1)S(1)}, bf16[5,45,45]{2,1,0:T(8,128)(2,1)}, u32[]{:S(2)}) copy-start(bf16[5,45,45]{2,1,0:T(8,128)(2,1)} %param.9) | copy-start | bytes 60754
  1.1 7.8 %copy-start = (bf16[3,48,768]{2,1,0:T(8,128)(2,1)}, bf16[3,48,768]{2,1,0:T(8,128)(2,1)S(1)}, u32[]{:S(2)}) copy-start(bf16[3,48,768]{2,1,0:T(8,128)(2,1)S(1)} %pad_maximum_fusion.own_ref) | copy-start | bytes 663556
  1.1 11.9 %collective-permute-start = (bf16[3,48,768]{2,1,0:T(8,128)(2,1)S(1)}, bf16[3,48,768]{2,1,0:T(8,128)(2,1)S(1)}, u32[]{:S(2)}, u32[]{:S(2)}) collective-permute-start(bf16[3,48,768]{2,1,0:T(8,128)(2,1)S(1)} %pad_maximum_fusion.own_ref), channel_id=1, source_target_pairs={{0,1},{1,2},{2,3},{4,5},{5,6},{6,7},{8,9},{9,10},{10,11},{12,13},{... | collective-permute-start | bytes 663560 | tf_op jit(solution)/shard_map/ppermute | solution.py:43
  6.0 11.3 %collective-permute-start.1 = (bf16[3,48,768]{2,1,0:T(8,128)(2,1)S(1)}, bf16[3,48,768]{2,1,0:T(8,128)(2,1)S(1)}, u32[]{:S(2)}, u32[]{:S(2)}) collective-permute-start(bf16[3,48,768]{2,1,0:T(8,128)(2,1)S(1)} %pad_maximum_fusion.own_ref), channel_id=1, source_target_pairs={{1,0},{2,1},{3,2},{5,4},{6,5},{7,6},{9,8},{10,9},{11,10},{13,12},{... | collective-permute-start | bytes 663560 | tf_op jit(solution)/shard_map/ppermute | solution.py:44
  8.8 0.7 %copy-start.11 = (s32[12,49]{1,0:T(8,128)S(1)}, s32[12,49]{1,0:T(8,128)}, u32[]{:S(2)}) copy-start(s32[12,49]{1,0:T(8,128)} %param.13) | copy-start | bytes 7060
  8.8 1.4 %copy-start.12 = (bf16[4,5,5]{2,0,1:T(4,128)(2,1)S(1)}, bf16[4,5,5]{2,0,1:T(4,128)(2,1)}, u32[]{:S(2)}) copy-start(bf16[4,5,5]{2,0,1:T(4,128)(2,1)} %param.11) | copy-start | bytes 604
  9.5 2.2 %copy-start.9 = (f32[4,5,3,90]{3,0,2,1:T(4,128)S(1)}, f32[4,5,3,90]{3,0,2,1:T(4,128)}, u32[]{:S(2)}) copy-start(f32[4,5,3,90]{3,0,2,1:T(4,128)} %param.12) | copy-start | bytes 64804
  13.0 4.3 %copy-start.3 = (bf16[3,48,768]{2,1,0:T(8,128)(2,1)}, bf16[3,48,768]{2,1,0:T(8,128)(2,1)S(1)}, u32[]{:S(2)}) copy-start(bf16[3,48,768]{2,1,0:T(8,128)(2,1)S(1)} %collective-permute-done.prev_ref) | copy-start | bytes 663556
  17.3 0.7 %copy-start.4 = (bf16[3,48,768]{2,1,0:T(8,128)(2,1)}, bf16[3,48,768]{2,1,0:T(8,128)(2,1)S(1)}, u32[]{:S(2)}) copy-start(bf16[3,48,768]{2,1,0:T(8,128)(2,1)S(1)} %collective-permute-done.1.next_ref) | copy-start | bytes 663556
  22.8 5.0 %copy-start.13 = (f32[4]{0:T(128)S(1)}, f32[4]{0:T(128)}, u32[]{:S(2)}) copy-start(f32[4]{0:T(128)} %constant.23.clone) | copy-start | bytes 52
  22.8 12.0 %all-to-all-start = ((bf16[8,3,20,90]{3,2,1,0:T(8,128)(2,1)}), bf16[8,3,20,90]{3,2,1,0:T(8,128)(2,1)S(1)}, u32[]{:S(2)}, u32[]{:S(2)}) async-start(bf16[8,3,20,90]{3,2,1,0:T(8,128)(2,1)} %get-tuple-element.7), calls=%async_computation | async-start | bytes 294912 | tf_op jit(solution)/shard_map/all_to_all | solution.py:310
  34.8 0.7 copy-start.2
  38.0 9.1 %all-to-all-start.1 = ((bf16[8,3,8,90]{3,2,1,0:T(8,128)(2,1)}), bf16[8,3,8,90]{3,2,1,0:T(8,128)(2,1)S(1)}, u32[]{:S(2)}, u32[]{:S(2)}) async-start(bf16[8,3,8,90]{3,2,1,0:T(8,128)(2,1)} %shard_map.83), calls=%async_computation.1 | async-start | bytes 98304 | tf_op jit(solution)/shard_map/all_to_all | solution.py:317
  47.1 0.6 copy-start.7
  49.8 8.2 %collective-permute-start.2 = (bf16[3,48,768]{2,1,0:T(8,128)(2,1)}, bf16[3,48,768]{2,1,0:T(8,128)(2,1)S(1)}, u32[]{:S(2)}, u32[]{:S(2)}) collective-permute-start(bf16[3,48,768]{2,1,0:T(8,128)(2,1)} %shard_map.84.own_ref), channel_id=1, source_target_pairs={{0,1},{1,2},{2,3},{4,5},{5,6},{6,7},{8,9},{9,10},{10,11},{12,13},{... | collective-permute-start | bytes 663560 | tf_op jit(solution)/shard_map/ppermute | solution.py:43
  53.2 10.2 %collective-permute-start.3 = (bf16[3,48,768]{2,1,0:T(8,128)(2,1)}, bf16[3,48,768]{2,1,0:T(8,128)(2,1)S(1)}, u32[]{:S(2)}, u32[]{:S(2)}) collective-permute-start(bf16[3,48,768]{2,1,0:T(8,128)(2,1)} %shard_map.84.own_ref), channel_id=1, source_target_pairs={{1,0},{2,1},{3,2},{5,4},{6,5},{7,6},{9,8},{10,9},{11,10},{13,12},{... | collective-permute-start | bytes 663560 | tf_op jit(solution)/shard_map/ppermute | solution.py:44
  58.0 5.4 %copy-start.5 = (bf16[3,48,768]{2,1,0:T(8,128)(2,1)}, bf16[3,48,768]{2,1,0:T(8,128)(2,1)S(1)}, u32[]{:S(2)}) copy-start(bf16[3,48,768]{2,1,0:T(8,128)(2,1)S(1)} %collective-permute-done.2.prev_ref) | copy-start | bytes 663556
  63.4 0.7 %copy-start.6 = (bf16[3,48,768]{2,1,0:T(8,128)(2,1)}, bf16[3,48,768]{2,1,0:T(8,128)(2,1)S(1)}, u32[]{:S(2)}) copy-start(bf16[3,48,768]{2,1,0:T(8,128)(2,1)S(1)} %collective-permute-done.3.next_ref) | copy-start | bytes 663556

commit v10 on v9

--- a/solution.py
+++ b/solution.py
@@ -243,14 +243,25 @@
         acc_ref[i2] = acc[i2]
 
 
-def backward_halo_kernel(basis_ref, step_ref, quad_ref, prev_ref, next_ref, acc_in_ref,
-                         table_ref, out_ref):
+def backward_prev_kernel(basis_ref, step_ref, quad_ref, prev_ref, acc_in_ref, table_ref,
+                         acc_ref):
+    rows = acc_in_ref.shape[0]
+    acc = backward_terms(
+        basis_ref, step_ref, quad_ref, table_ref, rows,
+        [(e, prev_ref, e) for e in range(HALF)],
+        [acc_in_ref[i2] for i2 in range(rows)],
+    )
+    for i2 in range(rows):
+        acc_ref[i2] = acc[i2]
+
+
+def backward_next_kernel(basis_ref, step_ref, quad_ref, next_ref, acc_in_ref, table_ref,
+                         out_ref):
     rows = acc_in_ref.shape[0]
     channels, width = out_ref.shape[1], out_ref.shape[2]
     acc = backward_terms(
         basis_ref, step_ref, quad_ref, table_ref, rows,
-        [(e, prev_ref, e) for e in range(HALF)]
-        + [(HALF + rows + e, next_ref, e) for e in range(HALF)],
+        [(HALF + rows + e, next_ref, e) for e in range(HALF)],
         [acc_in_ref[i2] for i2 in range(rows)],
     )
     for i2 in range(rows):
@@ -335,12 +346,23 @@
             bytes_accessed=rows * cp * width_p * 6,
         ),
     )(basis_flat, step_rows, quad_all, grad_filtered, tables)
+    with_prev = pl.pallas_call(
+        backward_prev_kernel,
+        out_shape=jax.ShapeDtypeStruct((rows, cp, width_p), jnp.float32),
+        in_specs=[smem(), smem(), smem()] + [vmem()] * 3,
+        out_specs=vmem(),
+        cost_estimate=pl.CostEstimate(
+            flops=2 * rows * HALF * cp * TAPS * cp * width_p,
+            transcendentals=0,
+            bytes_accessed=rows * cp * width_p * 10,
+        ),
+    )(basis_flat, step_rows, quad_all, g_low, own_terms, tables)
     result = pl.pallas_call(
-        backward_halo_kernel,
+        backward_next_kernel,
         out_shape=jax.ShapeDtypeStruct((rows, channels, width), jnp.bfloat16),
-        in_specs=[smem(), smem(), smem()] + [vmem()] * 4,
-        out_specs=vmem(),
-    )(basis_flat, step_rows, quad_all, g_low, g_high, own_terms, tables)
+        in_specs=[smem(), smem(), smem()] + [vmem()] * 3,
+        out_specs=vmem(),
+    )(basis_flat, step_rows, quad_all, g_high, with_prev, tables)
     return result[None]
 
 

time: 67.9 us -> 67.3 us (level)
  waiting for transfers between devices: 21.9 us -> 18.5 us
  Pallas kernels: 15.3 us -> 17.3 us
    ppermute x2, waiting for transfers between devices: 9.67 us -> 6.3 us  [halo(): high = lax.ppermute(block[:width], axis_name, backward)]
    pallas_call x1 -> x2, Pallas kernels: 3.26 us -> 5.31 us  [the longest x1 2.7 us: on_device(): pl.pallas_call(backward_prev_kernel, out_shape=jax.ShapeDtypeStruct((rows...]
  transfers between devices with their start and end apart: 6 -> 6, of which waited for: 5 -> 5; matrix products, arithmetic and copies ran while one was open for 10% -> 10% of each run, Pallas kernels for 4% -> 8%
where the time goes in v10:
time: 67.3 us; the launch traced here: 66.7 us
  starting transfers between devices  19.2 us (29%)
  waiting for transfers between devices  18.5 us (27%)
  Pallas kernels  17.3 us (26%)
  local copies, waits for them, and re-layouts  9.41 us (14%)
  other arithmetic  2.13 us (3%)
    ppermute x2, starting transfers between devices, halo(): low = lax.ppermute(block[block.shape[0] - width:], axis_name, forward)  8.26 us
    ppermute x2, waiting for transfers between devices, halo(): high = lax.ppermute(block[:width], axis_name, backward)  6.3 us
    all_to_all x1, waiting for transfers between devices, on_device(): lax.all_to_all(fc, 'member', split_axis=0, concat_axis=0, tiled=True)  6.22 us
    all_to_all x1, waiting for transfers between devices, on_device(): lax.all_to_all(gc_owned, 'member', split_axis=0, concat_axis=0, tiled=True)  5.14 us
    all_to_all x1, starting transfers between devices, on_device(): lax.all_to_all(fc, 'member', split_axis=0, concat_axis=0, tiled=True)  5.01 us
    pallas_call x1, Pallas kernels, on_device(): pl.pallas_call(forward_kernel, out_shape=(jax.ShapeDtypeStruct((rows, cp,...  4.7 us
    unnamed x32, local copies, waits for them, and re-layouts  4.39 us
    all_to_all x1, starting transfers between devices, on_device(): lax.all_to_all(gc_owned, 'member', split_axis=0, concat_axis=0, tiled=True)  3.34 us
  transfers between devices with their start and end apart: 6, of which 5 were waited for; matrix products, arithmetic and copies ran while one was open for 10% of the time, Pallas kernels for 8%

profile of v10, /device:TPU:0, one launch (start us, length us, event | category | flops | bytes accessed | tf_op | source)
XLA Modules:
  0.0 66.7 jit_solution(16782230860760821120)
XLA Ops:
  0.0 0.9 %pad_slice_fusion.1 = (bf16[3,48,24]{2,1,0:T(8,128)(2,1)S(1)}, bf16[3,48,24]{2,1,0:T(8,128)(2,1)S(1)}) fusion(bf16[3,45,720]{2,1,0:T(8,128)(2,1)} %bitcast.16), kind=kLoop, calls=%fused_computation.10 | loop fusion | bytes 208224 | tf_op jit(solution)/shard_map/slice | solution.py:29
  0.9 0.0 copy-done.1
  1.0 0.0 copy-start.10
  1.0 0.0 copy-start.8
  1.0 0.1 pad_maximum_fusion.own_ref
  1.1 0.0 copy-start
  1.1 4.9 %collective-permute-start = (bf16[3,48,768]{2,1,0:T(8,128)(2,1)S(1)}, bf16[3,48,768]{2,1,0:T(8,128)(2,1)S(1)}, u32[]{:S(2)}, u32[]{:S(2)}) collective-permute-start(bf16[3,48,768]{2,1,0:T(8,128)(2,1)S(1)} %pad_maximum_fusion.own_ref), channel_id=1, source_target_pairs={{0,1},{1,2},{2,3},{4,5},{5,6},{6,7},{8,9},{9,10},{10,11},{12,13},{... | collective-permute-start | bytes 663560 | tf_op jit(solution)/shard_map/ppermute | solution.py:43
  6.0 1.3 %collective-permute-start.1 = (bf16[3,48,768]{2,1,0:T(8,128)(2,1)S(1)}, bf16[3,48,768]{2,1,0:T(8,128)(2,1)S(1)}, u32[]{:S(2)}, u32[]{:S(2)}) collective-permute-start(bf16[3,48,768]{2,1,0:T(8,128)(2,1)S(1)} %pad_maximum_fusion.own_ref), channel_id=1, source_target_pairs={{1,0},{2,1},{3,2},{5,4},{6,5},{7,6},{9,8},{10,9},{11,10},{13,12},{... | collective-permute-start | bytes 663560 | tf_op jit(solution)/shard_map/ppermute | solution.py:44
  7.3 0.6 multiply_cosine_fusion.1.quad_ref
  7.9 0.6 pad.53.proj_ref
  8.5 0.1 copy.21
  8.6 0.1 copy.16
  8.8 0.0 copy-start.11
  8.8 0.0 copy-start.12
  8.8 0.1 copy.17
  9.0 0.6 copy-done.11
  9.5 0.7 %reshape.27.basis_ref = s32[588]{0:T(1024)} reshape(s32[12,49]{1,0:T(8,128)S(1)} %copy-done.11) | data formatting | bytes 4704 | tf_op jit(solution)/shard_map/reshape | solution.py:303
  10.2 0.1 copy.15
  10.3 0.1 reshape.28
  10.4 0.1 copy.18
  10.5 0.6 pad.43.sub_ref
  11.1 0.6 pad.37.sub_t_ref
  11.7 0.6 copy.23
  12.3 0.7 %pad_maximum_fusion.1.table_ref = bf16[2,6,48,48]{3,2,1,0:T(8,128)(2,1)} fusion(bf16[1,6,48,48]{3,2,1,0:T(8,128)(2,1)S(1)} %get-tuple-element.12, bf16[1,6,48,48]{3,2,1,0:T(8,128)(2,1)S(1)} %copy.17), kind=kLoop, calls=%fused_computation.1 | loop fusion | flops 27648 | bytes 110592 | tf_op jit(solution)/shard_map/stack | solution.py:302
  13.0 0.0 collective-permute-done.prev_ref
  13.0 4.3 %collective-permute-done.1.next_ref = bf16[3,48,768]{2,1,0:T(8,128)(2,1)S(1)} collective-permute-done((bf16[3,48,768]{2,1,0:T(8,128)(2,1)S(1)}, bf16[3,48,768]{2,1,0:T(8,128)(2,1)S(1)}, u32[]{:S(2)}, u32[]{:S(2)}) %collective-permute-start.1) | collective-permute-done | bytes 221216 | tf_op jit(solution)/shard_map/ppermute | solution.py:44
  17.3 0.7 %copy-done.4 = bf16[3,48,768]{2,1,0:T(8,128)(2,1)} copy-done((bf16[3,48,768]{2,1,0:T(8,128)(2,1)}, bf16[3,48,768]{2,1,0:T(8,128)(2,1)S(1)}, u32[]{:S(2)}) %copy-start.4) | copy-done | bytes 221208
  18.0 4.7 %shard_map.82 = (f32[3,48,768]{2,1,0:T(8,128)}, bf16[8,3,20,90]{3,2,1,0:T(8,128)(2,1)}) custom-call(s32[588]{0:T(1024)} %reshape.27.basis_ref, s32[12]{0:T(128)} %step_ref.7, f32[12]{0:T(128)} %multiply_cosine_fusion.1.quad_ref, bf16[3,48,768]{2,1,0:T(8,128)(2,1)} %copy-done.3, bf16[3,48,768]{2,1,0:T(8,128)(2,1)} %copy-done, bf16[3,48,768]{2,1,0:T(8,128)(2,1)} %copy-done.4, ...), custom_call_target="tpu_custom_call" | custom-call | tf_op jit(solution)/shard_map/pallas_call | solution.py:311
  22.8 5.0 %all-to-all-start = ((bf16[8,3,20,90]{3,2,1,0:T(8,128)(2,1)}), bf16[8,3,20,90]{3,2,1,0:T(8,128)(2,1)S(1)}, u32[]{:S(2)}, u32[]{:S(2)}) async-start(bf16[8,3,20,90]{3,2,1,0:T(8,128)(2,1)} %get-tuple-element.7), calls=%async_computation | async-start | bytes 294912 | tf_op jit(solution)/shard_map/all_to_all | solution.py:321
  27.8 0.1 multiply_cosine_fusion
  27.9 0.7 reshape.32.weight_ref
  28.5 6.2 %all-to-all-done.fc_ref = bf16[8,3,20,90]{3,2,1,0:T(8,128)(2,1)S(1)} async-done(((bf16[8,3,20,90]{3,2,1,0:T(8,128)(2,1)}), bf16[8,3,20,90]{3,2,1,0:T(8,128)(2,1)S(1)}, u32[]{:S(2)}, u32[]{:S(2)}) %all-to-all-start) | async-done | bytes 86432 | tf_op jit(solution)/shard_map/all_to_all | solution.py:321
  34.8 0.7 copy-done.2
  35.4 2.6 %shard_map.83 = bf16[8,3,8,90]{3,2,1,0:T(8,128)(2,1)} custom-call(f32[48]{0:T(128)} %reshape.32.weight_ref, bf16[8,20]{1,0:T(8,128)(2,1)} %pad.37.sub_t_ref, bf16[8,3,20,90]{3,2,1,0:T(8,128)(2,1)} %copy-done.2, f32[3,20,90]{2,1,0:T(8,128)} %bitcast.19), custom_call_target="tpu_custom_call" | custom-call | tf_op jit(solution)/shard_map/pallas_call | solution.py:322
  38.0 3.3 %all-to-all-start.1 = ((bf16[8,3,8,90]{3,2,1,0:T(8,128)(2,1)}), bf16[8,3,8,90]{3,2,1,0:T(8,128)(2,1)S(1)}, u32[]{:S(2)}, u32[]{:S(2)}) async-start(bf16[8,3,8,90]{3,2,1,0:T(8,128)(2,1)} %shard_map.83), calls=%async_computation.1 | async-start | bytes 98304 | tf_op jit(solution)/shard_map/all_to_all | solution.py:328
  41.4 0.6 pad_convert_fusion.proj_t_ref
  42.0 5.1 %all-to-all-done.1.gc_ref = bf16[8,3,8,90]{3,2,1,0:T(8,128)(2,1)S(1)} async-done(((bf16[8,3,8,90]{3,2,1,0:T(8,128)(2,1)}), bf16[8,3,8,90]{3,2,1,0:T(8,128)(2,1)S(1)}, u32[]{:S(2)}, u32[]{:S(2)}) %all-to-all-start.1) | async-done | bytes 34592 | tf_op jit(solution)/shard_map/all_to_all | solution.py:328
  47.1 0.6 copy-done.7
  47.7 2.0 %shard_map.84.own_ref = bf16[3,48,768]{2,1,0:T(8,128)(2,1)} custom-call(bf16[8,3,8,90]{3,2,1,0:T(8,128)(2,1)} %copy-done.7, f32[3,48,768]{2,1,0:T(8,128)} %get-tuple-element.8.slope_ref, f32[48,8]{1,0:T(8,128)} %pad_convert_fusion.proj_t_ref), custom_call_target="tpu_custom_call" | custom-call | tf_op jit(solution)/shard_map/pallas_call | solution.py:330
  49.8 3.4 %collective-permute-start.3 = (bf16[3,48,768]{2,1,0:T(8,128)(2,1)}, bf16[3,48,768]{2,1,0:T(8,128)(2,1)S(1)}, u32[]{:S(2)}, u32[]{:S(2)}) collective-permute-start(bf16[3,48,768]{2,1,0:T(8,128)(2,1)} %shard_map.84.own_ref), channel_id=1, source_target_pairs={{0,1},{1,2},{2,3},{4,5},{5,6},{6,7},{8,9},{9,10},{10,11},{12,13},{... | collective-permute-start | bytes 663560 | tf_op jit(solution)/shard_map/ppermute | solution.py:43
  53.2 1.3 %collective-permute-start.2 = (bf16[3,48,768]{2,1,0:T(8,128)(2,1)}, bf16[3,48,768]{2,1,0:T(8,128)(2,1)S(1)}, u32[]{:S(2)}, u32[]{:S(2)}) collective-permute-start(bf16[3,48,768]{2,1,0:T(8,128)(2,1)} %shard_map.84.own_ref), channel_id=1, source_target_pairs={{1,0},{2,1},{3,2},{5,4},{6,5},{7,6},{9,8},{10,9},{11,10},{13,12},{... | collective-permute-start | bytes 663560 | tf_op jit(solution)/shard_map/ppermute | solution.py:44
  54.5 2.7 %shard_map.85.acc_in_ref = f32[3,48,768]{2,1,0:T(8,128)} custom-call(s32[588]{0:T(1024)} %reshape.27.basis_ref, s32[12]{0:T(128)} %step_ref.7, f32[12]{0:T(128)} %multiply_cosine_fusion.1.quad_ref, bf16[3,48,768]{2,1,0:T(8,128)(2,1)} %shard_map.84.own_ref, bf16[2,6,48,48]{3,2,1,0:T(8,128)(2,1)} %pad_maximum_fusion.1.table_ref), custom_call_target="tpu_custom_call" | custom-call | flops 222953472 | bytes 663552 | tf_op jit(solution)/shard_map/pallas_call | solution.py:338
  57.2 0.8 %collective-permute-done.3.prev_ref = bf16[3,48,768]{2,1,0:T(8,128)(2,1)S(1)} collective-permute-done((bf16[3,48,768]{2,1,0:T(8,128)(2,1)}, bf16[3,48,768]{2,1,0:T(8,128)(2,1)S(1)}, u32[]{:S(2)}, u32[]{:S(2)}) %collective-permute-start.3) | collective-permute-done | bytes 221216 | tf_op jit(solution)/shard_map/ppermute | solution.py:43
  58.0 0.7 %copy-done.6 = bf16[3,48,768]{2,1,0:T(8,128)(2,1)} copy-done((bf16[3,48,768]{2,1,0:T(8,128)(2,1)}, bf16[3,48,768]{2,1,0:T(8,128)(2,1)S(1)}, u32[]{:S(2)}) %copy-start.6) | copy-done | bytes 221208
  58.7 2.7 %shard_map.86.acc_in_ref = f32[3,48,768]{2,1,0:T(8,128)} custom-call(s32[588]{0:T(1024)} %reshape.27.basis_ref, s32[12]{0:T(128)} %step_ref.7, f32[12]{0:T(128)} %multiply_cosine_fusion.1.quad_ref, bf16[3,48,768]{2,1,0:T(8,128)(2,1)} %copy-done.6, f32[3,48,768]{2,1,0:T(8,128)} %shard_map.85.acc_in_ref, bf16[2,6,48,48]{3,2,1,0:T(8,128)(2,1)} %pad_maximum_fusion.1.table_ref), custom_call_target="tpu_custom_call" | custom-call | flops 222953472 | bytes 1105920 | tf_op jit(solution)/shard_map/pallas_call | solution.py:349
  61.4 2.0 %collective-permute-done.2.next_ref = bf16[3,48,768]{2,1,0:T(8,128)(2,1)S(1)} collective-permute-done((bf16[3,48,768]{2,1,0:T(8,128)(2,1)}, bf16[3,48,768]{2,1,0:T(8,128)(2,1)S(1)}, u32[]{:S(2)}, u32[]{:S(2)}) %collective-permute-start.2) | collective-permute-done | bytes 221216 | tf_op jit(solution)/shard_map/ppermute | solution.py:44
  63.4 0.7 %copy-done.5 = bf16[3,48,768]{2,1,0:T(8,128)(2,1)} copy-done((bf16[3,48,768]{2,1,0:T(8,128)(2,1)}, bf16[3,48,768]{2,1,0:T(8,128)(2,1)S(1)}, u32[]{:S(2)}) %copy-start.5) | copy-done | bytes 221208
  64.1 2.6 %shard_map.87 = bf16[3,45,720]{2,1,0:T(8,128)(2,1)} custom-call(s32[588]{0:T(1024)} %reshape.27.basis_ref, s32[12]{0:T(128)} %step_ref.7, f32[12]{0:T(128)} %multiply_cosine_fusion.1.quad_ref, bf16[3,48,768]{2,1,0:T(8,128)(2,1)} %copy-done.5, f32[3,48,768]{2,1,0:T(8,128)} %shard_map.86.acc_in_ref, bf16[2,6,48,48]{3,2,1,0:T(8,128)(2,1)} %pad_maximum_fusion.1.table_ref), custom_call_target="tpu_custom_call" | custom-call | tf_op jit(solution)/shard_map/pallas_call | solution.py:360
  (20 shorter events, 0.1 us)
Async XLA Ops:
  0.0 1.0 %copy-start.1 = (bf16[1,3,45,720]{3,2,1,0:T(8,128)(2,1)S(1)}, bf16[1,3,45,720]{3,2,1,0:T(8,128)(2,1)}, u32[]{:S(2)}) copy-start(bf16[1,3,45,720]{3,2,1,0:T(8,128)(2,1)} %param.8) | copy-start | bytes 583204
  1.0 6.9 %copy-start.10 = (bf16[5,45]{1,0:T(8,128)(2,1)S(1)}, bf16[5,45]{1,0:T(8,128)(2,1)}, u32[]{:S(2)}) copy-start(bf16[5,45]{1,0:T(8,128)(2,1)} %param.10) | copy-start | bytes 1354
  1.0 7.6 %copy-start.8 = (bf16[5,45,45]{2,1,0:T(8,128)(2,1)S(1)}, bf16[5,45,45]{2,1,0:T(8,128)(2,1)}, u32[]{:S(2)}) copy-start(bf16[5,45,45]{2,1,0:T(8,128)(2,1)} %param.9) | copy-start | bytes 60754
  1.1 7.8 %copy-start = (bf16[3,48,768]{2,1,0:T(8,128)(2,1)}, bf16[3,48,768]{2,1,0:T(8,128)(2,1)S(1)}, u32[]{:S(2)}) copy-start(bf16[3,48,768]{2,1,0:T(8,128)(2,1)S(1)} %pad_maximum_fusion.own_ref) | copy-start | bytes 663556
  1.1 11.9 %collective-permute-start = (bf16[3,48,768]{2,1,0:T(8,128)(2,1)S(1)}, bf16[3,48,768]{2,1,0:T(8,128)(2,1)S(1)}, u32[]{:S(2)}, u32[]{:S(2)}) collective-permute-start(bf16[3,48,768]{2,1,0:T(8,128)(2,1)S(1)} %pad_maximum_fusion.own_ref), channel_id=1, source_target_pairs={{0,1},{1,2},{2,3},{4,5},{5,6},{6,7},{8,9},{9,10},{10,11},{12,13},{... | collective-permute-start | bytes 663560 | tf_op jit(solution)/shard_map/ppermute | solution.py:43
  6.0 11.3 %collective-permute-start.1 = (bf16[3,48,768]{2,1,0:T(8,128)(2,1)S(1)}, bf16[3,48,768]{2,1,0:T(8,128)(2,1)S(1)}, u32[]{:S(2)}, u32[]{:S(2)}) collective-permute-start(bf16[3,48,768]{2,1,0:T(8,128)(2,1)S(1)} %pad_maximum_fusion.own_ref), channel_id=1, source_target_pairs={{1,0},{2,1},{3,2},{5,4},{6,5},{7,6},{9,8},{10,9},{11,10},{13,12},{... | collective-permute-start | bytes 663560 | tf_op jit(solution)/shard_map/ppermute | solution.py:44
  8.8 0.7 %copy-start.11 = (s32[12,49]{1,0:T(8,128)S(1)}, s32[12,49]{1,0:T(8,128)}, u32[]{:S(2)}) copy-start(s32[12,49]{1,0:T(8,128)} %param.13) | copy-start | bytes 7060
  8.8 1.4 %copy-start.12 = (bf16[4,5,5]{2,0,1:T(4,128)(2,1)S(1)}, bf16[4,5,5]{2,0,1:T(4,128)(2,1)}, u32[]{:S(2)}) copy-start(bf16[4,5,5]{2,0,1:T(4,128)(2,1)} %param.11) | copy-start | bytes 604
  9.5 2.2 %copy-start.9 = (f32[4,5,3,90]{3,0,2,1:T(4,128)S(1)}, f32[4,5,3,90]{3,0,2,1:T(4,128)}, u32[]{:S(2)}) copy-start(f32[4,5,3,90]{3,0,2,1:T(4,128)} %param.12) | copy-start | bytes 64804
  13.0 4.3 %copy-start.3 = (bf16[3,48,768]{2,1,0:T(8,128)(2,1)}, bf16[3,48,768]{2,1,0:T(8,128)(2,1)S(1)}, u32[]{:S(2)}) copy-start(bf16[3,48,768]{2,1,0:T(8,128)(2,1)S(1)} %collective-permute-done.prev_ref) | copy-start | bytes 663556
  17.3 0.7 %copy-start.4 = (bf16[3,48,768]{2,1,0:T(8,128)(2,1)}, bf16[3,48,768]{2,1,0:T(8,128)(2,1)S(1)}, u32[]{:S(2)}) copy-start(bf16[3,48,768]{2,1,0:T(8,128)(2,1)S(1)} %collective-permute-done.1.next_ref) | copy-start | bytes 663556
  22.8 5.0 %copy-start.13 = (f32[4]{0:T(128)S(1)}, f32[4]{0:T(128)}, u32[]{:S(2)}) copy-start(f32[4]{0:T(128)} %constant.23.clone) | copy-start | bytes 52
  22.8 12.0 %all-to-all-start = ((bf16[8,3,20,90]{3,2,1,0:T(8,128)(2,1)}), bf16[8,3,20,90]{3,2,1,0:T(8,128)(2,1)S(1)}, u32[]{:S(2)}, u32[]{:S(2)}) async-start(bf16[8,3,20,90]{3,2,1,0:T(8,128)(2,1)} %get-tuple-element.7), calls=%async_computation | async-start | bytes 294912 | tf_op jit(solution)/shard_map/all_to_all | solution.py:321
  34.8 0.7 copy-start.2
  38.0 9.1 %all-to-all-start.1 = ((bf16[8,3,8,90]{3,2,1,0:T(8,128)(2,1)}), bf16[8,3,8,90]{3,2,1,0:T(8,128)(2,1)S(1)}, u32[]{:S(2)}, u32[]{:S(2)}) async-start(bf16[8,3,8,90]{3,2,1,0:T(8,128)(2,1)} %shard_map.83), calls=%async_computation.1 | async-start | bytes 98304 | tf_op jit(solution)/shard_map/all_to_all | solution.py:328
  47.1 0.6 copy-start.7
  49.8 8.2 %collective-permute-start.3 = (bf16[3,48,768]{2,1,0:T(8,128)(2,1)}, bf16[3,48,768]{2,1,0:T(8,128)(2,1)S(1)}, u32[]{:S(2)}, u32[]{:S(2)}) collective-permute-start(bf16[3,48,768]{2,1,0:T(8,128)(2,1)} %shard_map.84.own_ref), channel_id=1, source_target_pairs={{0,1},{1,2},{2,3},{4,5},{5,6},{6,7},{8,9},{9,10},{10,11},{12,13},{... | collective-permute-start | bytes 663560 | tf_op jit(solution)/shard_map/ppermute | solution.py:43
  53.2 10.2 %collective-permute-start.2 = (bf16[3,48,768]{2,1,0:T(8,128)(2,1)}, bf16[3,48,768]{2,1,0:T(8,128)(2,1)S(1)}, u32[]{:S(2)}, u32[]{:S(2)}) collective-permute-start(bf16[3,48,768]{2,1,0:T(8,128)(2,1)} %shard_map.84.own_ref), channel_id=1, source_target_pairs={{1,0},{2,1},{3,2},{5,4},{6,5},{7,6},{9,8},{10,9},{11,10},{13,12},{... | collective-permute-start | bytes 663560 | tf_op jit(solution)/shard_map/ppermute | solution.py:44
  58.0 0.7 %copy-start.6 = (bf16[3,48,768]{2,1,0:T(8,128)(2,1)}, bf16[3,48,768]{2,1,0:T(8,128)(2,1)S(1)}, u32[]{:S(2)}) copy-start(bf16[3,48,768]{2,1,0:T(8,128)(2,1)S(1)} %collective-permute-done.3.prev_ref) | copy-start | bytes 663556
  63.4 0.7 %copy-start.5 = (bf16[3,48,768]{2,1,0:T(8,128)(2,1)}, bf16[3,48,768]{2,1,0:T(8,128)(2,1)S(1)}, u32[]{:S(2)}) copy-start(bf16[3,48,768]{2,1,0:T(8,128)(2,1)S(1)} %collective-permute-done.2.next_ref) | copy-start | bytes 663556

commit v11 on v10

--- a/solution.py
+++ b/solution.py
@@ -124,9 +124,10 @@
         forecast = jnp.dot(
             sub_ref[...], coarse, preferred_element_type=jnp.float32
         ).astype(jnp.bfloat16)
-        blocks, block = fc_ref.shape[0], fc_ref.shape[3]
+        blocks, block = fc_ref.shape[0], fc_ref.shape[2]
+        cells = forecast.shape[0]
         for q in range(blocks):
-            fc_ref[q, i] = forecast[:, q * block : (q + 1) * block]
+            fc_ref[q, i * cells : (i + 1) * cells] = forecast[:, q * block : (q + 1) * block]
 
 
 def split3(x):
@@ -138,7 +139,9 @@
 
 
 def score_kernel(subcells, weight_ref, sub_t_ref, fc_ref, truth_ref, out_ref):
-    members, rows, cells, block = fc_ref.shape
+    members, rows, cells, block = (
+        fc_ref.shape[0], truth_ref.shape[0], truth_ref.shape[1], fc_ref.shape[2]
+    )
     total_rows = weight_ref.shape[0] // subcells
     slot = 128
     lanes = members * slot
@@ -153,7 +156,9 @@
             scale = jnp.where(cell_sub == s, weight_ref[s * total_rows + g], scale)
         values = jnp.concatenate(
             [
-                jnp.concatenate([fc_ref[n, i].astype(jnp.float32), pad], axis=1)
+                jnp.concatenate(
+                    [fc_ref[n, i * cells : (i + 1) * cells].astype(jnp.float32), pad], axis=1
+                )
                 for n in range(members)
             ],
             axis=1,
@@ -312,7 +317,7 @@
         forward_kernel,
         out_shape=(
             jax.ShapeDtypeStruct((rows, cp, width_p), jnp.float32),
-            jax.ShapeDtypeStruct((blocks, rows, svp, block), jnp.bfloat16),
+            jax.ShapeDtypeStruct((blocks, rows * svp, block), jnp.bfloat16),
         ),
         in_specs=[smem(), smem(), smem()] + [vmem()] * 6,
         out_specs=(vmem(), vmem()),

time: 67.3 us -> 67.4 us (level)
  starting transfers between devices: 19.2 us -> 21.8 us
  waiting for transfers between devices: 18.5 us -> 16.5 us
    ppermute x2, starting transfers between devices: 8.26 us -> 10.2 us  [halo(): low = lax.ppermute(block[block.shape[0] - width:], axis_name, forward)]
    all_to_all x1, waiting for transfers between devices: 6.22 us -> 4.78 us  [on_device(): lax.all_to_all(fc, 'member', split_axis=0, concat_axis=0, tiled=True)]
    ppermute x2, waiting for transfers between devices: 6.3 us -> 5.07 us  [halo(): high = lax.ppermute(block[:width], axis_name, backward)]
    ppermute x2, waiting for transfers between devices: 0.84 us -> 1.55 us  [halo(): low = lax.ppermute(block[block.shape[0] - width:], axis_name, forward)]
where the time goes in v11:
time: 67.4 us; the launch traced here: 66.8 us
  starting transfers between devices  21.8 us (32%)
  Pallas kernels  17.4 us (26%)
  waiting for transfers between devices  16.5 us (24%)
  local copies, waits for them, and re-layouts  8.84 us (13%)
  other arithmetic  2.13 us (3%)
    ppermute x2, starting transfers between devices, halo(): low = lax.ppermute(block[block.shape[0] - width:], axis_name, forward)  10.2 us
    all_to_all x1, starting transfers between devices, on_device(): lax.all_to_all(fc, 'member', split_axis=0, concat_axis=0, tiled=True)  5.53 us
    all_to_all x1, waiting for transfers between devices, on_device(): lax.all_to_all(gc_owned, 'member', split_axis=0, concat_axis=0, tiled=True)  5.14 us
    ppermute x2, waiting for transfers between devices, halo(): high = lax.ppermute(block[:width], axis_name, backward)  5.07 us
    all_to_all x1, waiting for transfers between devices, on_device(): lax.all_to_all(fc, 'member', split_axis=0, concat_axis=0, tiled=True)  4.78 us
    pallas_call x1, Pallas kernels, on_device(): pl.pallas_call(forward_kernel, out_shape=(jax.ShapeDtypeStruct((rows, cp,...  4.68 us
    unnamed x32, local copies, waits for them, and re-layouts  3.82 us
    all_to_all x1, starting transfers between devices, on_device(): lax.all_to_all(gc_owned, 'member', split_axis=0, concat_axis=0, tiled=True)  3.34 us
  transfers between devices with their start and end apart: 6, of which 5 were waited for; matrix products, arithmetic and copies ran while one was open for 10% of the time, Pallas kernels for 8%

profile of v11, /device:TPU:0, one launch (start us, length us, event | category | flops | bytes accessed | tf_op | source)
XLA Modules:
  0.0 66.8 jit_solution(18308308779212193759)
XLA Ops:
  0.0 0.9 %pad_slice_fusion.1 = (bf16[3,48,24]{2,1,0:T(8,128)(2,1)S(1)}, bf16[3,48,24]{2,1,0:T(8,128)(2,1)S(1)}) fusion(bf16[3,45,720]{2,1,0:T(8,128)(2,1)} %bitcast.16), kind=kLoop, calls=%fused_computation.10 | loop fusion | bytes 208224 | tf_op jit(solution)/shard_map/slice | solution.py:29
  0.9 0.0 copy-done.1
  1.0 0.0 copy-start.10
  1.0 0.0 copy-start.11
  1.0 0.0 copy-start.12
  1.0 0.1 pad_maximum_fusion.own_ref
  1.1 0.0 copy-start
  1.1 0.0 copy-start.8
  1.2 1.4 %collective-permute-start.1 = (bf16[3,48,768]{2,1,0:T(8,128)(2,1)S(1)}, bf16[3,48,768]{2,1,0:T(8,128)(2,1)S(1)}, u32[]{:S(2)}, u32[]{:S(2)}) collective-permute-start(bf16[3,48,768]{2,1,0:T(8,128)(2,1)S(1)} %pad_maximum_fusion.own_ref), channel_id=1, source_target_pairs={{1,0},{2,1},{3,2},{5,4},{6,5},{7,6},{9,8},{10,9},{11,10},{13,12},{... | collective-permute-start | bytes 663560 | tf_op jit(solution)/shard_map/ppermute | solution.py:44
  2.6 5.5 %collective-permute-start = (bf16[3,48,768]{2,1,0:T(8,128)(2,1)S(1)}, bf16[3,48,768]{2,1,0:T(8,128)(2,1)S(1)}, u32[]{:S(2)}, u32[]{:S(2)}) collective-permute-start(bf16[3,48,768]{2,1,0:T(8,128)(2,1)S(1)} %pad_maximum_fusion.own_ref), channel_id=1, source_target_pairs={{0,1},{1,2},{2,3},{4,5},{5,6},{6,7},{8,9},{9,10},{10,11},{12,13},{... | collective-permute-start | bytes 663560 | tf_op jit(solution)/shard_map/ppermute | solution.py:43
  8.1 0.6 multiply_cosine_fusion.1.quad_ref
  8.7 0.0 copy-done.10
  8.7 0.6 pad.53.proj_ref
  9.3 0.1 copy.21
  9.4 0.7 %reshape.27.basis_ref = s32[588]{0:T(1024)} reshape(s32[12,49]{1,0:T(8,128)S(1)} %copy-done.11) | data formatting | bytes 4704 | tf_op jit(solution)/shard_map/reshape | solution.py:308
  10.1 0.1 copy.15
  10.2 0.1 reshape.28
  10.3 0.1 copy.18
  10.4 0.6 pad.43.sub_ref
  11.0 0.1 copy.16
  11.2 0.1 copy.17
  11.3 0.7 %pad_maximum_fusion.1.table_ref = bf16[2,6,48,48]{3,2,1,0:T(8,128)(2,1)} fusion(bf16[1,6,48,48]{3,2,1,0:T(8,128)(2,1)S(1)} %get-tuple-element.12, bf16[1,6,48,48]{3,2,1,0:T(8,128)(2,1)S(1)} %copy.17), kind=kLoop, calls=%fused_computation.1 | loop fusion | flops 27648 | bytes 110592 | tf_op jit(solution)/shard_map/stack | solution.py:307
  12.0 0.0 collective-permute-done.1.next_ref
  12.0 0.7 %collective-permute-done.prev_ref = bf16[3,48,768]{2,1,0:T(8,128)(2,1)S(1)} collective-permute-done((bf16[3,48,768]{2,1,0:T(8,128)(2,1)S(1)}, bf16[3,48,768]{2,1,0:T(8,128)(2,1)S(1)}, u32[]{:S(2)}, u32[]{:S(2)}) %collective-permute-start) | collective-permute-done | bytes 221216 | tf_op jit(solution)/shard_map/ppermute | solution.py:43
  12.7 0.7 %copy-done.4 = bf16[3,48,768]{2,1,0:T(8,128)(2,1)} copy-done((bf16[3,48,768]{2,1,0:T(8,128)(2,1)}, bf16[3,48,768]{2,1,0:T(8,128)(2,1)S(1)}, u32[]{:S(2)}) %copy-start.4) | copy-done | bytes 221208
  13.4 4.7 %shard_map.82 = (f32[3,48,768]{2,1,0:T(8,128)}, bf16[8,60,90]{2,1,0:T(8,128)(2,1)}) custom-call(s32[588]{0:T(1024)} %reshape.27.basis_ref, s32[12]{0:T(128)} %step_ref.7, f32[12]{0:T(128)} %multiply_cosine_fusion.1.quad_ref, bf16[3,48,768]{2,1,0:T(8,128)(2,1)} %copy-done.4, bf16[3,48,768]{2,1,0:T(8,128)(2,1)} %copy-done, bf16[3,48,768]{2,1,0:T(8,128)(2,1)} %copy-done.3, ...), custom_call_target="tpu_custom_call" | custom-call | tf_op jit(solution)/shard_map/pallas_call | solution.py:316
  18.1 5.5 %all-to-all-start = ((bf16[8,60,90]{2,1,0:T(8,128)(2,1)}), bf16[8,60,90]{2,1,0:T(8,128)(2,1)S(1)}, u32[]{:S(2)}, u32[]{:S(2)}) async-start(bf16[8,60,90]{2,1,0:T(8,128)(2,1)} %get-tuple-element.7), calls=%async_computation | async-start | bytes 262144 | tf_op jit(solution)/shard_map/all_to_all | solution.py:326
  23.6 0.1 multiply_cosine_fusion
  23.8 0.7 reshape.32.weight_ref
  24.4 0.6 pad.37.sub_t_ref
  25.0 0.6 copy.23
  25.6 4.8 %all-to-all-done.fc_ref = bf16[8,60,90]{2,1,0:T(8,128)(2,1)S(1)} async-done(((bf16[8,60,90]{2,1,0:T(8,128)(2,1)}), bf16[8,60,90]{2,1,0:T(8,128)(2,1)S(1)}, u32[]{:S(2)}, u32[]{:S(2)}) %all-to-all-start) | async-done | bytes 86432 | tf_op jit(solution)/shard_map/all_to_all | solution.py:326
  30.4 0.7 copy-done.2
  31.1 2.6 %shard_map.83 = bf16[8,3,8,90]{3,2,1,0:T(8,128)(2,1)} custom-call(f32[48]{0:T(128)} %reshape.32.weight_ref, bf16[8,20]{1,0:T(8,128)(2,1)} %pad.37.sub_t_ref, bf16[8,60,90]{2,1,0:T(8,128)(2,1)} %copy-done.2, f32[3,20,90]{2,1,0:T(8,128)} %bitcast.19), custom_call_target="tpu_custom_call" | custom-call | tf_op jit(solution)/shard_map/pallas_call | solution.py:327
  33.7 3.3 %all-to-all-start.1 = ((bf16[8,3,8,90]{3,2,1,0:T(8,128)(2,1)}), bf16[8,3,8,90]{3,2,1,0:T(8,128)(2,1)S(1)}, u32[]{:S(2)}, u32[]{:S(2)}) async-start(bf16[8,3,8,90]{3,2,1,0:T(8,128)(2,1)} %shard_map.83), calls=%async_computation.1 | async-start | bytes 98304 | tf_op jit(solution)/shard_map/all_to_all | solution.py:333
  37.1 0.6 pad_convert_fusion.proj_t_ref
  37.7 5.1 %all-to-all-done.1.gc_ref = bf16[8,3,8,90]{3,2,1,0:T(8,128)(2,1)S(1)} async-done(((bf16[8,3,8,90]{3,2,1,0:T(8,128)(2,1)}), bf16[8,3,8,90]{3,2,1,0:T(8,128)(2,1)S(1)}, u32[]{:S(2)}, u32[]{:S(2)}) %all-to-all-start.1) | async-done | bytes 34592 | tf_op jit(solution)/shard_map/all_to_all | solution.py:333
  42.8 0.6 copy-done.7
  43.5 2.0 %shard_map.84.own_ref = bf16[3,48,768]{2,1,0:T(8,128)(2,1)} custom-call(bf16[8,3,8,90]{3,2,1,0:T(8,128)(2,1)} %copy-done.7, f32[3,48,768]{2,1,0:T(8,128)} %get-tuple-element.8.slope_ref, f32[48,8]{1,0:T(8,128)} %pad_convert_fusion.proj_t_ref), custom_call_target="tpu_custom_call" | custom-call | tf_op jit(solution)/shard_map/pallas_call | solution.py:335
  45.5 4.7 %collective-permute-start.3 = (bf16[3,48,768]{2,1,0:T(8,128)(2,1)}, bf16[3,48,768]{2,1,0:T(8,128)(2,1)S(1)}, u32[]{:S(2)}, u32[]{:S(2)}) collective-permute-start(bf16[3,48,768]{2,1,0:T(8,128)(2,1)} %shard_map.84.own_ref), channel_id=1, source_target_pairs={{0,1},{1,2},{2,3},{4,5},{5,6},{6,7},{8,9},{9,10},{10,11},{12,13},{... | collective-permute-start | bytes 663560 | tf_op jit(solution)/shard_map/ppermute | solution.py:43
  50.2 1.3 %collective-permute-start.2 = (bf16[3,48,768]{2,1,0:T(8,128)(2,1)}, bf16[3,48,768]{2,1,0:T(8,128)(2,1)S(1)}, u32[]{:S(2)}, u32[]{:S(2)}) collective-permute-start(bf16[3,48,768]{2,1,0:T(8,128)(2,1)} %shard_map.84.own_ref), channel_id=1, source_target_pairs={{1,0},{2,1},{3,2},{5,4},{6,5},{7,6},{9,8},{10,9},{11,10},{13,12},{... | collective-permute-start | bytes 663560 | tf_op jit(solution)/shard_map/ppermute | solution.py:44
  51.5 2.7 %shard_map.85.acc_in_ref = f32[3,48,768]{2,1,0:T(8,128)} custom-call(s32[588]{0:T(1024)} %reshape.27.basis_ref, s32[12]{0:T(128)} %step_ref.7, f32[12]{0:T(128)} %multiply_cosine_fusion.1.quad_ref, bf16[3,48,768]{2,1,0:T(8,128)(2,1)} %shard_map.84.own_ref, bf16[2,6,48,48]{3,2,1,0:T(8,128)(2,1)} %pad_maximum_fusion.1.table_ref), custom_call_target="tpu_custom_call" | custom-call | flops 222953472 | bytes 663552 | tf_op jit(solution)/shard_map/pallas_call | solution.py:343
  54.2 0.8 %collective-permute-done.3.prev_ref = bf16[3,48,768]{2,1,0:T(8,128)(2,1)S(1)} collective-permute-done((bf16[3,48,768]{2,1,0:T(8,128)(2,1)}, bf16[3,48,768]{2,1,0:T(8,128)(2,1)S(1)}, u32[]{:S(2)}, u32[]{:S(2)}) %collective-permute-start.3) | collective-permute-done | bytes 221216 | tf_op jit(solution)/shard_map/ppermute | solution.py:43
  55.1 0.7 %copy-done.6 = bf16[3,48,768]{2,1,0:T(8,128)(2,1)} copy-done((bf16[3,48,768]{2,1,0:T(8,128)(2,1)}, bf16[3,48,768]{2,1,0:T(8,128)(2,1)S(1)}, u32[]{:S(2)}) %copy-start.6) | copy-done | bytes 221208
  55.8 2.7 %shard_map.86.acc_in_ref = f32[3,48,768]{2,1,0:T(8,128)} custom-call(s32[588]{0:T(1024)} %reshape.27.basis_ref, s32[12]{0:T(128)} %step_ref.7, f32[12]{0:T(128)} %multiply_cosine_fusion.1.quad_ref, bf16[3,48,768]{2,1,0:T(8,128)(2,1)} %copy-done.6, f32[3,48,768]{2,1,0:T(8,128)} %shard_map.85.acc_in_ref, bf16[2,6,48,48]{3,2,1,0:T(8,128)(2,1)} %pad_maximum_fusion.1.table_ref), custom_call_target="tpu_custom_call" | custom-call | flops 222953472 | bytes 1105920 | tf_op jit(solution)/shard_map/pallas_call | solution.py:354
  58.5 5.1 %collective-permute-done.2.next_ref = bf16[3,48,768]{2,1,0:T(8,128)(2,1)S(1)} collective-permute-done((bf16[3,48,768]{2,1,0:T(8,128)(2,1)}, bf16[3,48,768]{2,1,0:T(8,128)(2,1)S(1)}, u32[]{:S(2)}, u32[]{:S(2)}) %collective-permute-start.2) | collective-permute-done | bytes 221216 | tf_op jit(solution)/shard_map/ppermute | solution.py:44
  63.5 0.7 %copy-done.5 = bf16[3,48,768]{2,1,0:T(8,128)(2,1)} copy-done((bf16[3,48,768]{2,1,0:T(8,128)(2,1)}, bf16[3,48,768]{2,1,0:T(8,128)(2,1)S(1)}, u32[]{:S(2)}) %copy-start.5) | copy-done | bytes 221208
  64.2 2.6 %shard_map.87 = bf16[3,45,720]{2,1,0:T(8,128)(2,1)} custom-call(s32[588]{0:T(1024)} %reshape.27.basis_ref, s32[12]{0:T(128)} %step_ref.7, f32[12]{0:T(128)} %multiply_cosine_fusion.1.quad_ref, bf16[3,48,768]{2,1,0:T(8,128)(2,1)} %copy-done.5, f32[3,48,768]{2,1,0:T(8,128)} %shard_map.86.acc_in_ref, bf16[2,6,48,48]{3,2,1,0:T(8,128)(2,1)} %pad_maximum_fusion.1.table_ref), custom_call_target="tpu_custom_call" | custom-call | tf_op jit(solution)/shard_map/pallas_call | solution.py:365
  (20 shorter events, 0.1 us)
Async XLA Ops:
  0.0 1.0 %copy-start.1 = (bf16[1,3,45,720]{3,2,1,0:T(8,128)(2,1)S(1)}, bf16[1,3,45,720]{3,2,1,0:T(8,128)(2,1)}, u32[]{:S(2)}) copy-start(bf16[1,3,45,720]{3,2,1,0:T(8,128)(2,1)} %param.8) | copy-start | bytes 583204
  1.0 7.7 %copy-start.10 = (bf16[5,45]{1,0:T(8,128)(2,1)S(1)}, bf16[5,45]{1,0:T(8,128)(2,1)}, u32[]{:S(2)}) copy-start(bf16[5,45]{1,0:T(8,128)(2,1)} %param.10) | copy-start | bytes 1354
  1.0 8.4 %copy-start.11 = (s32[12,49]{1,0:T(8,128)S(1)}, s32[12,49]{1,0:T(8,128)}, u32[]{:S(2)}) copy-start(s32[12,49]{1,0:T(8,128)} %param.13) | copy-start | bytes 7060
  1.0 9.1 %copy-start.12 = (bf16[4,5,5]{2,0,1:T(4,128)(2,1)S(1)}, bf16[4,5,5]{2,0,1:T(4,128)(2,1)}, u32[]{:S(2)}) copy-start(bf16[4,5,5]{2,0,1:T(4,128)(2,1)} %param.11) | copy-start | bytes 604
  1.1 10.2 %copy-start = (bf16[3,48,768]{2,1,0:T(8,128)(2,1)}, bf16[3,48,768]{2,1,0:T(8,128)(2,1)S(1)}, u32[]{:S(2)}) copy-start(bf16[3,48,768]{2,1,0:T(8,128)(2,1)S(1)} %pad_maximum_fusion.own_ref) | copy-start | bytes 663556
  1.1 9.9 %copy-start.8 = (bf16[5,45,45]{2,1,0:T(8,128)(2,1)S(1)}, bf16[5,45,45]{2,1,0:T(8,128)(2,1)}, u32[]{:S(2)}) copy-start(bf16[5,45,45]{2,1,0:T(8,128)(2,1)} %param.9) | copy-start | bytes 60754
  1.2 10.9 %collective-permute-start.1 = (bf16[3,48,768]{2,1,0:T(8,128)(2,1)S(1)}, bf16[3,48,768]{2,1,0:T(8,128)(2,1)S(1)}, u32[]{:S(2)}, u32[]{:S(2)}) collective-permute-start(bf16[3,48,768]{2,1,0:T(8,128)(2,1)S(1)} %pad_maximum_fusion.own_ref), channel_id=1, source_target_pairs={{1,0},{2,1},{3,2},{5,4},{6,5},{7,6},{9,8},{10,9},{11,10},{13,12},{... | collective-permute-start | bytes 663560 | tf_op jit(solution)/shard_map/ppermute | solution.py:44
  2.6 10.1 %collective-permute-start = (bf16[3,48,768]{2,1,0:T(8,128)(2,1)S(1)}, bf16[3,48,768]{2,1,0:T(8,128)(2,1)S(1)}, u32[]{:S(2)}, u32[]{:S(2)}) collective-permute-start(bf16[3,48,768]{2,1,0:T(8,128)(2,1)S(1)} %pad_maximum_fusion.own_ref), channel_id=1, source_target_pairs={{0,1},{1,2},{2,3},{4,5},{5,6},{6,7},{8,9},{9,10},{10,11},{12,13},{... | collective-permute-start | bytes 663560 | tf_op jit(solution)/shard_map/ppermute | solution.py:43
  12.0 0.7 %copy-start.3 = (bf16[3,48,768]{2,1,0:T(8,128)(2,1)}, bf16[3,48,768]{2,1,0:T(8,128)(2,1)S(1)}, u32[]{:S(2)}) copy-start(bf16[3,48,768]{2,1,0:T(8,128)(2,1)S(1)} %collective-permute-done.1.next_ref) | copy-start | bytes 663556
  12.7 0.7 %copy-start.4 = (bf16[3,48,768]{2,1,0:T(8,128)(2,1)}, bf16[3,48,768]{2,1,0:T(8,128)(2,1)S(1)}, u32[]{:S(2)}) copy-start(bf16[3,48,768]{2,1,0:T(8,128)(2,1)S(1)} %collective-permute-done.prev_ref) | copy-start | bytes 663556
  18.1 5.5 %copy-start.13 = (f32[4]{0:T(128)S(1)}, f32[4]{0:T(128)}, u32[]{:S(2)}) copy-start(f32[4]{0:T(128)} %constant.23.clone) | copy-start | bytes 52
  18.1 6.9 %copy-start.9 = (f32[4,5,3,90]{3,0,2,1:T(4,128)S(1)}, f32[4,5,3,90]{3,0,2,1:T(4,128)}, u32[]{:S(2)}) copy-start(f32[4,5,3,90]{3,0,2,1:T(4,128)} %param.12) | copy-start | bytes 64804
  18.1 12.3 %all-to-all-start = ((bf16[8,60,90]{2,1,0:T(8,128)(2,1)}), bf16[8,60,90]{2,1,0:T(8,128)(2,1)S(1)}, u32[]{:S(2)}, u32[]{:S(2)}) async-start(bf16[8,60,90]{2,1,0:T(8,128)(2,1)} %get-tuple-element.7), calls=%async_computation | async-start | bytes 262144 | tf_op jit(solution)/shard_map/all_to_all | solution.py:326
  30.4 0.7 copy-start.2
  33.7 9.1 %all-to-all-start.1 = ((bf16[8,3,8,90]{3,2,1,0:T(8,128)(2,1)}), bf16[8,3,8,90]{3,2,1,0:T(8,128)(2,1)S(1)}, u32[]{:S(2)}, u32[]{:S(2)}) async-start(bf16[8,3,8,90]{3,2,1,0:T(8,128)(2,1)} %shard_map.83), calls=%async_computation.1 | async-start | bytes 98304 | tf_op jit(solution)/shard_map/all_to_all | solution.py:333
  42.8 0.6 copy-start.7
  45.5 9.6 %collective-permute-start.3 = (bf16[3,48,768]{2,1,0:T(8,128)(2,1)}, bf16[3,48,768]{2,1,0:T(8,128)(2,1)S(1)}, u32[]{:S(2)}, u32[]{:S(2)}) collective-permute-start(bf16[3,48,768]{2,1,0:T(8,128)(2,1)} %shard_map.84.own_ref), channel_id=1, source_target_pairs={{0,1},{1,2},{2,3},{4,5},{5,6},{6,7},{8,9},{9,10},{10,11},{12,13},{... | collective-permute-start | bytes 663560 | tf_op jit(solution)/shard_map/ppermute | solution.py:43
  50.2 13.3 %collective-permute-start.2 = (bf16[3,48,768]{2,1,0:T(8,128)(2,1)}, bf16[3,48,768]{2,1,0:T(8,128)(2,1)S(1)}, u32[]{:S(2)}, u32[]{:S(2)}) collective-permute-start(bf16[3,48,768]{2,1,0:T(8,128)(2,1)} %shard_map.84.own_ref), channel_id=1, source_target_pairs={{1,0},{2,1},{3,2},{5,4},{6,5},{7,6},{9,8},{10,9},{11,10},{13,12},{... | collective-permute-start | bytes 663560 | tf_op jit(solution)/shard_map/ppermute | solution.py:44
  55.1 0.7 %copy-start.6 = (bf16[3,48,768]{2,1,0:T(8,128)(2,1)}, bf16[3,48,768]{2,1,0:T(8,128)(2,1)S(1)}, u32[]{:S(2)}) copy-start(bf16[3,48,768]{2,1,0:T(8,128)(2,1)S(1)} %collective-permute-done.3.prev_ref) | copy-start | bytes 663556
  63.5 0.7 %copy-start.5 = (bf16[3,48,768]{2,1,0:T(8,128)(2,1)}, bf16[3,48,768]{2,1,0:T(8,128)(2,1)S(1)}, u32[]{:S(2)}) copy-start(bf16[3,48,768]{2,1,0:T(8,128)(2,1)S(1)} %collective-permute-done.2.next_ref) | copy-start | bytes 663556

commit v12 on v10

--- a/solution.py
+++ b/solution.py
@@ -179,19 +179,19 @@
 
 
 def grad_filtered_kernel(gc_ref, slope_ref, proj_t_ref, out_ref):
-    blocks, rows = gc_ref.shape[0], gc_ref.shape[1]
+    blocks = gc_ref.shape[0]
     width_p = slope_ref.shape[2]
-    for i in range(rows):
-        row = jnp.concatenate([gc_ref[q, i] for q in range(blocks)], axis=1)
-        width = row.shape[1]
-        extra = width_p - width
-        lo = extra // 2
-        hi = extra - lo
-        ring = jnp.concatenate([row, row[:, :lo], row[:, width - hi :]], axis=1)
-        grad_act = jnp.dot(
-            proj_t_ref[...], ring.astype(jnp.float32), preferred_element_type=jnp.float32
-        )
-        out_ref[i] = (grad_act * slope_ref[i]).astype(jnp.bfloat16)
+    i = pl.program_id(0)
+    row = jnp.concatenate([gc_ref[q, i] for q in range(blocks)], axis=1)
+    width = row.shape[1]
+    extra = width_p - width
+    lo = extra // 2
+    hi = extra - lo
+    ring = jnp.concatenate([row, row[:, :lo], row[:, width - hi :]], axis=1)
+    grad_act = jnp.dot(
+        proj_t_ref[...], ring.astype(jnp.float32), preferred_element_type=jnp.float32
+    )
+    out_ref[0] = (grad_act * slope_ref[0]).astype(jnp.bfloat16)
 
 
 def backward_terms(basis_ref, step_ref, quad_ref, table_ref, rows, sources, acc):
@@ -330,8 +330,13 @@
     grad_filtered = pl.pallas_call(
         grad_filtered_kernel,
         out_shape=jax.ShapeDtypeStruct((rows, cp, width_p), jnp.bfloat16),
-        in_specs=[vmem()] * 3,
-        out_specs=vmem(),
+        grid=(rows,),
+        in_specs=[
+            pl.BlockSpec(gc_home.shape, lambda i: (0, 0, 0, 0)),
+            pl.BlockSpec((1, cp, width_p), lambda i: (i, 0, 0)),
+            pl.BlockSpec(proj_t.shape, lambda i: (0, 0)),
+        ],
+        out_specs=pl.BlockSpec((1, cp, width_p), lambda i: (i, 0, 0)),
     )(gc_home, slope, proj_t)
 
     g_low, g_high = halo(grad_filtered, "lat", HALF)

time: 67.3 us -> 68.3 us (1.015)
  Pallas kernels: 17.3 us -> 18.3 us
    pallas_call x1, Pallas kernels: 2.05 us -> 3.03 us  [on_device(): pl.pallas_call(grad_filtered_kernel, out_shape=jax.ShapeDtypeStruct((rows...]
where the time goes in v12:
time: 68.3 us; the launch traced here: 67.7 us
  starting transfers between devices  19.2 us (28%)
  waiting for transfers between devices  18.5 us (27%)
  Pallas kernels  18.3 us (27%)
  local copies, waits for them, and re-layouts  9.41 us (14%)
  other arithmetic  2.13 us (3%)
    ppermute x2, starting transfers between devices, halo(): low = lax.ppermute(block[block.shape[0] - width:], axis_name, forward)  8.25 us
    ppermute x2, waiting for transfers between devices, halo(): high = lax.ppermute(block[:width], axis_name, backward)  6.29 us
    all_to_all x1, waiting for transfers between devices, on_device(): lax.all_to_all(fc, 'member', split_axis=0, concat_axis=0, tiled=True)  6.22 us
    all_to_all x1, waiting for transfers between devices, on_device(): lax.all_to_all(gc_owned, 'member', split_axis=0, concat_axis=0, tiled=True)  5.14 us
    all_to_all x1, starting transfers between devices, on_device(): lax.all_to_all(fc, 'member', split_axis=0, concat_axis=0, tiled=True)  5.01 us
    pallas_call x1, Pallas kernels, on_device(): pl.pallas_call(forward_kernel, out_shape=(jax.ShapeDtypeStruct((rows, cp,...  4.7 us
    unnamed x32, local copies, waits for them, and re-layouts  4.39 us
    all_to_all x1, starting transfers between devices, on_device(): lax.all_to_all(gc_owned, 'member', split_axis=0, concat_axis=0, tiled=True)  3.34 us
  transfers between devices with their start and end apart: 6, of which 5 were waited for; matrix products, arithmetic and copies ran while one was open for 10% of the time, Pallas kernels for 8%

profile of v12, /device:TPU:0, one launch (start us, length us, event | category | flops | bytes accessed | tf_op | source)
XLA Modules:
  0.0 67.7 jit_solution(7400919782586272921)
XLA Ops:
  0.0 0.9 %pad_slice_fusion.1 = (bf16[3,48,24]{2,1,0:T(8,128)(2,1)S(1)}, bf16[3,48,24]{2,1,0:T(8,128)(2,1)S(1)}) fusion(bf16[3,45,720]{2,1,0:T(8,128)(2,1)} %bitcast.16), kind=kLoop, calls=%fused_computation.10 | loop fusion | bytes 208224 | tf_op jit(solution)/shard_map/slice | solution.py:29
  0.9 0.0 copy-done.1
  1.0 0.0 copy-start.10
  1.0 0.0 copy-start.8
  1.0 0.1 pad_maximum_fusion.own_ref
  1.1 0.0 copy-start
  1.1 4.9 %collective-permute-start = (bf16[3,48,768]{2,1,0:T(8,128)(2,1)S(1)}, bf16[3,48,768]{2,1,0:T(8,128)(2,1)S(1)}, u32[]{:S(2)}, u32[]{:S(2)}) collective-permute-start(bf16[3,48,768]{2,1,0:T(8,128)(2,1)S(1)} %pad_maximum_fusion.own_ref), channel_id=1, source_target_pairs={{0,1},{1,2},{2,3},{4,5},{5,6},{6,7},{8,9},{9,10},{10,11},{12,13},{... | collective-permute-start | bytes 663560 | tf_op jit(solution)/shard_map/ppermute | solution.py:43
  6.0 1.3 %collective-permute-start.1 = (bf16[3,48,768]{2,1,0:T(8,128)(2,1)S(1)}, bf16[3,48,768]{2,1,0:T(8,128)(2,1)S(1)}, u32[]{:S(2)}, u32[]{:S(2)}) collective-permute-start(bf16[3,48,768]{2,1,0:T(8,128)(2,1)S(1)} %pad_maximum_fusion.own_ref), channel_id=1, source_target_pairs={{1,0},{2,1},{3,2},{5,4},{6,5},{7,6},{9,8},{10,9},{11,10},{13,12},{... | collective-permute-start | bytes 663560 | tf_op jit(solution)/shard_map/ppermute | solution.py:44
  7.3 0.6 multiply_cosine_fusion.1.quad_ref
  7.9 0.6 pad.53.proj_ref
  8.5 0.1 copy.21
  8.6 0.1 copy.16
  8.8 0.0 copy-start.11
  8.8 0.0 copy-start.12
  8.8 0.1 copy.17
  9.0 0.6 copy-done.11
  9.5 0.7 reshape.27.basis_ref
  10.2 0.1 copy.15
  10.3 0.1 reshape.28
  10.4 0.1 copy.18
  10.5 0.6 pad.43.sub_ref
  11.1 0.6 pad.37.sub_t_ref
  11.7 0.6 copy.23
  12.3 0.7 pad_maximum_fusion.1.table_ref
  13.0 0.0 collective-permute-done.prev_ref
  13.0 4.3 %collective-permute-done.1.next_ref = bf16[3,48,768]{2,1,0:T(8,128)(2,1)S(1)} collective-permute-done((bf16[3,48,768]{2,1,0:T(8,128)(2,1)S(1)}, bf16[3,48,768]{2,1,0:T(8,128)(2,1)S(1)}, u32[]{:S(2)}, u32[]{:S(2)}) %collective-permute-start.1) | collective-permute-done | bytes 221216 | tf_op jit(solution)/shard_map/ppermute | solution.py:44
  17.3 0.7 %copy-done.4 = bf16[3,48,768]{2,1,0:T(8,128)(2,1)} copy-done((bf16[3,48,768]{2,1,0:T(8,128)(2,1)}, bf16[3,48,768]{2,1,0:T(8,128)(2,1)S(1)}, u32[]{:S(2)}) %copy-start.4) | copy-done | bytes 221208
  18.0 4.7 %shard_map.82 = (f32[3,48,768]{2,1,0:T(8,128)}, bf16[8,3,20,90]{3,2,1,0:T(8,128)(2,1)}) custom-call(s32[588]{0:T(1024)} %reshape.27.basis_ref, s32[12]{0:T(128)} %step_ref.7, f32[12]{0:T(128)} %multiply_cosine_fusion.1.quad_ref, bf16[3,48,768]{2,1,0:T(8,128)(2,1)} %copy-done.3, bf16[3,48,768]{2,1,0:T(8,128)(2,1)} %copy-done, bf16[3,48,768]{2,1,0:T(8,128)(2,1)} %copy-done.4, ...), custom_call_target="tpu_custom_call" | custom-call | tf_op jit(solution)/shard_map/pallas_call | solution.py:311
  22.7 5.0 %all-to-all-start = ((bf16[8,3,20,90]{3,2,1,0:T(8,128)(2,1)}), bf16[8,3,20,90]{3,2,1,0:T(8,128)(2,1)S(1)}, u32[]{:S(2)}, u32[]{:S(2)}) async-start(bf16[8,3,20,90]{3,2,1,0:T(8,128)(2,1)} %get-tuple-element.7), calls=%async_computation | async-start | bytes 294912 | tf_op jit(solution)/shard_map/all_to_all | solution.py:321
  27.8 0.1 multiply_cosine_fusion
  27.9 0.7 reshape.32.weight_ref
  28.5 6.2 %all-to-all-done.fc_ref = bf16[8,3,20,90]{3,2,1,0:T(8,128)(2,1)S(1)} async-done(((bf16[8,3,20,90]{3,2,1,0:T(8,128)(2,1)}), bf16[8,3,20,90]{3,2,1,0:T(8,128)(2,1)S(1)}, u32[]{:S(2)}, u32[]{:S(2)}) %all-to-all-start) | async-done | bytes 86432 | tf_op jit(solution)/shard_map/all_to_all | solution.py:321
  34.8 0.7 copy-done.2
  35.4 2.6 %shard_map.83 = bf16[8,3,8,90]{3,2,1,0:T(8,128)(2,1)} custom-call(f32[48]{0:T(128)} %reshape.32.weight_ref, bf16[8,20]{1,0:T(8,128)(2,1)} %pad.37.sub_t_ref, bf16[8,3,20,90]{3,2,1,0:T(8,128)(2,1)} %copy-done.2, f32[3,20,90]{2,1,0:T(8,128)} %bitcast.19), custom_call_target="tpu_custom_call" | custom-call | tf_op jit(solution)/shard_map/pallas_call | solution.py:322
  38.0 3.3 %all-to-all-start.1 = ((bf16[8,3,8,90]{3,2,1,0:T(8,128)(2,1)}), bf16[8,3,8,90]{3,2,1,0:T(8,128)(2,1)S(1)}, u32[]{:S(2)}, u32[]{:S(2)}) async-start(bf16[8,3,8,90]{3,2,1,0:T(8,128)(2,1)} %shard_map.83), calls=%async_computation.1 | async-start | bytes 98304 | tf_op jit(solution)/shard_map/all_to_all | solution.py:328
  41.4 0.6 pad_convert_fusion.proj_t_ref
  42.0 5.1 %all-to-all-done.1.gc_ref = bf16[8,3,8,90]{3,2,1,0:T(8,128)(2,1)S(1)} async-done(((bf16[8,3,8,90]{3,2,1,0:T(8,128)(2,1)}), bf16[8,3,8,90]{3,2,1,0:T(8,128)(2,1)S(1)}, u32[]{:S(2)}, u32[]{:S(2)}) %all-to-all-start.1) | async-done | bytes 34592 | tf_op jit(solution)/shard_map/all_to_all | solution.py:328
  47.1 0.6 copy-done.7
  47.7 3.0 %shard_map.84.own_ref = bf16[3,48,768]{2,1,0:T(8,128)(2,1)} custom-call(bf16[8,3,8,90]{3,2,1,0:T(8,128)(2,1)} %copy-done.7, f32[3,48,768]{2,1,0:T(8,128)} %get-tuple-element.8.slope_ref, f32[48,8]{1,0:T(8,128)} %pad_convert_fusion.proj_t_ref), custom_call_target="tpu_custom_call" | custom-call | tf_op jit(solution)/shard_map/pallas_call | solution.py:330
  50.8 3.4 %collective-permute-start.3 = (bf16[3,48,768]{2,1,0:T(8,128)(2,1)}, bf16[3,48,768]{2,1,0:T(8,128)(2,1)S(1)}, u32[]{:S(2)}, u32[]{:S(2)}) collective-permute-start(bf16[3,48,768]{2,1,0:T(8,128)(2,1)} %shard_map.84.own_ref), channel_id=1, source_target_pairs={{0,1},{1,2},{2,3},{4,5},{5,6},{6,7},{8,9},{9,10},{10,11},{12,13},{... | collective-permute-start | bytes 663560 | tf_op jit(solution)/shard_map/ppermute | solution.py:43
  54.2 1.3 %collective-permute-start.2 = (bf16[3,48,768]{2,1,0:T(8,128)(2,1)}, bf16[3,48,768]{2,1,0:T(8,128)(2,1)S(1)}, u32[]{:S(2)}, u32[]{:S(2)}) collective-permute-start(bf16[3,48,768]{2,1,0:T(8,128)(2,1)} %shard_map.84.own_ref), channel_id=1, source_target_pairs={{1,0},{2,1},{3,2},{5,4},{6,5},{7,6},{9,8},{10,9},{11,10},{13,12},{... | collective-permute-start | bytes 663560 | tf_op jit(solution)/shard_map/ppermute | solution.py:44
  55.5 2.7 %shard_map.85.acc_in_ref = f32[3,48,768]{2,1,0:T(8,128)} custom-call(s32[588]{0:T(1024)} %reshape.27.basis_ref, s32[12]{0:T(128)} %step_ref.7, f32[12]{0:T(128)} %multiply_cosine_fusion.1.quad_ref, bf16[3,48,768]{2,1,0:T(8,128)(2,1)} %shard_map.84.own_ref, bf16[2,6,48,48]{3,2,1,0:T(8,128)(2,1)} %pad_maximum_fusion.1.table_ref), custom_call_target="tpu_custom_call" | custom-call | flops 222953472 | bytes 663552 | tf_op jit(solution)/shard_map/pallas_call | solution.py:343
  58.2 0.8 %collective-permute-done.3.prev_ref = bf16[3,48,768]{2,1,0:T(8,128)(2,1)S(1)} collective-permute-done((bf16[3,48,768]{2,1,0:T(8,128)(2,1)}, bf16[3,48,768]{2,1,0:T(8,128)(2,1)S(1)}, u32[]{:S(2)}, u32[]{:S(2)}) %collective-permute-start.3) | collective-permute-done | bytes 221216 | tf_op jit(solution)/shard_map/ppermute | solution.py:43
  59.0 0.7 %copy-done.6 = bf16[3,48,768]{2,1,0:T(8,128)(2,1)} copy-done((bf16[3,48,768]{2,1,0:T(8,128)(2,1)}, bf16[3,48,768]{2,1,0:T(8,128)(2,1)S(1)}, u32[]{:S(2)}) %copy-start.6) | copy-done | bytes 221208
  59.7 2.7 %shard_map.86.acc_in_ref = f32[3,48,768]{2,1,0:T(8,128)} custom-call(s32[588]{0:T(1024)} %reshape.27.basis_ref, s32[12]{0:T(128)} %step_ref.7, f32[12]{0:T(128)} %multiply_cosine_fusion.1.quad_ref, bf16[3,48,768]{2,1,0:T(8,128)(2,1)} %copy-done.6, f32[3,48,768]{2,1,0:T(8,128)} %shard_map.85.acc_in_ref, bf16[2,6,48,48]{3,2,1,0:T(8,128)(2,1)} %pad_maximum_fusion.1.table_ref), custom_call_target="tpu_custom_call" | custom-call | flops 222953472 | bytes 1105920 | tf_op jit(solution)/shard_map/pallas_call | solution.py:354
  62.4 2.0 %collective-permute-done.2.next_ref = bf16[3,48,768]{2,1,0:T(8,128)(2,1)S(1)} collective-permute-done((bf16[3,48,768]{2,1,0:T(8,128)(2,1)}, bf16[3,48,768]{2,1,0:T(8,128)(2,1)S(1)}, u32[]{:S(2)}, u32[]{:S(2)}) %collective-permute-start.2) | collective-permute-done | bytes 221216 | tf_op jit(solution)/shard_map/ppermute | solution.py:44
  64.4 0.7 %copy-done.5 = bf16[3,48,768]{2,1,0:T(8,128)(2,1)} copy-done((bf16[3,48,768]{2,1,0:T(8,128)(2,1)}, bf16[3,48,768]{2,1,0:T(8,128)(2,1)S(1)}, u32[]{:S(2)}) %copy-start.5) | copy-done | bytes 221208
  65.1 2.6 %shard_map.87 = bf16[3,45,720]{2,1,0:T(8,128)(2,1)} custom-call(s32[588]{0:T(1024)} %reshape.27.basis_ref, s32[12]{0:T(128)} %step_ref.7, f32[12]{0:T(128)} %multiply_cosine_fusion.1.quad_ref, bf16[3,48,768]{2,1,0:T(8,128)(2,1)} %copy-done.5, f32[3,48,768]{2,1,0:T(8,128)} %shard_map.86.acc_in_ref, bf16[2,6,48,48]{3,2,1,0:T(8,128)(2,1)} %pad_maximum_fusion.1.table_ref), custom_call_target="tpu_custom_call" | custom-call | tf_op jit(solution)/shard_map/pallas_call | solution.py:365
  (20 shorter events, 0.1 us)
Async XLA Ops:
  0.0 1.0 %copy-start.1 = (bf16[1,3,45,720]{3,2,1,0:T(8,128)(2,1)S(1)}, bf16[1,3,45,720]{3,2,1,0:T(8,128)(2,1)}, u32[]{:S(2)}) copy-start(bf16[1,3,45,720]{3,2,1,0:T(8,128)(2,1)} %param.8) | copy-start | bytes 583204
  1.0 6.9 %copy-start.10 = (bf16[5,45]{1,0:T(8,128)(2,1)S(1)}, bf16[5,45]{1,0:T(8,128)(2,1)}, u32[]{:S(2)}) copy-start(bf16[5,45]{1,0:T(8,128)(2,1)} %param.10) | copy-start | bytes 1354
  1.0 7.6 %copy-start.8 = (bf16[5,45,45]{2,1,0:T(8,128)(2,1)S(1)}, bf16[5,45,45]{2,1,0:T(8,128)(2,1)}, u32[]{:S(2)}) copy-start(bf16[5,45,45]{2,1,0:T(8,128)(2,1)} %param.9) | copy-start | bytes 60754
  1.1 7.8 %copy-start = (bf16[3,48,768]{2,1,0:T(8,128)(2,1)}, bf16[3,48,768]{2,1,0:T(8,128)(2,1)S(1)}, u32[]{:S(2)}) copy-start(bf16[3,48,768]{2,1,0:T(8,128)(2,1)S(1)} %pad_maximum_fusion.own_ref) | copy-start | bytes 663556
  1.1 11.9 %collective-permute-start = (bf16[3,48,768]{2,1,0:T(8,128)(2,1)S(1)}, bf16[3,48,768]{2,1,0:T(8,128)(2,1)S(1)}, u32[]{:S(2)}, u32[]{:S(2)}) collective-permute-start(bf16[3,48,768]{2,1,0:T(8,128)(2,1)S(1)} %pad_maximum_fusion.own_ref), channel_id=1, source_target_pairs={{0,1},{1,2},{2,3},{4,5},{5,6},{6,7},{8,9},{9,10},{10,11},{12,13},{... | collective-permute-start | bytes 663560 | tf_op jit(solution)/shard_map/ppermute | solution.py:43
  6.0 11.3 %collective-permute-start.1 = (bf16[3,48,768]{2,1,0:T(8,128)(2,1)S(1)}, bf16[3,48,768]{2,1,0:T(8,128)(2,1)S(1)}, u32[]{:S(2)}, u32[]{:S(2)}) collective-permute-start(bf16[3,48,768]{2,1,0:T(8,128)(2,1)S(1)} %pad_maximum_fusion.own_ref), channel_id=1, source_target_pairs={{1,0},{2,1},{3,2},{5,4},{6,5},{7,6},{9,8},{10,9},{11,10},{13,12},{... | collective-permute-start | bytes 663560 | tf_op jit(solution)/shard_map/ppermute | solution.py:44
  8.8 0.7 %copy-start.11 = (s32[12,49]{1,0:T(8,128)S(1)}, s32[12,49]{1,0:T(8,128)}, u32[]{:S(2)}) copy-start(s32[12,49]{1,0:T(8,128)} %param.13) | copy-start | bytes 7060
  8.8 1.4 %copy-start.12 = (bf16[4,5,5]{2,0,1:T(4,128)(2,1)S(1)}, bf16[4,5,5]{2,0,1:T(4,128)(2,1)}, u32[]{:S(2)}) copy-start(bf16[4,5,5]{2,0,1:T(4,128)(2,1)} %param.11) | copy-start | bytes 604
  9.5 2.2 %copy-start.9 = (f32[4,5,3,90]{3,0,2,1:T(4,128)S(1)}, f32[4,5,3,90]{3,0,2,1:T(4,128)}, u32[]{:S(2)}) copy-start(f32[4,5,3,90]{3,0,2,1:T(4,128)} %param.12) | copy-start | bytes 64804
  13.0 4.3 %copy-start.3 = (bf16[3,48,768]{2,1,0:T(8,128)(2,1)}, bf16[3,48,768]{2,1,0:T(8,128)(2,1)S(1)}, u32[]{:S(2)}) copy-start(bf16[3,48,768]{2,1,0:T(8,128)(2,1)S(1)} %collective-permute-done.prev_ref) | copy-start | bytes 663556
  17.3 0.7 %copy-start.4 = (bf16[3,48,768]{2,1,0:T(8,128)(2,1)}, bf16[3,48,768]{2,1,0:T(8,128)(2,1)S(1)}, u32[]{:S(2)}) copy-start(bf16[3,48,768]{2,1,0:T(8,128)(2,1)S(1)} %collective-permute-done.1.next_ref) | copy-start | bytes 663556
  22.7 5.0 %copy-start.13 = (f32[4]{0:T(128)S(1)}, f32[4]{0:T(128)}, u32[]{:S(2)}) copy-start(f32[4]{0:T(128)} %constant.23.clone) | copy-start | bytes 52
  22.7 12.0 %all-to-all-start = ((bf16[8,3,20,90]{3,2,1,0:T(8,128)(2,1)}), bf16[8,3,20,90]{3,2,1,0:T(8,128)(2,1)S(1)}, u32[]{:S(2)}, u32[]{:S(2)}) async-start(bf16[8,3,20,90]{3,2,1,0:T(8,128)(2,1)} %get-tuple-element.7), calls=%async_computation | async-start | bytes 294912 | tf_op jit(solution)/shard_map/all_to_all | solution.py:321
  34.8 0.7 copy-start.2
  38.0 9.1 %all-to-all-start.1 = ((bf16[8,3,8,90]{3,2,1,0:T(8,128)(2,1)}), bf16[8,3,8,90]{3,2,1,0:T(8,128)(2,1)S(1)}, u32[]{:S(2)}, u32[]{:S(2)}) async-start(bf16[8,3,8,90]{3,2,1,0:T(8,128)(2,1)} %shard_map.83), calls=%async_computation.1 | async-start | bytes 98304 | tf_op jit(solution)/shard_map/all_to_all | solution.py:328
  47.1 0.6 copy-start.7
  50.8 8.2 %collective-permute-start.3 = (bf16[3,48,768]{2,1,0:T(8,128)(2,1)}, bf16[3,48,768]{2,1,0:T(8,128)(2,1)S(1)}, u32[]{:S(2)}, u32[]{:S(2)}) collective-permute-start(bf16[3,48,768]{2,1,0:T(8,128)(2,1)} %shard_map.84.own_ref), channel_id=1, source_target_pairs={{0,1},{1,2},{2,3},{4,5},{5,6},{6,7},{8,9},{9,10},{10,11},{12,13},{... | collective-permute-start | bytes 663560 | tf_op jit(solution)/shard_map/ppermute | solution.py:43
  54.2 10.2 %collective-permute-start.2 = (bf16[3,48,768]{2,1,0:T(8,128)(2,1)}, bf16[3,48,768]{2,1,0:T(8,128)(2,1)S(1)}, u32[]{:S(2)}, u32[]{:S(2)}) collective-permute-start(bf16[3,48,768]{2,1,0:T(8,128)(2,1)} %shard_map.84.own_ref), channel_id=1, source_target_pairs={{1,0},{2,1},{3,2},{5,4},{6,5},{7,6},{9,8},{10,9},{11,10},{13,12},{... | collective-permute-start | bytes 663560 | tf_op jit(solution)/shard_map/ppermute | solution.py:44
  59.0 0.7 %copy-start.6 = (bf16[3,48,768]{2,1,0:T(8,128)(2,1)}, bf16[3,48,768]{2,1,0:T(8,128)(2,1)S(1)}, u32[]{:S(2)}) copy-start(bf16[3,48,768]{2,1,0:T(8,128)(2,1)S(1)} %collective-permute-done.3.prev_ref) | copy-start | bytes 663556
  64.4 0.7 %copy-start.5 = (bf16[3,48,768]{2,1,0:T(8,128)(2,1)}, bf16[3,48,768]{2,1,0:T(8,128)(2,1)S(1)}, u32[]{:S(2)}) copy-start(bf16[3,48,768]{2,1,0:T(8,128)(2,1)S(1)} %collective-permute-done.2.next_ref) | copy-start | bytes 663556

commit v13 on v10

--- a/solution.py
+++ b/solution.py
@@ -189,7 +189,7 @@
         hi = extra - lo
         ring = jnp.concatenate([row, row[:, :lo], row[:, width - hi :]], axis=1)
         grad_act = jnp.dot(
-            proj_t_ref[...], ring.astype(jnp.float32), preferred_element_type=jnp.float32
+            proj_t_ref[...], ring, preferred_element_type=jnp.float32
         )
         out_ref[i] = (grad_act * slope_ref[i]).astype(jnp.bfloat16)
 
@@ -326,7 +326,7 @@
         out_specs=vmem(),
     )(weight_all, sub_t, fc_owned, truth)
     gc_home = lax.all_to_all(gc_owned, "member", split_axis=0, concat_axis=0, tiled=True)
-    proj_t = pad_axis(pad_axis(project.T, 0, cp), 1, vq).astype(jnp.float32)
+    proj_t = pad_axis(pad_axis(project.T, 0, cp), 1, vq)
     grad_filtered = pl.pallas_call(
         grad_filtered_kernel,
         out_shape=jax.ShapeDtypeStruct((rows, cp, width_p), jnp.bfloat16),

time: 67.3 us -> 67.5 us (level)
  starting transfers between devices: 19.2 us -> 21.7 us
  waiting for transfers between devices: 18.5 us -> 16.7 us
    ppermute x2, starting transfers between devices: 8.26 us -> 10.2 us  [halo(): low = lax.ppermute(block[block.shape[0] - width:], axis_name, forward)]
    ppermute x2, waiting for transfers between devices: 6.3 us -> 5.06 us  [halo(): high = lax.ppermute(block[:width], axis_name, backward)]
    all_to_all x1, waiting for transfers between devices: 6.22 us -> 5.01 us  [on_device(): lax.all_to_all(fc, 'member', split_axis=0, concat_axis=0, tiled=True)]
    ppermute x2, waiting for transfers between devices: 0.84 us -> 1.56 us  [halo(): low = lax.ppermute(block[block.shape[0] - width:], axis_name, forward)]
    pad x4 -> x5, local copies, waits for them, and re-layouts: 1.8 us -> 2.41 us  [pad_axis(): return jnp.pad(block, pads)]
where the time goes in v13:
time: 67.5 us; the launch traced here: 66.9 us
  starting transfers between devices  21.7 us (32%)
  Pallas kernels  17.3 us (26%)
  waiting for transfers between devices  16.7 us (25%)
  local copies, waits for them, and re-layouts  9.54 us (14%)
  other arithmetic  1.51 us (2%)
    ppermute x2, starting transfers between devices, halo(): low = lax.ppermute(block[block.shape[0] - width:], axis_name, forward)  10.2 us
    all_to_all x1, starting transfers between devices, on_device(): lax.all_to_all(fc, 'member', split_axis=0, concat_axis=0, tiled=True)  5.51 us
    ppermute x2, waiting for transfers between devices, halo(): high = lax.ppermute(block[:width], axis_name, backward)  5.06 us
    all_to_all x1, waiting for transfers between devices, on_device(): lax.all_to_all(gc_owned, 'member', split_axis=0, concat_axis=0, tiled=True)  5.04 us
    all_to_all x1, waiting for transfers between devices, on_device(): lax.all_to_all(fc, 'member', split_axis=0, concat_axis=0, tiled=True)  5.01 us
    pallas_call x1, Pallas kernels, on_device(): pl.pallas_call(forward_kernel, out_shape=(jax.ShapeDtypeStruct((rows, cp,...  4.7 us
    unnamed x32, local copies, waits for them, and re-layouts  3.92 us
    all_to_all x1, starting transfers between devices, on_device(): lax.all_to_all(gc_owned, 'member', split_axis=0, concat_axis=0, tiled=True)  3.34 us
  transfers between devices with their start and end apart: 6, of which 5 were waited for; matrix products, arithmetic and copies ran while one was open for 10% of the time, Pallas kernels for 8%

profile of v13, /device:TPU:0, one launch (start us, length us, event | category | flops | bytes accessed | tf_op | source)
XLA Modules:
  0.0 66.9 jit_solution(8893707041077799031)
XLA Ops:
  0.0 0.9 %pad_slice_fusion.1 = (bf16[3,48,24]{2,1,0:T(8,128)(2,1)S(1)}, bf16[3,48,24]{2,1,0:T(8,128)(2,1)S(1)}) fusion(bf16[3,45,720]{2,1,0:T(8,128)(2,1)} %bitcast.16), kind=kLoop, calls=%fused_computation.9 | loop fusion | bytes 208224 | tf_op jit(solution)/shard_map/slice | solution.py:29
  0.9 0.0 copy-done.1
  1.0 0.0 copy-start.11
  1.0 0.0 copy-start.8
  1.0 0.1 pad_maximum_fusion.own_ref
  1.1 1.3 %collective-permute-start.1 = (bf16[3,48,768]{2,1,0:T(8,128)(2,1)S(1)}, bf16[3,48,768]{2,1,0:T(8,128)(2,1)S(1)}, u32[]{:S(2)}, u32[]{:S(2)}) collective-permute-start(bf16[3,48,768]{2,1,0:T(8,128)(2,1)S(1)} %pad_maximum_fusion.own_ref), channel_id=1, source_target_pairs={{1,0},{2,1},{3,2},{5,4},{6,5},{7,6},{9,8},{10,9},{11,10},{13,12},{... | collective-permute-start | bytes 663560 | tf_op jit(solution)/shard_map/ppermute | solution.py:44
  2.4 5.5 %collective-permute-start = (bf16[3,48,768]{2,1,0:T(8,128)(2,1)S(1)}, bf16[3,48,768]{2,1,0:T(8,128)(2,1)S(1)}, u32[]{:S(2)}, u32[]{:S(2)}) collective-permute-start(bf16[3,48,768]{2,1,0:T(8,128)(2,1)S(1)} %pad_maximum_fusion.own_ref), channel_id=1, source_target_pairs={{0,1},{1,2},{2,3},{4,5},{5,6},{6,7},{8,9},{9,10},{10,11},{12,13},{... | collective-permute-start | bytes 663560 | tf_op jit(solution)/shard_map/ppermute | solution.py:43
  7.9 0.6 multiply_cosine_fusion.1.quad_ref
  8.6 0.0 copy-done.11
  8.6 0.7 %reshape.27.basis_ref = s32[588]{0:T(1024)} reshape(s32[12,49]{1,0:T(8,128)S(1)} %copy-done.11) | data formatting | bytes 4704 | tf_op jit(solution)/shard_map/reshape | solution.py:303
  9.2 0.0 copy-done.10
  9.2 0.6 pad.53.proj_ref
  9.8 0.1 copy-done.12
  9.9 0.1 copy.15
  10.1 0.1 reshape.28
  10.1 0.1 copy.18
  10.3 0.6 pad.43.sub_ref
  10.9 0.0 copy-done.8
  10.9 0.1 copy.16
  11.0 0.1 copy.17
  11.2 0.7 %pad_maximum_fusion.1.table_ref = bf16[2,6,48,48]{3,2,1,0:T(8,128)(2,1)} fusion(bf16[1,6,48,48]{3,2,1,0:T(8,128)(2,1)S(1)} %get-tuple-element.12, bf16[1,6,48,48]{3,2,1,0:T(8,128)(2,1)S(1)} %copy.17), kind=kLoop, calls=%fused_computation.1 | loop fusion | flops 27648 | bytes 110592 | tf_op jit(solution)/shard_map/stack | solution.py:302
  11.8 0.0 collective-permute-done.1.next_ref
  11.9 0.7 %collective-permute-done.prev_ref = bf16[3,48,768]{2,1,0:T(8,128)(2,1)S(1)} collective-permute-done((bf16[3,48,768]{2,1,0:T(8,128)(2,1)S(1)}, bf16[3,48,768]{2,1,0:T(8,128)(2,1)S(1)}, u32[]{:S(2)}, u32[]{:S(2)}) %collective-permute-start) | collective-permute-done | bytes 221216 | tf_op jit(solution)/shard_map/ppermute | solution.py:43
  12.6 0.7 %copy-done.4 = bf16[3,48,768]{2,1,0:T(8,128)(2,1)} copy-done((bf16[3,48,768]{2,1,0:T(8,128)(2,1)}, bf16[3,48,768]{2,1,0:T(8,128)(2,1)S(1)}, u32[]{:S(2)}) %copy-start.4) | copy-done | bytes 221208
  13.3 4.7 %shard_map.82 = (f32[3,48,768]{2,1,0:T(8,128)}, bf16[8,3,20,90]{3,2,1,0:T(8,128)(2,1)}) custom-call(s32[588]{0:T(1024)} %reshape.27.basis_ref, s32[12]{0:T(128)} %step_ref.7, f32[12]{0:T(128)} %multiply_cosine_fusion.1.quad_ref, bf16[3,48,768]{2,1,0:T(8,128)(2,1)} %copy-done.4, bf16[3,48,768]{2,1,0:T(8,128)(2,1)} %copy-done, bf16[3,48,768]{2,1,0:T(8,128)(2,1)} %copy-done.3, ...), custom_call_target="tpu_custom_call" | custom-call | tf_op jit(solution)/shard_map/pallas_call | solution.py:311
  18.0 5.5 %all-to-all-start = ((bf16[8,3,20,90]{3,2,1,0:T(8,128)(2,1)}), bf16[8,3,20,90]{3,2,1,0:T(8,128)(2,1)S(1)}, u32[]{:S(2)}, u32[]{:S(2)}) async-start(bf16[8,3,20,90]{3,2,1,0:T(8,128)(2,1)} %get-tuple-element.7), calls=%async_computation | async-start | bytes 294912 | tf_op jit(solution)/shard_map/all_to_all | solution.py:321
  23.5 0.1 multiply_cosine_fusion
  23.6 0.7 reshape.32.weight_ref
  24.3 0.6 pad.37.sub_t_ref
  24.9 0.6 copy.23
  25.5 5.0 %all-to-all-done.fc_ref = bf16[8,3,20,90]{3,2,1,0:T(8,128)(2,1)S(1)} async-done(((bf16[8,3,20,90]{3,2,1,0:T(8,128)(2,1)}), bf16[8,3,20,90]{3,2,1,0:T(8,128)(2,1)S(1)}, u32[]{:S(2)}, u32[]{:S(2)}) %all-to-all-start) | async-done | bytes 86432 | tf_op jit(solution)/shard_map/all_to_all | solution.py:321
  30.5 0.7 copy-done.2
  31.2 2.6 %shard_map.83 = bf16[8,3,8,90]{3,2,1,0:T(8,128)(2,1)} custom-call(f32[48]{0:T(128)} %reshape.32.weight_ref, bf16[8,20]{1,0:T(8,128)(2,1)} %pad.37.sub_t_ref, bf16[8,3,20,90]{3,2,1,0:T(8,128)(2,1)} %copy-done.2, f32[3,20,90]{2,1,0:T(8,128)} %bitcast.19), custom_call_target="tpu_custom_call" | custom-call | tf_op jit(solution)/shard_map/pallas_call | solution.py:322
  33.7 3.3 %all-to-all-start.1 = ((bf16[8,3,8,90]{3,2,1,0:T(8,128)(2,1)}), bf16[8,3,8,90]{3,2,1,0:T(8,128)(2,1)S(1)}, u32[]{:S(2)}, u32[]{:S(2)}) async-start(bf16[8,3,8,90]{3,2,1,0:T(8,128)(2,1)} %shard_map.83), calls=%async_computation.1 | async-start | bytes 98304 | tf_op jit(solution)/shard_map/all_to_all | solution.py:328
  37.1 0.1 copy.21
  37.2 0.6 pad.54.proj_t_ref
  37.8 5.0 %all-to-all-done.1.gc_ref = bf16[8,3,8,90]{3,2,1,0:T(8,128)(2,1)S(1)} async-done(((bf16[8,3,8,90]{3,2,1,0:T(8,128)(2,1)}), bf16[8,3,8,90]{3,2,1,0:T(8,128)(2,1)S(1)}, u32[]{:S(2)}, u32[]{:S(2)}) %all-to-all-start.1) | async-done | bytes 34592 | tf_op jit(solution)/shard_map/all_to_all | solution.py:328
  42.9 0.6 copy-done.7
  43.5 2.0 %shard_map.84.own_ref = bf16[3,48,768]{2,1,0:T(8,128)(2,1)} custom-call(bf16[8,3,8,90]{3,2,1,0:T(8,128)(2,1)} %copy-done.7, f32[3,48,768]{2,1,0:T(8,128)} %get-tuple-element.8.slope_ref, bf16[48,8]{1,0:T(8,128)(2,1)} %pad.54.proj_t_ref), custom_call_target="tpu_custom_call" | custom-call | tf_op jit(solution)/shard_map/pallas_call | solution.py:330
  45.5 4.8 %collective-permute-start.3 = (bf16[3,48,768]{2,1,0:T(8,128)(2,1)}, bf16[3,48,768]{2,1,0:T(8,128)(2,1)S(1)}, u32[]{:S(2)}, u32[]{:S(2)}) collective-permute-start(bf16[3,48,768]{2,1,0:T(8,128)(2,1)} %shard_map.84.own_ref), channel_id=1, source_target_pairs={{0,1},{1,2},{2,3},{4,5},{5,6},{6,7},{8,9},{9,10},{10,11},{12,13},{... | collective-permute-start | bytes 663560 | tf_op jit(solution)/shard_map/ppermute | solution.py:43
  50.3 1.3 %collective-permute-start.2 = (bf16[3,48,768]{2,1,0:T(8,128)(2,1)}, bf16[3,48,768]{2,1,0:T(8,128)(2,1)S(1)}, u32[]{:S(2)}, u32[]{:S(2)}) collective-permute-start(bf16[3,48,768]{2,1,0:T(8,128)(2,1)} %shard_map.84.own_ref), channel_id=1, source_target_pairs={{1,0},{2,1},{3,2},{5,4},{6,5},{7,6},{9,8},{10,9},{11,10},{13,12},{... | collective-permute-start | bytes 663560 | tf_op jit(solution)/shard_map/ppermute | solution.py:44
  51.6 2.7 %shard_map.85.acc_in_ref = f32[3,48,768]{2,1,0:T(8,128)} custom-call(s32[588]{0:T(1024)} %reshape.27.basis_ref, s32[12]{0:T(128)} %step_ref.7, f32[12]{0:T(128)} %multiply_cosine_fusion.1.quad_ref, bf16[3,48,768]{2,1,0:T(8,128)(2,1)} %shard_map.84.own_ref, bf16[2,6,48,48]{3,2,1,0:T(8,128)(2,1)} %pad_maximum_fusion.1.table_ref), custom_call_target="tpu_custom_call" | custom-call | flops 222953472 | bytes 663552 | tf_op jit(solution)/shard_map/pallas_call | solution.py:338
  54.3 0.8 %collective-permute-done.3.prev_ref = bf16[3,48,768]{2,1,0:T(8,128)(2,1)S(1)} collective-permute-done((bf16[3,48,768]{2,1,0:T(8,128)(2,1)}, bf16[3,48,768]{2,1,0:T(8,128)(2,1)S(1)}, u32[]{:S(2)}, u32[]{:S(2)}) %collective-permute-start.3) | collective-permute-done | bytes 221216 | tf_op jit(solution)/shard_map/ppermute | solution.py:43
  55.1 0.7 %copy-done.6 = bf16[3,48,768]{2,1,0:T(8,128)(2,1)} copy-done((bf16[3,48,768]{2,1,0:T(8,128)(2,1)}, bf16[3,48,768]{2,1,0:T(8,128)(2,1)S(1)}, u32[]{:S(2)}) %copy-start.6) | copy-done | bytes 221208
  55.8 2.7 %shard_map.86.acc_in_ref = f32[3,48,768]{2,1,0:T(8,128)} custom-call(s32[588]{0:T(1024)} %reshape.27.basis_ref, s32[12]{0:T(128)} %step_ref.7, f32[12]{0:T(128)} %multiply_cosine_fusion.1.quad_ref, bf16[3,48,768]{2,1,0:T(8,128)(2,1)} %copy-done.6, f32[3,48,768]{2,1,0:T(8,128)} %shard_map.85.acc_in_ref, bf16[2,6,48,48]{3,2,1,0:T(8,128)(2,1)} %pad_maximum_fusion.1.table_ref), custom_call_target="tpu_custom_call" | custom-call | flops 222953472 | bytes 1105920 | tf_op jit(solution)/shard_map/pallas_call | solution.py:349
  58.5 5.1 %collective-permute-done.2.next_ref = bf16[3,48,768]{2,1,0:T(8,128)(2,1)S(1)} collective-permute-done((bf16[3,48,768]{2,1,0:T(8,128)(2,1)}, bf16[3,48,768]{2,1,0:T(8,128)(2,1)S(1)}, u32[]{:S(2)}, u32[]{:S(2)}) %collective-permute-start.2) | collective-permute-done | bytes 221216 | tf_op jit(solution)/shard_map/ppermute | solution.py:44
  63.6 0.7 %copy-done.5 = bf16[3,48,768]{2,1,0:T(8,128)(2,1)} copy-done((bf16[3,48,768]{2,1,0:T(8,128)(2,1)}, bf16[3,48,768]{2,1,0:T(8,128)(2,1)S(1)}, u32[]{:S(2)}) %copy-start.5) | copy-done | bytes 221208
  64.3 2.6 %shard_map.87 = bf16[3,45,720]{2,1,0:T(8,128)(2,1)} custom-call(s32[588]{0:T(1024)} %reshape.27.basis_ref, s32[12]{0:T(128)} %step_ref.7, f32[12]{0:T(128)} %multiply_cosine_fusion.1.quad_ref, bf16[3,48,768]{2,1,0:T(8,128)(2,1)} %copy-done.5, f32[3,48,768]{2,1,0:T(8,128)} %shard_map.86.acc_in_ref, bf16[2,6,48,48]{3,2,1,0:T(8,128)(2,1)} %pad_maximum_fusion.1.table_ref), custom_call_target="tpu_custom_call" | custom-call | tf_op jit(solution)/shard_map/pallas_call | solution.py:360
  (20 shorter events, 0.1 us)
Async XLA Ops:
  0.0 1.0 %copy-start.1 = (bf16[1,3,45,720]{3,2,1,0:T(8,128)(2,1)S(1)}, bf16[1,3,45,720]{3,2,1,0:T(8,128)(2,1)}, u32[]{:S(2)}) copy-start(bf16[1,3,45,720]{3,2,1,0:T(8,128)(2,1)} %param.8) | copy-start | bytes 583204
  1.0 7.6 %copy-start.11 = (s32[12,49]{1,0:T(8,128)S(1)}, s32[12,49]{1,0:T(8,128)}, u32[]{:S(2)}) copy-start(s32[12,49]{1,0:T(8,128)} %param.13) | copy-start | bytes 7060
  1.0 9.9 %copy-start.8 = (bf16[5,45,45]{2,1,0:T(8,128)(2,1)S(1)}, bf16[5,45,45]{2,1,0:T(8,128)(2,1)}, u32[]{:S(2)}) copy-start(bf16[5,45,45]{2,1,0:T(8,128)(2,1)} %param.9) | copy-start | bytes 60754
  1.1 10.0 %copy-start = (bf16[3,48,768]{2,1,0:T(8,128)(2,1)}, bf16[3,48,768]{2,1,0:T(8,128)(2,1)S(1)}, u32[]{:S(2)}) copy-start(bf16[3,48,768]{2,1,0:T(8,128)(2,1)S(1)} %pad_maximum_fusion.own_ref) | copy-start | bytes 663556
  1.1 10.7 %collective-permute-start.1 = (bf16[3,48,768]{2,1,0:T(8,128)(2,1)S(1)}, bf16[3,48,768]{2,1,0:T(8,128)(2,1)S(1)}, u32[]{:S(2)}, u32[]{:S(2)}) collective-permute-start(bf16[3,48,768]{2,1,0:T(8,128)(2,1)S(1)} %pad_maximum_fusion.own_ref), channel_id=1, source_target_pairs={{1,0},{2,1},{3,2},{5,4},{6,5},{7,6},{9,8},{10,9},{11,10},{13,12},{... | collective-permute-start | bytes 663560 | tf_op jit(solution)/shard_map/ppermute | solution.py:44
  2.4 10.1 %collective-permute-start = (bf16[3,48,768]{2,1,0:T(8,128)(2,1)S(1)}, bf16[3,48,768]{2,1,0:T(8,128)(2,1)S(1)}, u32[]{:S(2)}, u32[]{:S(2)}) collective-permute-start(bf16[3,48,768]{2,1,0:T(8,128)(2,1)S(1)} %pad_maximum_fusion.own_ref), channel_id=1, source_target_pairs={{0,1},{1,2},{2,3},{4,5},{5,6},{6,7},{8,9},{9,10},{10,11},{12,13},{... | collective-permute-start | bytes 663560 | tf_op jit(solution)/shard_map/ppermute | solution.py:43
  8.6 0.7 %copy-start.10 = (bf16[5,45]{1,0:T(8,128)(2,1)S(1)}, bf16[5,45]{1,0:T(8,128)(2,1)}, u32[]{:S(2)}) copy-start(bf16[5,45]{1,0:T(8,128)(2,1)} %param.10) | copy-start | bytes 1354
  9.2 0.7 %copy-start.12 = (bf16[4,5,5]{2,0,1:T(4,128)(2,1)S(1)}, bf16[4,5,5]{2,0,1:T(4,128)(2,1)}, u32[]{:S(2)}) copy-start(bf16[4,5,5]{2,0,1:T(4,128)(2,1)} %param.11) | copy-start | bytes 604
  11.9 0.7 %copy-start.3 = (bf16[3,48,768]{2,1,0:T(8,128)(2,1)}, bf16[3,48,768]{2,1,0:T(8,128)(2,1)S(1)}, u32[]{:S(2)}) copy-start(bf16[3,48,768]{2,1,0:T(8,128)(2,1)S(1)} %collective-permute-done.1.next_ref) | copy-start | bytes 663556
  12.6 0.7 %copy-start.4 = (bf16[3,48,768]{2,1,0:T(8,128)(2,1)}, bf16[3,48,768]{2,1,0:T(8,128)(2,1)S(1)}, u32[]{:S(2)}) copy-start(bf16[3,48,768]{2,1,0:T(8,128)(2,1)S(1)} %collective-permute-done.prev_ref) | copy-start | bytes 663556
  18.0 5.5 %copy-start.13 = (f32[4]{0:T(128)S(1)}, f32[4]{0:T(128)}, u32[]{:S(2)}) copy-start(f32[4]{0:T(128)} %constant.23.clone) | copy-start | bytes 52
  18.0 6.9 %copy-start.9 = (f32[4,5,3,90]{3,0,2,1:T(4,128)S(1)}, f32[4,5,3,90]{3,0,2,1:T(4,128)}, u32[]{:S(2)}) copy-start(f32[4,5,3,90]{3,0,2,1:T(4,128)} %param.12) | copy-start | bytes 64804
  18.0 12.5 %all-to-all-start = ((bf16[8,3,20,90]{3,2,1,0:T(8,128)(2,1)}), bf16[8,3,20,90]{3,2,1,0:T(8,128)(2,1)S(1)}, u32[]{:S(2)}, u32[]{:S(2)}) async-start(bf16[8,3,20,90]{3,2,1,0:T(8,128)(2,1)} %get-tuple-element.7), calls=%async_computation | async-start | bytes 294912 | tf_op jit(solution)/shard_map/all_to_all | solution.py:321
  30.5 0.7 copy-start.2
  33.7 9.1 %all-to-all-start.1 = ((bf16[8,3,8,90]{3,2,1,0:T(8,128)(2,1)}), bf16[8,3,8,90]{3,2,1,0:T(8,128)(2,1)S(1)}, u32[]{:S(2)}, u32[]{:S(2)}) async-start(bf16[8,3,8,90]{3,2,1,0:T(8,128)(2,1)} %shard_map.83), calls=%async_computation.1 | async-start | bytes 98304 | tf_op jit(solution)/shard_map/all_to_all | solution.py:328
  42.8 0.6 copy-start.7
  45.5 9.6 %collective-permute-start.3 = (bf16[3,48,768]{2,1,0:T(8,128)(2,1)}, bf16[3,48,768]{2,1,0:T(8,128)(2,1)S(1)}, u32[]{:S(2)}, u32[]{:S(2)}) collective-permute-start(bf16[3,48,768]{2,1,0:T(8,128)(2,1)} %shard_map.84.own_ref), channel_id=1, source_target_pairs={{0,1},{1,2},{2,3},{4,5},{5,6},{6,7},{8,9},{9,10},{10,11},{12,13},{... | collective-permute-start | bytes 663560 | tf_op jit(solution)/shard_map/ppermute | solution.py:43
  50.3 13.3 %collective-permute-start.2 = (bf16[3,48,768]{2,1,0:T(8,128)(2,1)}, bf16[3,48,768]{2,1,0:T(8,128)(2,1)S(1)}, u32[]{:S(2)}, u32[]{:S(2)}) collective-permute-start(bf16[3,48,768]{2,1,0:T(8,128)(2,1)} %shard_map.84.own_ref), channel_id=1, source_target_pairs={{1,0},{2,1},{3,2},{5,4},{6,5},{7,6},{9,8},{10,9},{11,10},{13,12},{... | collective-permute-start | bytes 663560 | tf_op jit(solution)/shard_map/ppermute | solution.py:44
  55.1 0.7 %copy-start.6 = (bf16[3,48,768]{2,1,0:T(8,128)(2,1)}, bf16[3,48,768]{2,1,0:T(8,128)(2,1)S(1)}, u32[]{:S(2)}) copy-start(bf16[3,48,768]{2,1,0:T(8,128)(2,1)S(1)} %collective-permute-done.3.prev_ref) | copy-start | bytes 663556
  63.6 0.7 %copy-start.5 = (bf16[3,48,768]{2,1,0:T(8,128)(2,1)}, bf16[3,48,768]{2,1,0:T(8,128)(2,1)S(1)}, u32[]{:S(2)}) copy-start(bf16[3,48,768]{2,1,0:T(8,128)(2,1)S(1)} %collective-permute-done.2.next_ref) | copy-start | bytes 663556
